TPU v7x, 768 devices: a whole 4x8x12 slice. The times are simulated.
768 devices in a mesh: dp: 48 (over x, z_lo, core), tile: 16 (over z_hi, y).
Axes of the slice: x: 4, y: 8, z: 12 (z_hi: 2, z_lo: 6; z = z_hi * 6 + z_lo), core: 2. Of those that a mesh axis runs over, the one named last changes fastest.
Arguments:
- features: bfloat16 [48, 256, 128, 256], P('dp', 'tile'), may hold values from -6 to 6
- cotangent: bfloat16 [48, 256, 128, 256], P('dp', 'tile'), may hold values from -6 to 6
- conv_weight: bfloat16 [2304, 256], P('dp'), may hold values from -0.125 to 0.125
- norm_gain: float32 [256], replicated, may hold values from 0.1 to 1.9
- norm_bias: float32 [256], replicated, may hold values from -3 to 3
- film_rows: float32 [48, 512], P('dp'), may hold values from -3 to 3
Outputs:
- output: float32 [48, 256, 128, 256], P('dp', 'tile')
- grad_weight: float32 [2304, 256], P('dp', 'tile')
All inputs are finite; a program needn't handle non-finite values.
Results may differ from a plain program's by a relative error of at most 0.0029.
Values may be sent and summed in bfloat16 or wider, within the bound.
No kernel may reach another device: no remote copies, remote signals or barrier semaphores. Data moves between devices by JAX's collectives and lax.ppermute only.
A program may use at most 64 MiB of HBM per device.

v0:
```python
import jax
import jax.numpy as jnp
from jax import lax
from jax.sharding import PartitionSpec as P

G = 32


def extended_2(cells, sides, width):
    for axis, dim in sides:
        count = lax.axis_size(axis)
        ends = count - 1
        head = lax.slice_in_dim(cells, 0, width, axis=dim)
        tail = lax.slice_in_dim(cells, cells.shape[dim] - width, cells.shape[dim], axis=dim)
        cells = jnp.concatenate(
            [
                lax.ppermute(tail, axis, [(i, (i + 1) % count) for i in range(ends)]),
                cells,
                lax.ppermute(head, axis, [((i + 1) % count, i) for i in range(ends)]),
            ],
            axis=dim,
        )
    return cells


def body(features, cotangent, conv_weight, norm_gain, norm_bias, film_rows):
    rows = features.shape[1]
    cols = features.shape[2]
    width = features.shape[3]
    values = features[0].astype(jnp.float32)
    grouped = values.reshape(rows, cols, G, width // G)
    sums, squares = lax.psum(
        (jnp.sum(grouped, axis=(0, 1, 3)), jnp.sum(grouped * grouped, axis=(0, 1, 3))), "tile"
    )
    count = rows * lax.axis_size("tile") * cols * (width // G)
    mean = sums / count
    var = squares / count - mean * mean
    mean_c = jnp.repeat(mean, width // G)
    inv_c = jnp.repeat(1.0 / jnp.sqrt(var + 1e-05), width // G)
    film = film_rows[0]
    normed = (values - mean_c) * inv_c * norm_gain + norm_bias
    act = jax.nn.silu(normed * (1.0 + film[:width]) + film[width:]).astype(jnp.bfloat16)
    extended = extended_2(act, (("tile", 0),), 1)
    padded = jnp.pad(extended, ((0, 0), (1, 1), (0, 0)))
    taps = [padded[i : i + rows, j : j + cols, :] for i in range(3) for j in range(3)]
    patches = jnp.concatenate(taps, axis=-1).reshape(rows * cols, 9 * width)
    full_weight = lax.all_gather(conv_weight, "dp", axis=0, tiled=True)
    conv = jnp.dot(patches, full_weight, preferred_element_type=jnp.float32)
    output = (conv.reshape(rows, cols, width) + values)[None]
    positions = lax.axis_size("dp") * rows * lax.axis_size("tile") * cols
    cot_rows = cotangent[0].reshape(rows * cols, width)
    summed_rows = lax.psum_scatter(
        lax.dot_general(
            patches, cot_rows, (((0,), (0,)), ((), ())), preferred_element_type=jnp.float32
        ),
        "dp",
        scatter_dimension=0,
        tiled=True,
    )
    grad_sum = lax.psum_scatter(summed_rows, "tile", scatter_dimension=1, tiled=True)
    grad_weight = grad_sum / jnp.sqrt(jnp.float32(positions))
    return (output, grad_weight)


def solution(mesh):
    in_specs = (
        P("dp", "tile", None, None),
        P("dp", "tile", None, None),
        P("dp", None),
        P(),
        P(),
        P("dp", None),
    )
    out_specs = (P("dp", "tile", None, None), P("dp", "tile"))
    return jax.shard_map(body, mesh=mesh, in_specs=in_specs, out_specs=out_specs, check_vma=False)
```

profile of v0, /device:TPU:1, one launch (start us, length us, event | category | flops | bytes accessed | tf_op | source)
XLA Modules:
  0.0 739.9 jit_solution(2751872993861321814)
XLA Ops:
  7.2 1.6 convert_reduce_fusion
  9.0 0.1 reduce_sum.25
  9.3 65.6 %all-reduce.1 = (f32[32]{0:T(128)S(1)}, f32[32]{0:T(128)S(1)}) all-reduce(f32[32]{0:T(128)S(1)} %reduce_sum.37, f32[32]{0:T(128)S(1)} %reduce_sum.25), channel_id=1, replica_groups=mesh['dp'=48,'tile'=16] {'tile'}, use_global_device_ids=true, to_apply=%region_5.6 | all-reduce | flops 64 | bytes 512 | tf_op jit(solution)/shard_map/psum | solution.py:32
  75.2 0.7 slice_add_fusion
  75.9 2.1 multiply_convert_fusion
  78.0 1.3 collective-permute-start
  79.3 1.3 collective-permute-start.1
  80.6 3.7 collective-permute-done.1
  84.3 0.5 fusion.14
  85.1 0.4 slice_dynamic-update-slice_fusion.4
  85.6 0.7 copy-done.1
  86.3 0.9 constant_dynamic-update-slice_fusion
  87.2 0.4 slice_dynamic-update-slice_fusion.2
  87.7 0.4 slice_dynamic-update-slice_fusion
  88.1 3.6 copy-done.2
  91.7 4.2 fusion.19
  95.9 0.7 all-gather.2.cloned.1.call-update
  96.7 299.8 %reduce-scatter.5.cloned.1.call-done = f32[48,256]{1,0:T(8,128)} async-done(((f32[2304,256]{1,0:T(8,128)}), f32[48,256]{1,0:T(8,128)}) %reduce-scatter.5.cloned.1.call-update) | async-done | bytes 49168 | tf_op jit(solution)/shard_map/reduce_scatter | solution.py:52
  396.5 1.5 copy.11
  398.1 98.8 %all-gather.2.cloned.1.call-done = bf16[2304,256]{1,0:T(8,128)(2,1)} async-done(((bf16[48,256]{1,0:T(8,128)(2,1)}), bf16[2304,256]{1,0:T(8,128)(2,1)}) %all-gather.2.cloned.1.call-update) | async-done | bytes 1179664 | tf_op jit(solution)/shard_map/all_gather | solution.py:47
  496.9 7.9 %fusion.8 = f32[1,16,128,256]{3,2,1,0:T(8,128)} fusion(bf16[1,16,128,256]{3,2,1,0:T(8,128)(2,1)S(1)} %copy-done.1, bf16[16,128,2304]{2,1,0:T(8,128)(2,1)} %copy-done.2, bf16[2304,256]{1,0:T(8,128)(2,1)} %all-gather.2.cloned.1.call-done), kind=kOutput, calls=%fused_computation.13 | convolution fusion | flops 2416967680 | bytes 13762560 | tf_op jit(solution)/shard_map/dot_general | solution.py:48
  504.8 227.1 %reduce-scatter.7.cloned.1.call-done = f32[16,48]{1,0:T(8,128)} async-done(((f32[256,48]{1,0:T(8,128)}), f32[16,48]{1,0:T(8,128)}) %reduce-scatter.7.cloned.1.call-update) | async-done | bytes 3088
  731.9 0.8 copy.12
  732.7 0.7 copy.10
  (29 shorter events, 1.3 us)
Async XLA Ops:
  7.2 80.9 %copy-start = (bf16[1,16,128,256]{3,2,1,0:T(8,128)(2,1)S(1)}, bf16[1,16,128,256]{3,2,1,0:T(8,128)(2,1)}, u32[]{:S(2)}) copy-start(bf16[1,16,128,256]{3,2,1,0:T(8,128)(2,1)} %param.7) | copy-start | bytes 3145732
  7.2 389.3 %reduce-scatter.5.cloned.1.call-start = ((), (), s32[]{:S(2)}) async-start(), calls=%async_computation.3 | async-start | bytes 2408448 | tf_op jit(solution)/shard_map/reduce_scatter | solution.py:52
  78.0 2.6 collective-permute-start
  79.3 5.0 collective-permute-start.1
  85.1 1.2 copy-start.1
  85.1 1.2 copy-start.3
  85.1 1.2 copy-start.4
  88.1 3.6 copy-start.2
  95.9 401.0 %all-gather.2.cloned.1.call-start = ((), (), s32[]{:S(2)}) async-start(), calls=%async_computation.2 | async-start | bytes 1204224 | tf_op jit(solution)/shard_map/all_gather | solution.py:47
  96.6 635.3 %reduce-scatter.7.cloned.1.call-start = ((), (), s32[]{:S(2)}) async-start(), calls=%async_computation.4 | async-start | bytes 139264
Sparse Core Ops, SparseCore 0:
  96.0 300.4 reduce-scatter.4
  399.0 97.8 all-gather.1
  501.9 229.9 reduce-scatter.6
where the time goes:
time: 745 us; the launch traced here: 740 us
  waiting for transfers between devices  630 us (85%)
  blocking collectives  65.6 us (9%)
  between operations  13.9 us (2%)
  matrix products  12.1 us (2%)
  local copies, waits for them, and re-layouts  9.2 us (1%)
    reduce_scatter x1, waiting for transfers between devices, body(): lax.psum_scatter(lax.dot_general(patches, cot_rows, (((0,), (0,)), ((), (...  300 us
    unnamed x4, waiting for transfers between devices  228 us
    all_gather x1, waiting for transfers between devices, body(): full_weight = lax.all_gather(conv_weight, 'dp', axis=0, tiled=True)  98.8 us
    psum x1, blocking collectives, body(): lax.psum((jnp.sum(grouped, axis=(0, 1, 3)), jnp.sum(grouped * grouped, ax...  65.6 us
  transfers between devices with their start and end apart: 5, of which 4 were waited for; matrix products, arithmetic and copies ran while one was open for 1% of the time, Pallas kernels for 0%

commit v1 on v0

--- a/solution.py
+++ b/solution.py
@@ -23,16 +23,31 @@
     return cells
 
 
+def gather_a2a(x, axis):
+    n = lax.axis_size(axis)
+    spread = jnp.broadcast_to(x[None], (n,) + x.shape)
+    got = lax.all_to_all(spread, axis, 0, 0)
+    return got.reshape((n * x.shape[0],) + x.shape[1:])
+
+
+def sum_a2a(x, axis):
+    got = lax.all_to_all(x, axis, 0, 0)
+    return jnp.sum(got, axis=0)
+
+
 def body(features, cotangent, conv_weight, norm_gain, norm_bias, film_rows):
     rows = features.shape[1]
     cols = features.shape[2]
     width = features.shape[3]
+    ndp = lax.axis_size("dp")
+    ntile = lax.axis_size("tile")
+    full_weight = gather_a2a(conv_weight, "dp")
     values = features[0].astype(jnp.float32)
     grouped = values.reshape(rows, cols, G, width // G)
-    sums, squares = lax.psum(
-        (jnp.sum(grouped, axis=(0, 1, 3)), jnp.sum(grouped * grouped, axis=(0, 1, 3))), "tile"
-    )
-    count = rows * lax.axis_size("tile") * cols * (width // G)
+    stats = jnp.concatenate([jnp.sum(grouped, axis=(0, 1, 3)), jnp.sum(grouped * grouped, axis=(0, 1, 3))])
+    stats = sum_a2a(jnp.broadcast_to(stats[None], (ntile,) + stats.shape), "tile")
+    sums, squares = stats[:G], stats[G:]
+    count = rows * ntile * cols * (width // G)
     mean = sums / count
     var = squares / count - mean * mean
     mean_c = jnp.repeat(mean, width // G)
@@ -44,21 +59,18 @@
     padded = jnp.pad(extended, ((0, 0), (1, 1), (0, 0)))
     taps = [padded[i : i + rows, j : j + cols, :] for i in range(3) for j in range(3)]
     patches = jnp.concatenate(taps, axis=-1).reshape(rows * cols, 9 * width)
-    full_weight = lax.all_gather(conv_weight, "dp", axis=0, tiled=True)
+    positions = ndp * rows * ntile * cols
+    cot_rows = cotangent[0].reshape(rows * cols, width)
+    partial = lax.dot_general(
+        patches, cot_rows, (((0,), (0,)), ((), ())), preferred_element_type=jnp.float32
+    )
+    kdim = partial.shape[0]
+    summed_rows = sum_a2a(partial.reshape(ndp, kdim // ndp, width), "dp")
+    blocks = summed_rows.reshape(kdim // ndp, ntile, width // ntile).transpose(1, 0, 2)
+    grad_sum = sum_a2a(blocks, "tile")
+    grad_weight = grad_sum / jnp.sqrt(jnp.float32(positions))
     conv = jnp.dot(patches, full_weight, preferred_element_type=jnp.float32)
     output = (conv.reshape(rows, cols, width) + values)[None]
-    positions = lax.axis_size("dp") * rows * lax.axis_size("tile") * cols
-    cot_rows = cotangent[0].reshape(rows * cols, width)
-    summed_rows = lax.psum_scatter(
-        lax.dot_general(
-            patches, cot_rows, (((0,), (0,)), ((), ())), preferred_element_type=jnp.float32
-        ),
-        "dp",
-        scatter_dimension=0,
-        tiled=True,
-    )
-    grad_sum = lax.psum_scatter(summed_rows, "tile", scatter_dimension=1, tiled=True)
-    grad_weight = grad_sum / jnp.sqrt(jnp.float32(positions))
     return (output, grad_weight)
 
 

time: 745 us -> 249 us (0.33)
  waiting for transfers between devices: 630 us -> 64.2 us
  starting transfers between devices: 2.7 us -> 43.3 us
  blocking collectives: 65.6 us -> 94.9 us
  between operations: 13.9 us -> 0.86 us
  local copies, waits for them, and re-layouts: 9.2 us -> 22.1 us
    reduce_scatter x1 -> x0, waiting for transfers between devices: 300 us -> none  [body(): lax.psum_scatter(lax.dot_general(patches, cot_rows, (((0,), (0,)), ((), (...]
    unnamed x4 -> x0, waiting for transfers between devices: 228 us -> none
    all_gather x1 -> x0, waiting for transfers between devices: 98.8 us -> none  [body(): full_weight = lax.all_gather(conv_weight, 'dp', axis=0, tiled=True)]
    all_to_all x0 -> x1, blocking collectives: none -> 94.9 us  [sum_a2a(): got = lax.all_to_all(x, axis, 0, 0)]
    psum x1 -> x0, blocking collectives: 65.6 us -> none  [body(): lax.psum((jnp.sum(grouped, axis=(0, 1, 3)), jnp.sum(grouped * grouped, ax...]
    all_to_all x0 -> x3, waiting for transfers between devices: none -> 60.5 us  [the longest x1 41.6 us: gather_a2a(): got = lax.all_to_all(spread, axis, 0, 0)]
    all_to_all x0 -> x3, starting transfers between devices: none -> 39.7 us  [the longest x2 33.7 us: sum_a2a(): got = lax.all_to_all(x, axis, 0, 0)]
    dot_general x0 -> x1, local copies, waits for them, and re-layouts: none -> 12.7 us  [body(): lax.dot_general(patches, cot_rows, (((0,), (0,)), ((), ())), preferred_el...]
  transfers between devices with their start and end apart: 5 -> 5, of which waited for: 4 -> 4; matrix products, arithmetic and copies ran while one was open for 1% -> 4% of each run, Pallas kernels for 0% -> 0%
where the time goes in v1:
time: 249 us; the launch traced here: 248 us
  blocking collectives  94.9 us (38%)
  waiting for transfers between devices  64.2 us (26%)
  starting transfers between devices  43.3 us (17%)
  local copies, waits for them, and re-layouts  22.1 us (9%)
  matrix products  12.8 us (5%)
  other arithmetic  9.59 us (4%)
    all_to_all x1, blocking collectives, sum_a2a(): got = lax.all_to_all(x, axis, 0, 0)  94.9 us
    all_to_all x1, waiting for transfers between devices, gather_a2a(): got = lax.all_to_all(spread, axis, 0, 0)  41.6 us
    all_to_all x2, starting transfers between devices, sum_a2a(): got = lax.all_to_all(x, axis, 0, 0)  33.7 us
    all_to_all x2, waiting for transfers between devices, sum_a2a(): got = lax.all_to_all(x, axis, 0, 0)  18.9 us
    dot_general x1, local copies, waits for them, and re-layouts, body(): lax.dot_general(patches, cot_rows, (((0,), (0,)), ((), ())), preferred_el...  12.7 us
    dot_general x1, matrix products, body(): conv = jnp.dot(patches, full_weight, preferred_element_type=jnp.float32)  7.64 us
    unnamed x19, local copies, waits for them, and re-layouts  6.24 us
    all_to_all x1, starting transfers between devices, gather_a2a(): got = lax.all_to_all(spread, axis, 0, 0)  6.09 us
  transfers between devices with their start and end apart: 5, of which 4 were waited for; matrix products, arithmetic and copies ran while one was open for 4% of the time, Pallas kernels for 0%

profile of v1, /device:TPU:1, one launch (start us, length us, event | category | flops | bytes accessed | tf_op | source)
XLA Modules:
  0.0 247.8 jit_solution(9917629379704979946)
XLA Ops:
  0.6 1.6 convert_reduce_fusion
  2.8 0.6 broadcast_in_dim.10
  3.4 20.4 %all-to-all-start = ((f32[16,1,64]{2,1,0:T(1,128)}), f32[16,1,64]{2,1,0:T(1,128)S(1)}, u32[]{:S(2)}, u32[]{:S(2)}) async-start(f32[16,1,64]{2,1,0:T(1,128)} %broadcast_in_dim.10), calls=%async_computation | async-start | bytes 16384 | tf_op jit(solution)/shard_map/all_to_all | solution.py:34
  23.8 0.7 slice_add_fusion
  24.5 12.9 %all-to-all-done = f32[16,1,64]{2,1,0:T(1,128)S(1)} async-done(((f32[16,1,64]{2,1,0:T(1,128)}), f32[16,1,64]{2,1,0:T(1,128)S(1)}, u32[]{:S(2)}, u32[]{:S(2)}) %all-to-all-start) | async-done | bytes 4128 | tf_op jit(solution)/shard_map/all_to_all | solution.py:34
  37.8 2.1 multiply_convert_fusion
  39.9 2.2 collective-permute-start
  42.1 1.3 collective-permute-start.1
  43.5 3.7 %collective-permute-done.1 = bf16[1,128,256]{2,1,0:T(8,128)(2,1)S(1)} collective-permute-done((bf16[1,128,256]{2,1,0:T(8,128)(2,1)S(1)}, bf16[1,128,256]{2,1,0:T(8,128)(2,1)S(1)}, u32[]{:S(2)}, u32[]{:S(2)}) %collective-permute-start.1) | collective-permute-done | bytes 65568 | tf_op jit(solution)/shard_map/ppermute | solution.py:19
  48.4 0.7 copy-done.2
  49.1 0.9 constant_dynamic-update-slice_fusion
  50.9 3.6 %copy-done.1 = bf16[16,128,2304]{2,1,0:T(8,128)(2,1)} copy-done((bf16[16,128,2304]{2,1,0:T(8,128)(2,1)}, bf16[16,128,2304]{2,1,0:T(8,128)(2,1)S(1)}, u32[]{:S(2)}) %copy-start.1) | copy-done | bytes 9437208
  54.5 12.7 %copy.15 = bf16[2304,2048]{1,0:T(8,128)(2,1)} copy(bf16[2304,2048]{0,1:T(8,128)(2,1)} %bitcast.48) | data formatting | bytes 18874368 | tf_op jit(solution)/shard_map/dot_general | solution.py:64
  67.2 5.2 %fusion.18 = f32[48,48,256]{2,1,0:T(8,128)S(1)} fusion(bf16[48,48,2048]{2,1,0:T(8,128)(2,1)} %bitcast.49, bf16[2048,256,1]{1,0,2:T(8,128)(2,1)S(1)} %bitcast.47), kind=kOutput, calls=%fused_computation.39 | convolution fusion | flops 2415919104 | bytes 12845056 | tf_op jit(solution)/shard_map/dot_general | solution.py:64
  72.4 94.9 %all_to_all.21 = f32[48,48,256]{2,1,0:T(8,128)} all-to-all(f32[48,48,256]{2,1,0:T(8,128)S(1)} %fusion.18), channel_id=1, replica_groups=mesh['dp'=48,'tile'=16] {'dp'}, dimensions={0} | all-to-all | bytes 4718592 | tf_op jit(solution)/shard_map/all_to_all | solution.py:34
  167.4 1.1 broadcast_in_dim.13
  168.5 6.1 %all-to-all-start.1 = ((bf16[48,48,256]{2,1,0:T(8,128)(2,1)}), bf16[48,48,256]{2,1,0:T(8,128)(2,1)S(1)}, u32[]{:S(2)}, u32[]{:S(2)}) async-start(bf16[48,48,256]{2,1,0:T(8,128)(2,1)} %broadcast_in_dim.13), calls=%async_computation.1 | async-start | bytes 2359296 | tf_op jit(solution)/shard_map/all_to_all | solution.py:29
  174.6 1.8 reduce_sum.66
  176.5 0.8 reshape.52
  177.2 41.6 %all-to-all-done.1 = bf16[48,48,256]{2,1,0:T(8,128)(2,1)S(1)} async-done(((bf16[48,48,256]{2,1,0:T(8,128)(2,1)}), bf16[48,48,256]{2,1,0:T(8,128)(2,1)S(1)}, u32[]{:S(2)}, u32[]{:S(2)}) %all-to-all-start.1) | async-done | bytes 1179680 | tf_op jit(solution)/shard_map/all_to_all | solution.py:29
  218.8 13.2 %all-to-all-start.3 = ((f32[16,1,768]{2,1,0:T(1,128)}), f32[16,1,768]{2,1,0:T(1,128)S(1)}, u32[]{:S(2)}, u32[]{:S(2)}) async-start(f32[16,1,768]{2,1,0:T(1,128)} %reshape.52), calls=%async_computation.3 | async-start | bytes 98304 | tf_op jit(solution)/shard_map/all_to_all | solution.py:34
  232.1 7.6 %fusion.8 = f32[1,16,128,256]{3,2,1,0:T(8,128)} fusion(bf16[1,16,128,256]{3,2,1,0:T(8,128)(2,1)S(1)} %copy-done.2, bf16[16,128,2304]{2,1,0:T(8,128)(2,1)} %copy-done.1, bf16[2304,256,1]{1,0,2:T(8,128)(2,1)S(1)} %bitcast.50), kind=kOutput, calls=%fused_computation.13 | convolution fusion | flops 2416967680 | bytes 13762560 | tf_op jit(solution)/shard_map/dot_general | solution.py:72
  239.7 6.0 %all-to-all-done.3 = f32[16,1,768]{2,1,0:T(1,128)S(1)} async-done(((f32[16,1,768]{2,1,0:T(1,128)}), f32[16,1,768]{2,1,0:T(1,128)S(1)}, u32[]{:S(2)}, u32[]{:S(2)}) %all-to-all-start.3) | async-done | bytes 49184 | tf_op jit(solution)/shard_map/all_to_all | solution.py:34
  246.3 0.8 reduce.5
  (37 shorter events, 4.3 us)
Async XLA Ops:
  0.6 66.6 %copy-start = (bf16[1,16,128,256]{3,2,1,0:T(8,128)(2,1)S(1)}, bf16[1,16,128,256]{3,2,1,0:T(8,128)(2,1)}, u32[]{:S(2)}) copy-start(bf16[1,16,128,256]{3,2,1,0:T(8,128)(2,1)} %param.7) | copy-start | bytes 3145732
  3.4 34.0 %all-to-all-start = ((f32[16,1,64]{2,1,0:T(1,128)}), f32[16,1,64]{2,1,0:T(1,128)S(1)}, u32[]{:S(2)}, u32[]{:S(2)}) async-start(f32[16,1,64]{2,1,0:T(1,128)} %broadcast_in_dim.10), calls=%async_computation | async-start | bytes 16384 | tf_op jit(solution)/shard_map/all_to_all | solution.py:34
  39.9 3.5 %collective-permute-start = (bf16[1,128,256]{2,1,0:T(8,128)(2,1)S(1)}, bf16[1,128,256]{2,1,0:T(8,128)(2,1)S(1)}, u32[]{:S(2)}, u32[]{:S(2)}) collective-permute-start(bf16[1,128,256]{2,1,0:T(8,128)(2,1)S(1)} %get-tuple-element.4), channel_id=1, source_target_pairs={{0,1},{1,2},{2,3},{3,4},{4,5},{5,6},{6,7},{7,8},{8,9},{9,10},{10,1... | collective-permute-start | bytes 196616 | tf_op jit(solution)/shard_map/ppermute | solution.py:17
  42.1 5.0 %collective-permute-start.1 = (bf16[1,128,256]{2,1,0:T(8,128)(2,1)S(1)}, bf16[1,128,256]{2,1,0:T(8,128)(2,1)S(1)}, u32[]{:S(2)}, u32[]{:S(2)}) collective-permute-start(bf16[1,128,256]{2,1,0:T(8,128)(2,1)S(1)} %get-tuple-element.5), channel_id=1, source_target_pairs={{1,0},{2,1},{3,2},{4,3},{5,4},{6,5},{7,6},{8,7},{9,8},{10,9},{11,1... | collective-permute-start | bytes 196616 | tf_op jit(solution)/shard_map/ppermute | solution.py:19
  47.9 1.2 copy-start.2
  47.9 1.2 copy-start.4
  47.9 1.2 copy-start.5
  50.9 3.6 %copy-start.1 = (bf16[16,128,2304]{2,1,0:T(8,128)(2,1)}, bf16[16,128,2304]{2,1,0:T(8,128)(2,1)S(1)}, u32[]{:S(2)}) copy-start(bf16[16,128,2304]{2,1,0:T(8,128)(2,1)S(1)} %slice_dynamic-update-slice_fusion) | copy-start | bytes 28311556
  72.4 95.0 %copy-start.3 = (bf16[48,256]{1,0:T(8,128)(2,1)S(1)}, bf16[48,256]{1,0:T(8,128)(2,1)}, u32[]{:S(2)}) copy-start(bf16[48,256]{1,0:T(8,128)(2,1)} %param.8) | copy-start | bytes 73732
  168.5 50.4 %all-to-all-start.1 = ((bf16[48,48,256]{2,1,0:T(8,128)(2,1)}), bf16[48,48,256]{2,1,0:T(8,128)(2,1)S(1)}, u32[]{:S(2)}, u32[]{:S(2)}) async-start(bf16[48,48,256]{2,1,0:T(8,128)(2,1)} %broadcast_in_dim.13), calls=%async_computation.1 | async-start | bytes 2359296 | tf_op jit(solution)/shard_map/all_to_all | solution.py:29
  218.8 26.9 %all-to-all-start.3 = ((f32[16,1,768]{2,1,0:T(1,128)}), f32[16,1,768]{2,1,0:T(1,128)S(1)}, u32[]{:S(2)}, u32[]{:S(2)}) async-start(f32[16,1,768]{2,1,0:T(1,128)} %reshape.52), calls=%async_computation.3 | async-start | bytes 98304 | tf_op jit(solution)/shard_map/all_to_all | solution.py:34

commit v2 on v1

--- a/solution.py
+++ b/solution.py
@@ -4,6 +4,27 @@
 from jax.sharding import PartitionSpec as P
 
 G = 32
+
+DP_SUB = {"x": (12, 4), "zl": (2, 6), "c": (1, 2)}
+TILE_SUB = {"zh": (8, 2), "y": (1, 8)}
+
+
+def sub_of(name):
+    if name in DP_SUB:
+        return ("dp",) + DP_SUB[name]
+    return ("tile",) + TILE_SUB[name]
+
+
+def shift_pairs(total, stride, size, j):
+    pairs = []
+    for i in range(total):
+        k = (i // stride) % size
+        pairs.append((i, i + ((k + j) % size - k) * stride))
+    return pairs
+
+
+def coord(axis, stride, size):
+    return (lax.axis_index(axis) // stride) % size
 
 
 def extended_2(cells, sides, width):
@@ -23,16 +44,36 @@
     return cells
 
 
-def gather_a2a(x, axis):
-    n = lax.axis_size(axis)
-    spread = jnp.broadcast_to(x[None], (n,) + x.shape)
-    got = lax.all_to_all(spread, axis, 0, 0)
-    return got.reshape((n * x.shape[0],) + x.shape[1:])
+def stage_gather(y, name):
+    axis, stride, size = sub_of(name)
+    total = lax.axis_size(axis)
+    k = coord(axis, stride, size)
+    out = jnp.zeros((size,) + y.shape, y.dtype)
+    out = lax.dynamic_update_index_in_dim(out, y, k, 0)
+    for j in range(1, size):
+        got = lax.ppermute(y, axis, shift_pairs(total, stride, size, j))
+        out = lax.dynamic_update_index_in_dim(out, got, (k - j) % size, 0)
+    return out
 
 
-def sum_a2a(x, axis):
-    got = lax.all_to_all(x, axis, 0, 0)
-    return jnp.sum(got, axis=0)
+def stage_scatter(x, name):
+    axis, stride, size = sub_of(name)
+    total = lax.axis_size(axis)
+    k = coord(axis, stride, size)
+    acc = lax.dynamic_index_in_dim(x, k, 0, keepdims=False)
+    for j in range(1, size):
+        piece = lax.dynamic_index_in_dim(x, (k + j) % size, 0, keepdims=False)
+        acc = acc + lax.ppermute(piece, axis, shift_pairs(total, stride, size, j))
+    return acc
+
+
+def tile_allreduce(v):
+    total = lax.axis_size("tile")
+    step = 1
+    while step < total:
+        v = v + lax.ppermute(v, "tile", [(i, i ^ step) for i in range(total)])
+        step *= 2
+    return v
 
 
 def body(features, cotangent, conv_weight, norm_gain, norm_bias, film_rows):
@@ -41,11 +82,14 @@
     width = features.shape[3]
     ndp = lax.axis_size("dp")
     ntile = lax.axis_size("tile")
-    full_weight = gather_a2a(conv_weight, "dp")
+    w = stage_gather(conv_weight, "c")
+    w = stage_gather(w, "zl")
+    w = stage_gather(w, "x")
+    full_weight = w.reshape(ndp * conv_weight.shape[0], width)
     values = features[0].astype(jnp.float32)
     grouped = values.reshape(rows, cols, G, width // G)
     stats = jnp.concatenate([jnp.sum(grouped, axis=(0, 1, 3)), jnp.sum(grouped * grouped, axis=(0, 1, 3))])
-    stats = sum_a2a(jnp.broadcast_to(stats[None], (ntile,) + stats.shape), "tile")
+    stats = tile_allreduce(stats)
     sums, squares = stats[:G], stats[G:]
     count = rows * ntile * cols * (width // G)
     mean = sums / count
@@ -61,14 +105,20 @@
     patches = jnp.concatenate(taps, axis=-1).reshape(rows * cols, 9 * width)
     positions = ndp * rows * ntile * cols
     cot_rows = cotangent[0].reshape(rows * cols, width)
-    partial = lax.dot_general(
-        patches, cot_rows, (((0,), (0,)), ((), ())), preferred_element_type=jnp.float32
+    part_t = lax.dot_general(
+        cot_rows, patches, (((0,), (0,)), ((), ())), preferred_element_type=jnp.float32
     )
-    kdim = partial.shape[0]
-    summed_rows = sum_a2a(partial.reshape(ndp, kdim // ndp, width), "dp")
-    blocks = summed_rows.reshape(kdim // ndp, ntile, width // ntile).transpose(1, 0, 2)
-    grad_sum = sum_a2a(blocks, "tile")
-    grad_weight = grad_sum / jnp.sqrt(jnp.float32(positions))
+    kdim = part_t.shape[1]
+    per = kdim // ndp
+    q = width // ntile
+    g = part_t.reshape(2, 8, q, 4, 6, 2, per)
+    g = g.transpose(5, 1, 4, 3, 0, 6, 2).reshape(2, 8, 6, 4, 2, per * q)
+    g = stage_scatter(g, "c")
+    g = stage_scatter(g, "y")
+    g = stage_scatter(g, "zl")
+    g = stage_scatter(g, "x")
+    g = stage_scatter(g, "zh")
+    grad_weight = g.reshape(per, q) / jnp.sqrt(jnp.float32(positions))
     conv = jnp.dot(patches, full_weight, preferred_element_type=jnp.float32)
     output = (conv.reshape(rows, cols, width) + values)[None]
     return (output, grad_weight)

time: 249 us -> 245 us (0.984)
  blocking collectives: 94.9 us -> 0 us
  starting transfers between devices: 43.3 us -> 133 us
  local copies, waits for them, and re-layouts: 22.1 us -> 55.5 us
  waiting for transfers between devices: 64.2 us -> 33.8 us
  other arithmetic: 9.59 us -> 5.75 us
    ppermute x0 -> x30, starting transfers between devices: none -> 128 us  [the longest x17 72.6 us: stage_scatter(): acc = acc + lax.ppermute(piece, axis, shift_pairs(total, stride, size, j))]
    all_to_all x1 -> x0, blocking collectives: 94.9 us -> none  [sum_a2a(): got = lax.all_to_all(x, axis, 0, 0)]
    all_to_all x3 -> x0, waiting for transfers between devices: 60.5 us -> none  [the longest x1 41.6 us: gather_a2a(): got = lax.all_to_all(spread, axis, 0, 0)]
    all_to_all x3 -> x0, starting transfers between devices: 39.7 us -> none  [the longest x2 33.7 us: sum_a2a(): got = lax.all_to_all(x, axis, 0, 0)]
    ppermute x0 -> x30, waiting for transfers between devices: none -> 33.8 us  [the longest x17 20.1 us: stage_scatter(): acc = acc + lax.ppermute(piece, axis, shift_pairs(total, stride, size, j))]
    reshape x0 -> x2, local copies, waits for them, and re-layouts: none -> 25.7 us  [the longest x1 13.6 us: body(): g = g.transpose(5, 1, 4, 3, 0, 6, 2).reshape(2, 8, 6, 4, 2, per * q)]
    transpose x0 -> x1, local copies, waits for them, and re-layouts: none -> 16 us  [body(): g = g.transpose(5, 1, 4, 3, 0, 6, 2).reshape(2, 8, 6, 4, 2, per * q)]
    dot_general x1, local copies, waits for them, and re-layouts: 12.7 us -> 3.08 us  [body(): lax.dot_general(cot_rows, patches, (((0,), (0,)), ((), ())), preferred_el...]
  transfers between devices with their start and end apart: 5 -> 32, of which waited for: 4 -> 10; matrix products, arithmetic and copies ran while one was open for 4% -> 27% of each run, Pallas kernels for 0% -> 0%
where the time goes in v2:
time: 245 us; the launch traced here: 242 us
  starting transfers between devices  133 us (54%)
  local copies, waits for them, and re-layouts  55.5 us (23%)
  waiting for transfers between devices  33.8 us (14%)
  matrix products  11.9 us (5%)
  other arithmetic  5.75 us (2%)
    ppermute x17, starting transfers between devices, stage_scatter(): acc = acc + lax.ppermute(piece, axis, shift_pairs(total, stride, size, j))  72.6 us
    ppermute x9, starting transfers between devices, stage_gather(): got = lax.ppermute(y, axis, shift_pairs(total, stride, size, j))  39.7 us
    ppermute x17, waiting for transfers between devices, stage_scatter(): acc = acc + lax.ppermute(piece, axis, shift_pairs(total, stride, size, j))  20.1 us
    transpose x1, local copies, waits for them, and re-layouts, body(): g = g.transpose(5, 1, 4, 3, 0, 6, 2).reshape(2, 8, 6, 4, 2, per * q)  16 us
    ppermute x4, starting transfers between devices, tile_allreduce(): v = v + lax.ppermute(v, 'tile', [(i, i ^ step) for i in range(total)])  15.3 us
    reshape x1, local copies, waits for them, and re-layouts, body(): g = g.transpose(5, 1, 4, 3, 0, 6, 2).reshape(2, 8, 6, 4, 2, per * q)  13.6 us
    ppermute x4, waiting for transfers between devices, tile_allreduce(): v = v + lax.ppermute(v, 'tile', [(i, i ^ step) for i in range(total)])  12.7 us
    reshape x1, local copies, waits for them, and re-layouts, body(): g = part_t.reshape(2, 8, q, 4, 6, 2, per)  12.1 us
  transfers between devices with their start and end apart: 32, of which 10 were waited for; matrix products, arithmetic and copies ran while one was open for 27% of the time, Pallas kernels for 0%

profile of v2, /device:TPU:1, one launch (start us, length us, event | category | flops | bytes accessed | tf_op | source)
XLA Modules:
  0.0 242.3 jit_solution(1955702512283620976)
XLA Ops:
  2.8 4.0 %collective-permute-start = (f32[64]{0:T(128)S(1)}, f32[64]{0:T(128)S(1)}, u32[]{:S(2)}, u32[]{:S(2)}) collective-permute-start(f32[64]{0:T(128)S(1)} %pad_maximum_fusion.2), channel_id=1, source_target_pairs={{0,1},{1,0},{2,3},{3,2},{4,5},{5,4},{6,7},{7,6},{8,9},{9,8},{10,11... | collective-permute-start | bytes 776 | tf_op jit(solution)/shard_map/ppermute | solution.py:74
  6.9 10.3 %collective-permute-start.6 = (bf16[48,256]{1,0:T(8,128)(2,1)}, bf16[48,256]{1,0:T(8,128)(2,1)S(1)}, u32[]{:S(2)}, u32[]{:S(2)}) collective-permute-start(bf16[48,256]{1,0:T(8,128)(2,1)} %param.8), channel_id=1, source_target_pairs={{0,16},{16,0},{32,48},{48,32},{64,80},{80,64},{96,112},{112,96},{1... | collective-permute-start | bytes 73736 | tf_op jit(solution)/shard_map/ppermute | solution.py:54
  26.5 6.3 %collective-permute-done.2 = f32[64]{0:T(128)S(1)} collective-permute-done((f32[64]{0:T(128)S(1)}, f32[64]{0:T(128)S(1)}, u32[]{:S(2)}, u32[]{:S(2)}) %collective-permute-start.2) | collective-permute-done | bytes 288 | tf_op jit(solution)/shard_map/ppermute | solution.py:74
  32.7 7.4 %collective-permute-start.3 = (f32[64]{0:T(128)S(1)}, f32[64]{0:T(128)S(1)}, u32[]{:S(2)}, u32[]{:S(2)}) collective-permute-start(f32[64]{0:T(128)S(1)} %add.377), channel_id=1, source_target_pairs={{0,8},{1,9},{2,10},{3,11},{4,12},{5,13},{6,14},{7,15},{8,0},{9,1},... | collective-permute-start | bytes 776 | tf_op jit(solution)/shard_map/ppermute | solution.py:74
  46.0 4.3 %collective-permute-start.4 = (bf16[1,128,256]{2,1,0:T(8,128)(2,1)S(1)}, bf16[1,128,256]{2,1,0:T(8,128)(2,1)S(1)}, u32[]{:S(2)}, u32[]{:S(2)}) collective-permute-start(bf16[1,128,256]{2,1,0:T(8,128)(2,1)S(1)} %get-tuple-element.16), channel_id=1, source_target_pairs={{0,1},{1,2},{2,3},{3,4},{4,5},{5,6},{6,7},{7,8},{8,9},{9,10},{10,1... | collective-permute-start | bytes 196616 | tf_op jit(solution)/shard_map/ppermute | solution.py:38
  54.9 7.7 %collective-permute-start.9 = (bf16[2,48,256]{2,1,0:T(8,128)(2,1)S(1)}, bf16[2,48,256]{2,1,0:T(8,128)(2,1)S(1)}, u32[]{:S(2)}, u32[]{:S(2)}) collective-permute-start(bf16[2,48,256]{2,1,0:T(8,128)(2,1)S(1)} %bitcast_dynamic-update-slice_fusion.10), channel_id=1, source_target_pairs={{0,96},{16,112},{32,128},{48,144},{64,160},{80,176},{96,0},{112,16... | collective-permute-start | bytes 147464 | tf_op jit(solution)/shard_map/ppermute | solution.py:54
  67.9 3.7 %copy-done.3 = bf16[16,128,2304]{2,1,0:T(8,128)(2,1)} copy-done((bf16[16,128,2304]{2,1,0:T(8,128)(2,1)}, bf16[16,128,2304]{2,1,0:T(8,128)(2,1)S(1)}, u32[]{:S(2)}) %copy-start.3) | copy-done | bytes 9437208
  71.6 4.2 %convolution_bitcast_fusion = f32[256,2304]{0,1:T(8,128)} fusion(bf16[2048,2304]{1,0:T(8,128)(2,1)S(1)} %bitcast.149, bf16[2048,256]{1,0:T(8,128)(2,1)S(1)} %bitcast.139), kind=kOutput, calls=%fused_computation | convolution fusion | flops 2415919104 | bytes 12845056 | tf_op jit(solution)/shard_map/dot_general | solution.py:108
  78.9 12.1 %reshape.45 = f32[2,8,16,4,6,2,48]{6,5,4,3,2,1,0:T(2,128)} reshape(f32[256,2304]{1,0:T(8,128)} %copy.8) | data formatting | bytes 4718592 | tf_op jit(solution)/shard_map/reshape | solution.py:114
  91.0 16.0 %copy.9 = f32[2,8,6,4,2,48,16]{6,5,1,4,3,2,0:T(8,128)} copy(f32[2,8,6,4,2,48,16]{5,0,2,3,6,1,4:T(2,128)} %bitcast.140) | data formatting | bytes 4718592 | tf_op jit(solution)/shard_map/transpose | solution.py:115
  107.0 13.6 %reshape.46 = f32[2,8,6,4,2,768]{5,1,4,3,2,0:T(8,128)} reshape(f32[2,8,6,4,2,48,16]{6,5,1,4,3,2,0:T(8,128)} %copy.9) | data formatting | bytes 4718592 | tf_op jit(solution)/shard_map/reshape | solution.py:115
  122.1 6.8 %collective-permute-start.15 = (f32[8,6,4,2,768]{4,0,3,2,1:T(8,128)S(1)}, f32[8,6,4,2,768]{4,0,3,2,1:T(8,128)S(1)}, u32[]{:S(2)}, u32[]{:S(2)}) collective-permute-start(f32[8,6,4,2,768]{4,0,3,2,1:T(8,128)S(1)} %dynamic-slice_bitcast_fusion), channel_id=1, source_target_pairs={{0,16},{16,0},{32,48},{48,32},{64,80},{80,64},{96,112},{112,96},{1... | collective-permute-start | bytes 3538952 | tf_op jit(solution)/shard_map/ppermute | solution.py:66
  128.9 4.7 %collective-permute-start.11 = (bf16[2,48,256]{2,1,0:T(8,128)(2,1)S(1)}, bf16[2,48,256]{2,1,0:T(8,128)(2,1)S(1)}, u32[]{:S(2)}, u32[]{:S(2)}) collective-permute-start(bf16[2,48,256]{2,1,0:T(8,128)(2,1)S(1)} %bitcast_dynamic-update-slice_fusion.10), channel_id=1, source_target_pairs={{0,160},{16,176},{32,0},{48,16},{64,32},{80,48},{96,64},{112,80},{... | collective-permute-start | bytes 147464 | tf_op jit(solution)/shard_map/ppermute | solution.py:54
  138.8 13.3 %collective-permute-start.22 = (f32[6,4,2,768]{3,2,1,0:T(2,128)S(1)}, f32[6,4,2,768]{3,2,1,0:T(2,128)S(1)}, u32[]{:S(2)}, u32[]{:S(2)}) collective-permute-start(f32[6,4,2,768]{3,2,1,0:T(2,128)S(1)} %bitcast.148), channel_id=1, source_target_pairs={{0,7},{1,0},{2,1},{3,2},{4,3},{5,4},{6,5},{7,6},{8,15},{9,8},{10,9... | collective-permute-start | bytes 442376 | tf_op jit(solution)/shard_map/ppermute | solution.py:66
  156.3 7.5 %collective-permute-start.19 = (f32[6,4,2,768]{3,2,1,0:T(2,128)S(1)}, f32[6,4,2,768]{3,2,1,0:T(2,128)S(1)}, u32[]{:S(2)}, u32[]{:S(2)}) collective-permute-start(f32[6,4,2,768]{3,2,1,0:T(2,128)S(1)} %bitcast.143), channel_id=1, source_target_pairs={{0,4},{1,5},{2,6},{3,7},{4,0},{5,1},{6,2},{7,3},{8,12},{9,13},{10,... | collective-permute-start | bytes 442376 | tf_op jit(solution)/shard_map/ppermute | solution.py:66
  172.6 4.4 %collective-permute-start.13 = (bf16[6,2,48,256]{3,2,1,0:T(8,128)(2,1)S(1)}, bf16[6,2,48,256]{3,2,1,0:T(8,128)(2,1)S(1)}, u32[]{:S(2)}, u32[]{:S(2)}) collective-permute-start(bf16[6,2,48,256]{3,2,1,0:T(8,128)(2,1)S(1)} %bitcast_dynamic-update-slice_fusion.4), channel_id=1, source_target_pairs={{0,384},{16,400},{32,416},{48,432},{64,448},{80,464},{96,480},{112... | collective-permute-start | bytes 884744 | tf_op jit(solution)/shard_map/ppermute | solution.py:54
  177.7 8.3 %collective-permute-done.17 = f32[6,4,2,768]{3,2,1,0:T(2,128)S(1)} collective-permute-done((f32[6,4,2,768]{3,2,1,0:T(2,128)S(1)}, f32[6,4,2,768]{3,2,1,0:T(2,128)S(1)}, u32[]{:S(2)}, u32[]{:S(2)}) %collective-permute-start.17) | collective-permute-done | bytes 147488 | tf_op jit(solution)/shard_map/ppermute | solution.py:66
  186.0 4.6 %collective-permute-done.16 = f32[6,4,2,768]{3,2,1,0:T(2,128)S(1)} collective-permute-done((f32[6,4,2,768]{3,2,1,0:T(2,128)S(1)}, f32[6,4,2,768]{3,2,1,0:T(2,128)S(1)}, u32[]{:S(2)}, u32[]{:S(2)}) %collective-permute-start.16) | collective-permute-done | bytes 147488 | tf_op jit(solution)/shard_map/ppermute | solution.py:66
  190.9 7.6 %collective-permute-start.27 = (f32[4,2,768]{2,1,0:T(2,128)S(1)}, f32[4,2,768]{2,1,0:T(2,128)S(1)}, u32[]{:S(2)}, u32[]{:S(2)}) collective-permute-start(f32[4,2,768]{2,1,0:T(2,128)S(1)} %get-tuple-element.19), channel_id=1, source_target_pairs={{0,160},{16,176},{32,0},{48,16},{64,32},{80,48},{96,64},{112,80},{... | collective-permute-start | bytes 73736 | tf_op jit(solution)/shard_map/ppermute | solution.py:66
  202.3 4.3 %collective-permute-start.24 = (f32[4,2,768]{2,1,0:T(2,128)S(1)}, f32[4,2,768]{2,1,0:T(2,128)S(1)}, u32[]{:S(2)}, u32[]{:S(2)}) collective-permute-start(f32[4,2,768]{2,1,0:T(2,128)S(1)} %get-tuple-element.22), channel_id=1, source_target_pairs={{0,64},{16,80},{32,96},{48,112},{64,128},{80,144},{96,160},{112,17... | collective-permute-start | bytes 73736 | tf_op jit(solution)/shard_map/ppermute | solution.py:66
  219.4 3.4 %collective-permute-start.29 = (f32[2,768]{1,0:T(2,128)S(1)}, f32[2,768]{1,0:T(2,128)S(1)}, u32[]{:S(2)}, u32[]{:S(2)}) collective-permute-start(f32[2,768]{1,0:T(2,128)S(1)} %get-tuple-element.25), channel_id=1, source_target_pairs={{0,384},{16,400},{32,416},{48,432},{64,448},{80,464},{96,480},{112... | collective-permute-start | bytes 18440 | tf_op jit(solution)/shard_map/ppermute | solution.py:66
  225.3 3.5 %collective-permute-done.28 = f32[2,768]{1,0:T(2,128)S(1)} collective-permute-done((f32[2,768]{1,0:T(2,128)S(1)}, f32[2,768]{1,0:T(2,128)S(1)}, u32[]{:S(2)}, u32[]{:S(2)}) %collective-permute-start.28) | collective-permute-done | bytes 6176 | tf_op jit(solution)/shard_map/ppermute | solution.py:66
  228.8 5.1 %collective-permute-start.31 = (f32[768]{0:T(1024)S(1)}, f32[768]{0:T(1024)S(1)}, u32[]{:S(2)}, u32[]{:S(2)}) collective-permute-start(f32[768]{0:T(1024)S(1)} %get-tuple-element.6), channel_id=1, source_target_pairs={{0,8},{1,9},{2,10},{3,11},{4,12},{5,13},{6,14},{7,15},{8,0},{9,1},... | collective-permute-start | bytes 9224 | tf_op jit(solution)/shard_map/ppermute | solution.py:66
  233.8 7.7 %fusion.8 = f32[1,16,128,256]{3,2,1,0:T(8,128)} fusion(bf16[1,16,128,256]{3,2,1,0:T(8,128)(2,1)S(1)} %copy-done.1, bf16[16,128,2304]{2,1,0:T(8,128)(2,1)} %copy-done.3, bf16[2304,256,1]{1,0,2:T(8,128)(2,1)S(1)} %bitcast.141), kind=kOutput, calls=%fused_computation.14 | convolution fusion | flops 2416967680 | bytes 13762560 | tf_op jit(solution)/shard_map/dot_general | solution.py:122
  (120 shorter events, 69.7 us)
Async XLA Ops:
  2.8 16.4 %collective-permute-start = (f32[64]{0:T(128)S(1)}, f32[64]{0:T(128)S(1)}, u32[]{:S(2)}, u32[]{:S(2)}) collective-permute-start(f32[64]{0:T(128)S(1)} %pad_maximum_fusion.2), channel_id=1, source_target_pairs={{0,1},{1,0},{2,3},{3,2},{4,5},{5,4},{6,7},{7,6},{8,9},{9,8},{10,11... | collective-permute-start | bytes 776 | tf_op jit(solution)/shard_map/ppermute | solution.py:74
  6.9 43.4 %collective-permute-start.6 = (bf16[48,256]{1,0:T(8,128)(2,1)}, bf16[48,256]{1,0:T(8,128)(2,1)S(1)}, u32[]{:S(2)}, u32[]{:S(2)}) collective-permute-start(bf16[48,256]{1,0:T(8,128)(2,1)} %param.8), channel_id=1, source_target_pairs={{0,16},{16,0},{32,48},{48,32},{64,80},{80,64},{96,112},{112,96},{1... | collective-permute-start | bytes 73736 | tf_op jit(solution)/shard_map/ppermute | solution.py:54
  44.7 17.9 %collective-permute-start.5 = (bf16[1,128,256]{2,1,0:T(8,128)(2,1)S(1)}, bf16[1,128,256]{2,1,0:T(8,128)(2,1)S(1)}, u32[]{:S(2)}, u32[]{:S(2)}) collective-permute-start(bf16[1,128,256]{2,1,0:T(8,128)(2,1)S(1)} %get-tuple-element.17), channel_id=1, source_target_pairs={{1,0},{2,1},{3,2},{4,3},{5,4},{6,5},{7,6},{8,7},{9,8},{10,9},{11,1... | collective-permute-start | bytes 196616 | tf_op jit(solution)/shard_map/ppermute | solution.py:40
  46.0 18.9 %collective-permute-start.4 = (bf16[1,128,256]{2,1,0:T(8,128)(2,1)S(1)}, bf16[1,128,256]{2,1,0:T(8,128)(2,1)S(1)}, u32[]{:S(2)}, u32[]{:S(2)}) collective-permute-start(bf16[1,128,256]{2,1,0:T(8,128)(2,1)S(1)} %get-tuple-element.16), channel_id=1, source_target_pairs={{0,1},{1,2},{2,3},{3,4},{4,5},{5,6},{6,7},{7,8},{8,9},{9,10},{10,1... | collective-permute-start | bytes 196616 | tf_op jit(solution)/shard_map/ppermute | solution.py:38
  50.3 78.6 %collective-permute-start.7 = (bf16[2,48,256]{2,1,0:T(8,128)(2,1)S(1)}, bf16[2,48,256]{2,1,0:T(8,128)(2,1)S(1)}, u32[]{:S(2)}, u32[]{:S(2)}) collective-permute-start(bf16[2,48,256]{2,1,0:T(8,128)(2,1)S(1)} %bitcast_dynamic-update-slice_fusion.10), channel_id=1, source_target_pairs={{0,32},{16,48},{32,64},{48,80},{64,96},{80,112},{96,128},{112,144}... | collective-permute-start | bytes 147464 | tf_op jit(solution)/shard_map/ppermute | solution.py:54
  52.2 81.4 %collective-permute-start.8 = (bf16[2,48,256]{2,1,0:T(8,128)(2,1)S(1)}, bf16[2,48,256]{2,1,0:T(8,128)(2,1)S(1)}, u32[]{:S(2)}, u32[]{:S(2)}) collective-permute-start(bf16[2,48,256]{2,1,0:T(8,128)(2,1)S(1)} %bitcast_dynamic-update-slice_fusion.10), channel_id=1, source_target_pairs={{0,64},{16,80},{32,96},{48,112},{64,128},{80,144},{96,160},{112,17... | collective-permute-start | bytes 147464 | tf_op jit(solution)/shard_map/ppermute | solution.py:54
  54.9 78.8 %collective-permute-start.9 = (bf16[2,48,256]{2,1,0:T(8,128)(2,1)S(1)}, bf16[2,48,256]{2,1,0:T(8,128)(2,1)S(1)}, u32[]{:S(2)}, u32[]{:S(2)}) collective-permute-start(bf16[2,48,256]{2,1,0:T(8,128)(2,1)S(1)} %bitcast_dynamic-update-slice_fusion.10), channel_id=1, source_target_pairs={{0,96},{16,112},{32,128},{48,144},{64,160},{80,176},{96,0},{112,16... | collective-permute-start | bytes 147464 | tf_op jit(solution)/shard_map/ppermute | solution.py:54
  62.6 71.1 %collective-permute-start.10 = (bf16[2,48,256]{2,1,0:T(8,128)(2,1)S(1)}, bf16[2,48,256]{2,1,0:T(8,128)(2,1)S(1)}, u32[]{:S(2)}, u32[]{:S(2)}) collective-permute-start(bf16[2,48,256]{2,1,0:T(8,128)(2,1)S(1)} %bitcast_dynamic-update-slice_fusion.10), channel_id=1, source_target_pairs={{0,128},{16,144},{32,160},{48,176},{64,0},{80,16},{96,32},{112,48}... | collective-permute-start | bytes 147464 | tf_op jit(solution)/shard_map/ppermute | solution.py:54
  122.1 15.1 %collective-permute-start.15 = (f32[8,6,4,2,768]{4,0,3,2,1:T(8,128)S(1)}, f32[8,6,4,2,768]{4,0,3,2,1:T(8,128)S(1)}, u32[]{:S(2)}, u32[]{:S(2)}) collective-permute-start(f32[8,6,4,2,768]{4,0,3,2,1:T(8,128)S(1)} %dynamic-slice_bitcast_fusion), channel_id=1, source_target_pairs={{0,16},{16,0},{32,48},{48,32},{64,80},{80,64},{96,112},{112,96},{1... | collective-permute-start | bytes 3538952 | tf_op jit(solution)/shard_map/ppermute | solution.py:66
  134.8 29.3 %collective-permute-start.12 = (bf16[6,2,48,256]{3,2,1,0:T(8,128)(2,1)S(1)}, bf16[6,2,48,256]{3,2,1,0:T(8,128)(2,1)S(1)}, u32[]{:S(2)}, u32[]{:S(2)}) collective-permute-start(bf16[6,2,48,256]{3,2,1,0:T(8,128)(2,1)S(1)} %bitcast_dynamic-update-slice_fusion.4), channel_id=1, source_target_pairs={{0,192},{16,208},{32,224},{48,240},{64,256},{80,272},{96,288},{112... | collective-permute-start | bytes 884744 | tf_op jit(solution)/shard_map/ppermute | solution.py:54
  138.8 27.3 %collective-permute-start.22 = (f32[6,4,2,768]{3,2,1,0:T(2,128)S(1)}, f32[6,4,2,768]{3,2,1,0:T(2,128)S(1)}, u32[]{:S(2)}, u32[]{:S(2)}) collective-permute-start(f32[6,4,2,768]{3,2,1,0:T(2,128)S(1)} %bitcast.148), channel_id=1, source_target_pairs={{0,7},{1,0},{2,1},{3,2},{4,3},{5,4},{6,5},{7,6},{8,15},{9,8},{10,9... | collective-permute-start | bytes 442376 | tf_op jit(solution)/shard_map/ppermute | solution.py:66
  152.1 17.3 %collective-permute-start.21 = (f32[6,4,2,768]{3,2,1,0:T(2,128)S(1)}, f32[6,4,2,768]{3,2,1,0:T(2,128)S(1)}, u32[]{:S(2)}, u32[]{:S(2)}) collective-permute-start(f32[6,4,2,768]{3,2,1,0:T(2,128)S(1)} %bitcast.147), channel_id=1, source_target_pairs={{0,6},{1,7},{2,0},{3,1},{4,2},{5,3},{6,4},{7,5},{8,14},{9,15},{10,... | collective-permute-start | bytes 442376 | tf_op jit(solution)/shard_map/ppermute | solution.py:66
  154.3 18.2 %collective-permute-start.20 = (f32[6,4,2,768]{3,2,1,0:T(2,128)S(1)}, f32[6,4,2,768]{3,2,1,0:T(2,128)S(1)}, u32[]{:S(2)}, u32[]{:S(2)}) collective-permute-start(f32[6,4,2,768]{3,2,1,0:T(2,128)S(1)} %bitcast.145), channel_id=1, source_target_pairs={{0,5},{1,6},{2,7},{3,0},{4,1},{5,2},{6,3},{7,4},{8,13},{9,14},{10,... | collective-permute-start | bytes 442376 | tf_op jit(solution)/shard_map/ppermute | solution.py:66
  156.3 20.6 %collective-permute-start.19 = (f32[6,4,2,768]{3,2,1,0:T(2,128)S(1)}, f32[6,4,2,768]{3,2,1,0:T(2,128)S(1)}, u32[]{:S(2)}, u32[]{:S(2)}) collective-permute-start(f32[6,4,2,768]{3,2,1,0:T(2,128)S(1)} %bitcast.143), channel_id=1, source_target_pairs={{0,4},{1,5},{2,6},{3,7},{4,0},{5,1},{6,2},{7,3},{8,12},{9,13},{10,... | collective-permute-start | bytes 442376 | tf_op jit(solution)/shard_map/ppermute | solution.py:66
  164.1 13.6 %collective-permute-start.18 = (f32[6,4,2,768]{3,2,1,0:T(2,128)S(1)}, f32[6,4,2,768]{3,2,1,0:T(2,128)S(1)}, u32[]{:S(2)}, u32[]{:S(2)}) collective-permute-start(f32[6,4,2,768]{3,2,1,0:T(2,128)S(1)} %bitcast.146), channel_id=1, source_target_pairs={{0,3},{1,4},{2,5},{3,6},{4,7},{5,0},{6,1},{7,2},{8,11},{9,12},{10,... | collective-permute-start | bytes 442376 | tf_op jit(solution)/shard_map/ppermute | solution.py:66
  166.0 20.0 %collective-permute-start.17 = (f32[6,4,2,768]{3,2,1,0:T(2,128)S(1)}, f32[6,4,2,768]{3,2,1,0:T(2,128)S(1)}, u32[]{:S(2)}, u32[]{:S(2)}) collective-permute-start(f32[6,4,2,768]{3,2,1,0:T(2,128)S(1)} %bitcast.144), channel_id=1, source_target_pairs={{0,2},{1,3},{2,4},{3,5},{4,6},{5,7},{6,0},{7,1},{8,10},{9,11},{10,... | collective-permute-start | bytes 442376 | tf_op jit(solution)/shard_map/ppermute | solution.py:66
  169.4 21.2 %collective-permute-start.16 = (f32[6,4,2,768]{3,2,1,0:T(2,128)S(1)}, f32[6,4,2,768]{3,2,1,0:T(2,128)S(1)}, u32[]{:S(2)}, u32[]{:S(2)}) collective-permute-start(f32[6,4,2,768]{3,2,1,0:T(2,128)S(1)} %bitcast.142), channel_id=1, source_target_pairs={{0,1},{1,2},{2,3},{3,4},{4,5},{5,6},{6,7},{7,0},{8,9},{9,10},{10,1... | collective-permute-start | bytes 442376 | tf_op jit(solution)/shard_map/ppermute | solution.py:66
  172.6 34.0 %collective-permute-start.13 = (bf16[6,2,48,256]{3,2,1,0:T(8,128)(2,1)S(1)}, bf16[6,2,48,256]{3,2,1,0:T(8,128)(2,1)S(1)}, u32[]{:S(2)}, u32[]{:S(2)}) collective-permute-start(bf16[6,2,48,256]{3,2,1,0:T(8,128)(2,1)S(1)} %bitcast_dynamic-update-slice_fusion.4), channel_id=1, source_target_pairs={{0,384},{16,400},{32,416},{48,432},{64,448},{80,464},{96,480},{112... | collective-permute-start | bytes 884744 | tf_op jit(solution)/shard_map/ppermute | solution.py:54
  190.9 18.8 %collective-permute-start.27 = (f32[4,2,768]{2,1,0:T(2,128)S(1)}, f32[4,2,768]{2,1,0:T(2,128)S(1)}, u32[]{:S(2)}, u32[]{:S(2)}) collective-permute-start(f32[4,2,768]{2,1,0:T(2,128)S(1)} %get-tuple-element.19), channel_id=1, source_target_pairs={{0,160},{16,176},{32,0},{48,16},{64,32},{80,48},{96,64},{112,80},{... | collective-permute-start | bytes 73736 | tf_op jit(solution)/shard_map/ppermute | solution.py:66
  198.4 14.7 %collective-permute-start.26 = (f32[4,2,768]{2,1,0:T(2,128)S(1)}, f32[4,2,768]{2,1,0:T(2,128)S(1)}, u32[]{:S(2)}, u32[]{:S(2)}) collective-permute-start(f32[4,2,768]{2,1,0:T(2,128)S(1)} %get-tuple-element.20), channel_id=1, source_target_pairs={{0,128},{16,144},{32,160},{48,176},{64,0},{80,16},{96,32},{112,48}... | collective-permute-start | bytes 73736 | tf_op jit(solution)/shard_map/ppermute | solution.py:66
  200.4 12.7 %collective-permute-start.25 = (f32[4,2,768]{2,1,0:T(2,128)S(1)}, f32[4,2,768]{2,1,0:T(2,128)S(1)}, u32[]{:S(2)}, u32[]{:S(2)}) collective-permute-start(f32[4,2,768]{2,1,0:T(2,128)S(1)} %get-tuple-element.21), channel_id=1, source_target_pairs={{0,96},{16,112},{32,128},{48,144},{64,160},{80,176},{96,0},{112,16... | collective-permute-start | bytes 73736 | tf_op jit(solution)/shard_map/ppermute | solution.py:66
  202.3 10.8 %collective-permute-start.24 = (f32[4,2,768]{2,1,0:T(2,128)S(1)}, f32[4,2,768]{2,1,0:T(2,128)S(1)}, u32[]{:S(2)}, u32[]{:S(2)}) collective-permute-start(f32[4,2,768]{2,1,0:T(2,128)S(1)} %get-tuple-element.22), channel_id=1, source_target_pairs={{0,64},{16,80},{32,96},{48,112},{64,128},{80,144},{96,160},{112,17... | collective-permute-start | bytes 73736 | tf_op jit(solution)/shard_map/ppermute | solution.py:66
  209.7 15.4 %collective-permute-start.14 = (bf16[6,2,48,256]{3,2,1,0:T(8,128)(2,1)S(1)}, bf16[6,2,48,256]{3,2,1,0:T(8,128)(2,1)S(1)}, u32[]{:S(2)}, u32[]{:S(2)}) collective-permute-start(bf16[6,2,48,256]{3,2,1,0:T(8,128)(2,1)S(1)} %bitcast_dynamic-update-slice_fusion.4), channel_id=1, source_target_pairs={{0,576},{16,592},{32,608},{48,624},{64,640},{80,656},{96,672},{112... | collective-permute-start | bytes 884744 | tf_op jit(solution)/shard_map/ppermute | solution.py:54
  228.8 12.7 %collective-permute-start.31 = (f32[768]{0:T(1024)S(1)}, f32[768]{0:T(1024)S(1)}, u32[]{:S(2)}, u32[]{:S(2)}) collective-permute-start(f32[768]{0:T(1024)S(1)} %get-tuple-element.6), channel_id=1, source_target_pairs={{0,8},{1,9},{2,10},{3,11},{4,12},{5,13},{6,14},{7,15},{8,0},{9,1},... | collective-permute-start | bytes 9224 | tf_op jit(solution)/shard_map/ppermute | solution.py:66
  (14 other events, 277.1 us)

commit v3 on v1

v3 whole, which is shorter than its diff:
```python
import jax
import jax.numpy as jnp
from jax import lax
from jax.sharding import PartitionSpec as P

G = 32


def coord(axis, stride, size):
    return (lax.axis_index(axis) // stride) % size


def halve(x, dim, axis, stride):
    total = lax.axis_size(axis)
    k = coord(axis, stride, 2)
    pairs = [(i, i + (1 - 2 * ((i // stride) % 2)) * stride) for i in range(total)]
    mine = lax.dynamic_index_in_dim(x, k, dim, keepdims=False)
    other = lax.dynamic_index_in_dim(x, 1 - k, dim, keepdims=False)
    return mine + lax.ppermute(other, axis, pairs)


def direct(x, dim, axis, stride, size):
    total = lax.axis_size(axis)
    k = coord(axis, stride, size)
    acc = lax.dynamic_index_in_dim(x, k, dim, keepdims=False)
    for j in range(1, size):
        pairs = []
        for i in range(total):
            m = (i // stride) % size
            pairs.append((i, i + ((m + j) % size - m) * stride))
        piece = lax.dynamic_index_in_dim(x, (k + j) % size, dim, keepdims=False)
        acc = acc + lax.ppermute(piece, axis, pairs)
    return acc


def gather_a2a(x, axis):
    n = lax.axis_size(axis)
    spread = jnp.broadcast_to(x[None], (n,) + x.shape)
    got = lax.all_to_all(spread, axis, 0, 0)
    return got.reshape((n * x.shape[0],) + x.shape[1:])


def body(features, cotangent, conv_weight, norm_gain, norm_bias, film_rows):
    rows = features.shape[1]
    cols = features.shape[2]
    width = features.shape[3]
    ndp = lax.axis_size("dp")
    ntile = lax.axis_size("tile")
    t = lax.axis_index("tile")
    full_weight = gather_a2a(conv_weight, "dp")
    raw = features[0]
    above = lax.ppermute(raw[rows - 1 :], "tile", [(i, i + 1) for i in range(ntile - 1)])
    below = lax.ppermute(raw[:1], "tile", [(i + 1, i) for i in range(ntile - 1)])
    values = raw.astype(jnp.float32)
    grouped = values.reshape(rows, cols, G, width // G)
    stats = jnp.concatenate([jnp.sum(grouped, axis=(0, 1, 3)), jnp.sum(grouped * grouped, axis=(0, 1, 3))])
    stats = jnp.sum(lax.all_to_all(jnp.broadcast_to(stats[None], (ntile,) + stats.shape), "tile", 0, 0), axis=0)
    sums, squares = stats[:G], stats[G:]
    count = rows * ntile * cols * (width // G)
    mean = sums / count
    var = squares / count - mean * mean
    mean_c = jnp.repeat(mean, width // G)
    inv_c = jnp.repeat(1.0 / jnp.sqrt(var + 1e-05), width // G)
    film = film_rows[0]
    ext = jnp.concatenate([above, raw, below], axis=0).astype(jnp.float32)
    normed = (ext - mean_c) * inv_c * norm_gain + norm_bias
    act = jax.nn.silu(normed * (1.0 + film[:width]) + film[width:]).astype(jnp.bfloat16)
    row_id = lax.broadcasted_iota(jnp.int32, (rows + 2, 1, 1), 0)
    outside = ((row_id == 0) & (t == 0)) | ((row_id == rows + 1) & (t == ntile - 1))
    act = jnp.where(outside, jnp.zeros_like(act), act)
    padded = jnp.pad(act, ((0, 0), (1, 1), (0, 0)))
    taps = [padded[i : i + rows, j : j + cols, :] for i in range(3) for j in range(3)]
    patches = jnp.concatenate(taps, axis=-1).reshape(rows * cols, 9 * width)
    positions = ndp * rows * ntile * cols
    cot_rows = cotangent[0].reshape(rows * cols, width)
    part_t = lax.dot_general(
        cot_rows, patches, (((0,), (0,)), ((), ())), preferred_element_type=jnp.float32
    )
    per = part_t.shape[1] // ndp
    q = width // ntile
    g = part_t.T.reshape(2, 2, 3, 2, 2, per, width)
    g = halve(g, 4, "dp", 1)
    g = halve(g, 0, "dp", 24)
    g = halve(g, 0, "dp", 12)
    g = direct(g, 0, "dp", 4, 3)
    g = halve(g, 0, "dp", 2)
    span = width
    for stride in (8, 4, 2, 1):
        span //= 2
        g = halve(g.reshape(per, 2, span), 1, "tile", stride)
    grad_weight = g / jnp.sqrt(jnp.float32(positions))
    conv = jnp.dot(patches, full_weight, preferred_element_type=jnp.float32)
    output = (conv.reshape(rows, cols, width) + values)[None]
    return (output, grad_weight)


def solution(mesh):
    in_specs = (
        P("dp", "tile", None, None),
        P("dp", "tile", None, None),
        P("dp", None),
        P(),
        P(),
        P("dp", None),
    )
    out_specs = (P("dp", "tile", None, None), P("dp", "tile"))
    return jax.shard_map(body, mesh=mesh, in_specs=in_specs, out_specs=out_specs, check_vma=False)
```

time: 249 us -> 194 us (0.78)
  the two profiles are of different devices: /device:TPU:1 before, /device:TPU:6 now
where the time goes in v3:
time: 194 us; the launch traced here: 193 us
  waiting for transfers between devices  75.4 us (39%)
  starting transfers between devices  67.6 us (35%)
  local copies, waits for them, and re-layouts  25.7 us (13%)
  matrix products  13.1 us (7%)
  other arithmetic  9.55 us (5%)
    ppermute x8, waiting for transfers between devices, halve(): return mine + lax.ppermute(other, axis, pairs)  43 us
    ppermute x8, starting transfers between devices, halve(): return mine + lax.ppermute(other, axis, pairs)  25.1 us
    all_to_all x1, starting transfers between devices, body(): lax.all_to_all(jnp.broadcast_to(stats[None], (ntile,) + stats.shape), 'ti...  19.9 us
    ppermute x2, waiting for transfers between devices, direct(): acc = acc + lax.ppermute(piece, axis, pairs)  18.3 us
    all_to_all x1, waiting for transfers between devices, body(): lax.all_to_all(jnp.broadcast_to(stats[None], (ntile,) + stats.shape), 'ti...  14 us
    dot_general x1, local copies, waits for them, and re-layouts, body(): lax.dot_general(cot_rows, patches, (((0,), (0,)), ((), ())), preferred_el...  12.7 us
    all_to_all x1, starting transfers between devices, gather_a2a(): got = lax.all_to_all(spread, axis, 0, 0)  9.65 us
    unnamed x20, local copies, waits for them, and re-layouts  7.97 us
  transfers between devices with their start and end apart: 14, of which 11 were waited for; matrix products, arithmetic and copies ran while one was open for 4% of the time, Pallas kernels for 0%

profile of v3, /device:TPU:6, one launch (start us, length us, event | category | flops | bytes accessed | tf_op | source)
XLA Modules:
  0.0 192.7 jit_solution(8933585093446722566)
XLA Ops:
  2.9 4.5 %collective-permute-start = (bf16[1,128,256]{2,1,0:T(8,128)(2,1)S(1)}, bf16[1,128,256]{2,1,0:T(8,128)(2,1)S(1)}, u32[]{:S(2)}, u32[]{:S(2)}) collective-permute-start(bf16[1,128,256]{2,1,0:T(8,128)(2,1)S(1)} %get-tuple-element.4), channel_id=1, source_target_pairs={{0,1},{1,2},{2,3},{3,4},{4,5},{5,6},{6,7},{7,8},{8,9},{9,10},{10,1... | collective-permute-start | bytes 196616 | tf_op jit(solution)/shard_map/ppermute | solution.py:52
  10.1 19.9 %all-to-all-start = ((f32[16,1,64]{2,1,0:T(1,128)}), f32[16,1,64]{2,1,0:T(1,128)S(1)}, u32[]{:S(2)}, u32[]{:S(2)}) async-start(f32[16,1,64]{2,1,0:T(1,128)} %broadcast_in_dim.38), calls=%async_computation | async-start | bytes 16384 | tf_op jit(solution)/shard_map/all_to_all | solution.py:57
  30.7 14.0 %all-to-all-done = f32[16,1,64]{2,1,0:T(1,128)S(1)} async-done(((f32[16,1,64]{2,1,0:T(1,128)}), f32[16,1,64]{2,1,0:T(1,128)S(1)}, u32[]{:S(2)}, u32[]{:S(2)}) %all-to-all-start) | async-done | bytes 4128 | tf_op jit(solution)/shard_map/all_to_all | solution.py:57
  50.0 3.7 %copy-done.1 = bf16[16,128,2304]{2,1,0:T(8,128)(2,1)} copy-done((bf16[16,128,2304]{2,1,0:T(8,128)(2,1)}, bf16[16,128,2304]{2,1,0:T(8,128)(2,1)S(1)}, u32[]{:S(2)}) %copy-start.1) | copy-done | bytes 9437208
  53.7 12.7 %copy.19 = bf16[2304,2048]{1,0:T(8,128)(2,1)} copy(bf16[2304,2048]{0,1:T(8,128)(2,1)} %bitcast.69) | data formatting | bytes 18874368 | tf_op jit(solution)/shard_map/dot_general | solution.py:76
  66.4 5.2 %fusion.4 = f32[2,2,3,2,2,48,256]{6,5,4,3,2,1,0:T(8,128)S(1)} fusion(bf16[2,2,3,2,2,48,2048]{6,5,4,3,2,1,0:T(8,128)(2,1)} %bitcast.70, bf16[2048,256,1,1,1,1,1]{1,0,6,5,4,3,2:T(8,128)(2,1)S(1)} %bitcast.68), kind=kOutput, calls=%fused_computation.44 | convolution fusion | flops 2415919104 | bytes 12845056 | tf_op jit(solution)/shard_map/dot_general | solution.py:76
  75.1 2.9 %collective-permute-done.2 = f32[2,2,3,2,48,256]{5,4,3,2,1,0:T(8,128)} collective-permute-done((f32[2,2,3,2,48,256]{5,4,3,2,1,0:T(8,128)S(1)}, f32[2,2,3,2,48,256]{5,4,3,2,1,0:T(8,128)}, u32[]{:S(2)}, u32[]{:S(2)}) %collective-permute-start.2) | collective-permute-done | bytes 1179680 | tf_op jit(solution)/shard_map/ppermute | solution.py:19
  80.7 3.3 %collective-permute-start.3 = (f32[2,3,2,48,256]{4,3,2,1,0:T(8,128)}, f32[2,3,2,48,256]{4,3,2,1,0:T(8,128)}, u32[]{:S(2)}, u32[]{:S(2)}) collective-permute-start(f32[2,3,2,48,256]{4,3,2,1,0:T(8,128)} %dynamic-slice_bitcast_fusion.1), channel_id=1, source_target_pairs={{0,384},{16,400},{32,416},{48,432},{64,448},{80,464},{96,480},{112... | collective-permute-start | bytes 1769480 | tf_op jit(solution)/shard_map/ppermute | solution.py:19
  85.1 9.6 %all-to-all-start.1 = ((bf16[48,48,256]{2,1,0:T(8,128)(2,1)}), bf16[48,48,256]{2,1,0:T(8,128)(2,1)}, u32[]{:S(2)}, u32[]{:S(2)}) async-start(bf16[48,48,256]{2,1,0:T(8,128)(2,1)} %broadcast_in_dim.41), calls=%async_computation.1 | async-start | bytes 2359296 | tf_op jit(solution)/shard_map/all_to_all | solution.py:39
  94.8 8.3 %collective-permute-done.3 = f32[2,3,2,48,256]{4,3,2,1,0:T(8,128)} collective-permute-done((f32[2,3,2,48,256]{4,3,2,1,0:T(8,128)}, f32[2,3,2,48,256]{4,3,2,1,0:T(8,128)}, u32[]{:S(2)}, u32[]{:S(2)}) %collective-permute-start.3) | collective-permute-done | bytes 589856 | tf_op jit(solution)/shard_map/ppermute | solution.py:19
  105.1 3.4 %collective-permute-start.4 = (f32[3,2,48,256]{3,2,1,0:T(8,128)S(1)}, f32[3,2,48,256]{3,2,1,0:T(8,128)S(1)}, u32[]{:S(2)}, u32[]{:S(2)}) collective-permute-start(f32[3,2,48,256]{3,2,1,0:T(8,128)S(1)} %dynamic-slice_bitcast_fusion.2), channel_id=1, source_target_pairs={{0,192},{16,208},{32,224},{48,240},{64,256},{80,272},{96,288},{112... | collective-permute-start | bytes 884744 | tf_op jit(solution)/shard_map/ppermute | solution.py:19
  108.6 7.9 %collective-permute-done.4 = f32[3,2,48,256]{3,2,1,0:T(8,128)S(1)} collective-permute-done((f32[3,2,48,256]{3,2,1,0:T(8,128)S(1)}, f32[3,2,48,256]{3,2,1,0:T(8,128)S(1)}, u32[]{:S(2)}, u32[]{:S(2)}) %collective-permute-start.4) | collective-permute-done | bytes 294944 | tf_op jit(solution)/shard_map/ppermute | solution.py:19
  117.6 5.3 %collective-permute-start.6 = (f32[2,48,256]{2,1,0:T(8,128)S(1)}, f32[2,48,256]{2,1,0:T(8,128)S(1)}, u32[]{:S(2)}, u32[]{:S(2)}) collective-permute-start(f32[2,48,256]{2,1,0:T(8,128)S(1)} %get-tuple-element.7), channel_id=1, source_target_pairs={{0,128},{16,144},{32,160},{48,176},{64,0},{80,16},{96,32},{112,48}... | collective-permute-start | bytes 294920 | tf_op jit(solution)/shard_map/ppermute | solution.py:32
  124.8 13.2 %collective-permute-done.6 = f32[2,48,256]{2,1,0:T(8,128)S(1)} collective-permute-done((f32[2,48,256]{2,1,0:T(8,128)S(1)}, f32[2,48,256]{2,1,0:T(8,128)S(1)}, u32[]{:S(2)}, u32[]{:S(2)}) %collective-permute-start.6) | collective-permute-done | bytes 98336 | tf_op jit(solution)/shard_map/ppermute | solution.py:32
  138.0 5.1 %collective-permute-done.5 = f32[2,48,256]{2,1,0:T(8,128)S(1)} collective-permute-done((f32[2,48,256]{2,1,0:T(8,128)S(1)}, f32[2,48,256]{2,1,0:T(8,128)S(1)}, u32[]{:S(2)}, u32[]{:S(2)}) %collective-permute-start.5) | collective-permute-done | bytes 98336 | tf_op jit(solution)/shard_map/ppermute | solution.py:32
  143.2 4.6 %collective-permute-start.7 = (f32[48,256]{1,0:T(8,128)S(1)}, f32[48,256]{1,0:T(8,128)S(1)}, u32[]{:S(2)}, u32[]{:S(2)}) collective-permute-start(f32[48,256]{1,0:T(8,128)S(1)} %dynamic-slice_bitcast_fusion.5), channel_id=1, source_target_pairs={{0,32},{16,48},{32,0},{48,16},{64,96},{80,112},{96,64},{112,80},{1... | collective-permute-start | bytes 147464 | tf_op jit(solution)/shard_map/ppermute | solution.py:19
  150.0 4.3 %collective-permute-start.8 = (f32[48,128]{1,0:T(8,128)S(1)}, f32[48,128]{1,0:T(8,128)S(1)}, u32[]{:S(2)}, u32[]{:S(2)}) collective-permute-start(f32[48,128]{1,0:T(8,128)S(1)} %bitcast.79), channel_id=1, source_target_pairs={{0,8},{1,9},{2,10},{3,11},{4,12},{5,13},{6,14},{7,15},{8,0},{9,1},... | collective-permute-start | bytes 73736 | tf_op jit(solution)/shard_map/ppermute | solution.py:19
  154.3 7.7 %collective-permute-done.8 = f32[48,128]{1,0:T(8,128)S(1)} collective-permute-done((f32[48,128]{1,0:T(8,128)S(1)}, f32[48,128]{1,0:T(8,128)S(1)}, u32[]{:S(2)}, u32[]{:S(2)}) %collective-permute-start.8) | collective-permute-done | bytes 24608 | tf_op jit(solution)/shard_map/ppermute | solution.py:19
  162.2 2.5 %collective-permute-start.9 = (f32[48,64]{0,1:T(8,128)S(1)}, f32[48,64]{0,1:T(8,128)S(1)}, u32[]{:S(2)}, u32[]{:S(2)}) collective-permute-start(f32[48,64]{0,1:T(8,128)S(1)} %bitcast.77), channel_id=1, source_target_pairs={{0,4},{1,5},{2,6},{3,7},{4,0},{5,1},{6,2},{7,3},{8,12},{9,13},{10,... | collective-permute-start | bytes 36872 | tf_op jit(solution)/shard_map/ppermute | solution.py:19
  164.9 7.2 %collective-permute-done.9 = f32[48,64]{0,1:T(8,128)S(1)} collective-permute-done((f32[48,64]{0,1:T(8,128)S(1)}, f32[48,64]{0,1:T(8,128)S(1)}, u32[]{:S(2)}, u32[]{:S(2)}) %collective-permute-start.9) | collective-permute-done | bytes 12320 | tf_op jit(solution)/shard_map/ppermute | solution.py:19
  174.5 4.2 %collective-permute-done.10 = f32[48,32]{0,1:T(8,128)S(1)} collective-permute-done((f32[48,32]{0,1:T(8,128)S(1)}, f32[48,32]{0,1:T(8,128)S(1)}, u32[]{:S(2)}, u32[]{:S(2)}) %collective-permute-start.10) | collective-permute-done | bytes 6176 | tf_op jit(solution)/shard_map/ppermute | solution.py:19
  178.7 2.6 %collective-permute-start.11 = (f32[48,16]{0,1:T(8,128)S(1)}, f32[48,16]{0,1:T(8,128)S(1)}, u32[]{:S(2)}, u32[]{:S(2)}) collective-permute-start(f32[48,16]{0,1:T(8,128)S(1)} %dynamic-slice_bitcast_fusion.7), channel_id=1, source_target_pairs={{0,1},{1,0},{2,3},{3,2},{4,5},{5,4},{6,7},{7,6},{8,9},{9,8},{10,11... | collective-permute-start | bytes 9224 | tf_op jit(solution)/shard_map/ppermute | solution.py:19
  181.3 2.9 %collective-permute-done.11 = f32[48,16]{0,1:T(8,128)S(1)} collective-permute-done((f32[48,16]{0,1:T(8,128)S(1)}, f32[48,16]{0,1:T(8,128)S(1)}, u32[]{:S(2)}, u32[]{:S(2)}) %collective-permute-start.11) | collective-permute-done | bytes 3104 | tf_op jit(solution)/shard_map/ppermute | solution.py:19
  184.8 7.9 %add_bitcast_fusion = f32[1,16,128,256]{3,2,1,0:T(8,128)} fusion(bf16[16,128,2304]{2,1,0:T(8,128)(2,1)} %copy-done.1, bf16[2304,256,1]{1,0,2:T(8,128)(2,1)} %bitcast.7, bf16[1,16,128,256]{3,2,1,0:T(8,128)(2,1)S(1)} %copy-done.2), kind=kOutput, calls=%fused_computation.4 | convolution fusion | flops 2416967680 | bytes 13762560 | tf_op jit(solution)/shard_map/dot_general | solution.py:92
  (68 shorter events, 28.4 us)
Async XLA Ops:
  0.6 65.8 %copy-start = (bf16[1,16,128,256]{3,2,1,0:T(8,128)(2,1)S(1)}, bf16[1,16,128,256]{3,2,1,0:T(8,128)(2,1)}, u32[]{:S(2)}) copy-start(bf16[1,16,128,256]{3,2,1,0:T(8,128)(2,1)} %param.7) | copy-start | bytes 3145732
  1.6 43.5 %collective-permute-start.1 = (bf16[1,128,256]{2,1,0:T(8,128)(2,1)S(1)}, bf16[1,128,256]{2,1,0:T(8,128)(2,1)S(1)}, u32[]{:S(2)}, u32[]{:S(2)}) collective-permute-start(bf16[1,128,256]{2,1,0:T(8,128)(2,1)S(1)} %get-tuple-element.5), channel_id=1, source_target_pairs={{1,0},{2,1},{3,2},{4,3},{5,4},{6,5},{7,6},{8,7},{9,8},{10,9},{11,1... | collective-permute-start | bytes 196616 | tf_op jit(solution)/shard_map/ppermute | solution.py:53
  2.9 42.3 %collective-permute-start = (bf16[1,128,256]{2,1,0:T(8,128)(2,1)S(1)}, bf16[1,128,256]{2,1,0:T(8,128)(2,1)S(1)}, u32[]{:S(2)}, u32[]{:S(2)}) collective-permute-start(bf16[1,128,256]{2,1,0:T(8,128)(2,1)S(1)} %get-tuple-element.4), channel_id=1, source_target_pairs={{0,1},{1,2},{2,3},{3,4},{4,5},{5,6},{6,7},{7,8},{8,9},{9,10},{10,1... | collective-permute-start | bytes 196616 | tf_op jit(solution)/shard_map/ppermute | solution.py:52
  10.1 34.6 %all-to-all-start = ((f32[16,1,64]{2,1,0:T(1,128)}), f32[16,1,64]{2,1,0:T(1,128)S(1)}, u32[]{:S(2)}, u32[]{:S(2)}) async-start(f32[16,1,64]{2,1,0:T(1,128)} %broadcast_in_dim.38), calls=%async_computation | async-start | bytes 16384 | tf_op jit(solution)/shard_map/all_to_all | solution.py:57
  50.0 3.7 %copy-start.1 = (bf16[16,128,2304]{2,1,0:T(8,128)(2,1)}, bf16[16,128,2304]{2,1,0:T(8,128)(2,1)S(1)}, u32[]{:S(2)}) copy-start(bf16[16,128,2304]{2,1,0:T(8,128)(2,1)S(1)} %slice_dynamic-update-slice_fusion.3) | copy-start | bytes 28311556
  71.6 1.4 copy-start.3
  73.1 4.9 %collective-permute-start.2 = (f32[2,2,3,2,48,256]{5,4,3,2,1,0:T(8,128)S(1)}, f32[2,2,3,2,48,256]{5,4,3,2,1,0:T(8,128)}, u32[]{:S(2)}, u32[]{:S(2)}) collective-permute-start(f32[2,2,3,2,48,256]{5,4,3,2,1,0:T(8,128)S(1)} %dynamic-slice_bitcast_fusion), channel_id=1, source_target_pairs={{0,16},{16,0},{32,48},{48,32},{64,80},{80,64},{96,112},{112,96},{1... | collective-permute-start | bytes 3538952 | tf_op jit(solution)/shard_map/ppermute | solution.py:19
  75.1 8.9 %copy-start.5 = (bf16[48,256]{1,0:T(8,128)(2,1)S(1)}, bf16[48,256]{1,0:T(8,128)(2,1)}, u32[]{:S(2)}) copy-start(bf16[48,256]{1,0:T(8,128)(2,1)} %param.8) | copy-start | bytes 73732
  80.7 22.4 %collective-permute-start.3 = (f32[2,3,2,48,256]{4,3,2,1,0:T(8,128)}, f32[2,3,2,48,256]{4,3,2,1,0:T(8,128)}, u32[]{:S(2)}, u32[]{:S(2)}) collective-permute-start(f32[2,3,2,48,256]{4,3,2,1,0:T(8,128)} %dynamic-slice_bitcast_fusion.1), channel_id=1, source_target_pairs={{0,384},{16,400},{32,416},{48,432},{64,448},{80,464},{96,480},{112... | collective-permute-start | bytes 1769480 | tf_op jit(solution)/shard_map/ppermute | solution.py:19
  85.1 99.7 %all-to-all-start.1 = ((bf16[48,48,256]{2,1,0:T(8,128)(2,1)}), bf16[48,48,256]{2,1,0:T(8,128)(2,1)}, u32[]{:S(2)}, u32[]{:S(2)}) async-start(bf16[48,48,256]{2,1,0:T(8,128)(2,1)} %broadcast_in_dim.41), calls=%async_computation.1 | async-start | bytes 2359296 | tf_op jit(solution)/shard_map/all_to_all | solution.py:39
  94.8 90.0 %copy-start.2 = (bf16[1,16,128,256]{3,2,1,0:T(8,128)(2,1)S(1)}, bf16[1,16,128,256]{3,2,1,0:T(8,128)(2,1)}, u32[]{:S(2)}) copy-start(bf16[1,16,128,256]{3,2,1,0:T(8,128)(2,1)} %param.6) | copy-start | bytes 3145732
  104.2 0.8 copy-start.4
  105.1 11.4 %collective-permute-start.4 = (f32[3,2,48,256]{3,2,1,0:T(8,128)S(1)}, f32[3,2,48,256]{3,2,1,0:T(8,128)S(1)}, u32[]{:S(2)}, u32[]{:S(2)}) collective-permute-start(f32[3,2,48,256]{3,2,1,0:T(8,128)S(1)} %dynamic-slice_bitcast_fusion.2), channel_id=1, source_target_pairs={{0,192},{16,208},{32,224},{48,240},{64,256},{80,272},{96,288},{112... | collective-permute-start | bytes 884744 | tf_op jit(solution)/shard_map/ppermute | solution.py:19
  117.6 20.5 %collective-permute-start.6 = (f32[2,48,256]{2,1,0:T(8,128)S(1)}, f32[2,48,256]{2,1,0:T(8,128)S(1)}, u32[]{:S(2)}, u32[]{:S(2)}) collective-permute-start(f32[2,48,256]{2,1,0:T(8,128)S(1)} %get-tuple-element.7), channel_id=1, source_target_pairs={{0,128},{16,144},{32,160},{48,176},{64,0},{80,16},{96,32},{112,48}... | collective-permute-start | bytes 294920 | tf_op jit(solution)/shard_map/ppermute | solution.py:32
  122.8 20.3 %collective-permute-start.5 = (f32[2,48,256]{2,1,0:T(8,128)S(1)}, f32[2,48,256]{2,1,0:T(8,128)S(1)}, u32[]{:S(2)}, u32[]{:S(2)}) collective-permute-start(f32[2,48,256]{2,1,0:T(8,128)S(1)} %get-tuple-element.6), channel_id=1, source_target_pairs={{0,64},{16,80},{32,96},{48,112},{64,128},{80,144},{96,160},{112,17... | collective-permute-start | bytes 294920 | tf_op jit(solution)/shard_map/ppermute | solution.py:32
  143.2 6.7 %collective-permute-start.7 = (f32[48,256]{1,0:T(8,128)S(1)}, f32[48,256]{1,0:T(8,128)S(1)}, u32[]{:S(2)}, u32[]{:S(2)}) collective-permute-start(f32[48,256]{1,0:T(8,128)S(1)} %dynamic-slice_bitcast_fusion.5), channel_id=1, source_target_pairs={{0,32},{16,48},{32,0},{48,16},{64,96},{80,112},{96,64},{112,80},{1... | collective-permute-start | bytes 147464 | tf_op jit(solution)/shard_map/ppermute | solution.py:19
  150.0 12.0 %collective-permute-start.8 = (f32[48,128]{1,0:T(8,128)S(1)}, f32[48,128]{1,0:T(8,128)S(1)}, u32[]{:S(2)}, u32[]{:S(2)}) collective-permute-start(f32[48,128]{1,0:T(8,128)S(1)} %bitcast.79), channel_id=1, source_target_pairs={{0,8},{1,9},{2,10},{3,11},{4,12},{5,13},{6,14},{7,15},{8,0},{9,1},... | collective-permute-start | bytes 73736 | tf_op jit(solution)/shard_map/ppermute | solution.py:19
  162.2 9.8 %collective-permute-start.9 = (f32[48,64]{0,1:T(8,128)S(1)}, f32[48,64]{0,1:T(8,128)S(1)}, u32[]{:S(2)}, u32[]{:S(2)}) collective-permute-start(f32[48,64]{0,1:T(8,128)S(1)} %bitcast.77), channel_id=1, source_target_pairs={{0,4},{1,5},{2,6},{3,7},{4,0},{5,1},{6,2},{7,3},{8,12},{9,13},{10,... | collective-permute-start | bytes 36872 | tf_op jit(solution)/shard_map/ppermute | solution.py:19
  172.1 6.6 %collective-permute-start.10 = (f32[48,32]{0,1:T(8,128)S(1)}, f32[48,32]{0,1:T(8,128)S(1)}, u32[]{:S(2)}, u32[]{:S(2)}) collective-permute-start(f32[48,32]{0,1:T(8,128)S(1)} %dynamic-slice_bitcast_fusion.6), channel_id=1, source_target_pairs={{0,2},{1,3},{2,0},{3,1},{4,6},{5,7},{6,4},{7,5},{8,10},{9,11},{10,... | collective-permute-start | bytes 18440 | tf_op jit(solution)/shard_map/ppermute | solution.py:19
  178.7 5.5 %collective-permute-start.11 = (f32[48,16]{0,1:T(8,128)S(1)}, f32[48,16]{0,1:T(8,128)S(1)}, u32[]{:S(2)}, u32[]{:S(2)}) collective-permute-start(f32[48,16]{0,1:T(8,128)S(1)} %dynamic-slice_bitcast_fusion.7), channel_id=1, source_target_pairs={{0,1},{1,0},{2,3},{3,2},{4,5},{5,4},{6,7},{7,6},{8,9},{9,8},{10,11... | collective-permute-start | bytes 9224 | tf_op jit(solution)/shard_map/ppermute | solution.py:19

commit v4 on v3

--- a/solution.py
+++ b/solution.py
@@ -47,7 +47,7 @@
     ndp = lax.axis_size("dp")
     ntile = lax.axis_size("tile")
     t = lax.axis_index("tile")
-    full_weight = gather_a2a(conv_weight, "dp")
+    full_weight = lax.all_gather(conv_weight, "dp", axis=0, tiled=True)
     raw = features[0]
     above = lax.ppermute(raw[rows - 1 :], "tile", [(i, i + 1) for i in range(ntile - 1)])
     below = lax.ppermute(raw[:1], "tile", [(i + 1, i) for i in range(ntile - 1)])
@@ -73,8 +73,8 @@
     patches = jnp.concatenate(taps, axis=-1).reshape(rows * cols, 9 * width)
     positions = ndp * rows * ntile * cols
     cot_rows = cotangent[0].reshape(rows * cols, width)
-    part_t = lax.dot_general(
-        cot_rows, patches, (((0,), (0,)), ((), ())), preferred_element_type=jnp.float32
+    part_t = lax.optimization_barrier(
+        lax.dot_general(cot_rows, patches, (((0,), (0,)), ((), ())), preferred_element_type=jnp.float32)
     )
     per = part_t.shape[1] // ndp
     q = width // ntile

time: 194 us -> 182 us (0.938)
  the two profiles are of different devices: /device:TPU:6 before, /device:TPU:1 now
where the time goes in v4:
time: 182 us; the launch traced here: 181 us
  waiting for transfers between devices  82 us (45%)
  starting transfers between devices  55.3 us (30%)
  between operations  14.7 us (8%)
  matrix products  10.7 us (6%)
  other arithmetic  9.55 us (5%)
  local copies, waits for them, and re-layouts  8.94 us (5%)
    ppermute x8, waiting for transfers between devices, halve(): return mine + lax.ppermute(other, axis, pairs)  46 us
    ppermute x8, starting transfers between devices, halve(): return mine + lax.ppermute(other, axis, pairs)  22.1 us
    all_to_all x1, starting transfers between devices, body(): lax.all_to_all(jnp.broadcast_to(stats[None], (ntile,) + stats.shape), 'ti...  19.8 us
    all_gather x1, waiting for transfers between devices, body(): full_weight = lax.all_gather(conv_weight, 'dp', axis=0, tiled=True)  14.8 us
    all_to_all x1, waiting for transfers between devices, body(): lax.all_to_all(jnp.broadcast_to(stats[None], (ntile,) + stats.shape), 'ti...  12.8 us
    ppermute x2, waiting for transfers between devices, direct(): acc = acc + lax.ppermute(piece, axis, pairs)  8.47 us
    dot_general x1, matrix products, body(): conv = jnp.dot(patches, full_weight, preferred_element_type=jnp.float32)  7.92 us
    ppermute x2, starting transfers between devices, direct(): acc = acc + lax.ppermute(piece, axis, pairs)  7.48 us
  transfers between devices with their start and end apart: 14, of which 10 were waited for; matrix products, arithmetic and copies ran while one was open for 8% of the time, Pallas kernels for 0%

profile of v4, /device:TPU:1, one launch (start us, length us, event | category | flops | bytes accessed | tf_op | source)
XLA Modules:
  0.0 181.3 jit_solution(8273145363305767003)
XLA Ops:
  9.5 4.7 %collective-permute-start = (bf16[1,128,256]{2,1,0:T(8,128)(2,1)S(1)}, bf16[1,128,256]{2,1,0:T(8,128)(2,1)S(1)}, u32[]{:S(2)}, u32[]{:S(2)}) collective-permute-start(bf16[1,128,256]{2,1,0:T(8,128)(2,1)S(1)} %get-tuple-element.4), channel_id=1, source_target_pairs={{0,1},{1,2},{2,3},{3,4},{4,5},{5,6},{6,7},{7,8},{8,9},{9,10},{10,1... | collective-permute-start | bytes 196616 | tf_op jit(solution)/shard_map/ppermute | solution.py:52
  16.8 19.8 %all-to-all-start = ((f32[16,1,64]{2,1,0:T(1,128)}), f32[16,1,64]{2,1,0:T(1,128)S(1)}, u32[]{:S(2)}, u32[]{:S(2)}) async-start(f32[16,1,64]{2,1,0:T(1,128)} %broadcast_in_dim.32), calls=%async_computation | async-start | bytes 16384 | tf_op jit(solution)/shard_map/all_to_all | solution.py:57
  37.3 12.8 %all-to-all-done = f32[16,1,64]{2,1,0:T(1,128)S(1)} async-done(((f32[16,1,64]{2,1,0:T(1,128)}), f32[16,1,64]{2,1,0:T(1,128)S(1)}, u32[]{:S(2)}, u32[]{:S(2)}) %all-to-all-start) | async-done | bytes 4128 | tf_op jit(solution)/shard_map/all_to_all | solution.py:57
  50.5 2.3 %fusion.1 = bf16[18,128,256]{2,1,0:T(8,128)(2,1)S(1)} fusion(bf16[1,128,256]{2,1,0:T(8,128)(2,1)S(1)} %collective-permute-done.1, bf16[16,128,256]{2,1,0:T(8,128)(2,1)} %bitcast.65, bf16[1,128,256]{2,1,0:T(8,128)(2,1)S(1)} %collective-permute-done, f32[256]{0:T(256)S(1)} %bitcast.79, f32[256]{0:T(256)S(1)} %bitcast.78, f32[256]{0:T(256)} %param.10, ...), kind=kLoop, calls=%fused_computation.6 | loop fusion | flops 8847360 | bytes 2365458 | tf_op jit(solution)/shard_map/jit(_where)/select_n | solution.py:70
  55.4 2.8 %convolution_bitcast_fusion = f32[256,2304]{0,1:T(8,128)S(1)} fusion(bf16[2048,2304]{1,0:T(8,128)(2,1)S(1)} %bitcast.70, bf16[2048,256]{1,0:T(8,128)(2,1)S(1)} %bitcast.64), kind=kOutput, calls=%fused_computation | convolution fusion | flops 2415919104 | bytes 12845056 | tf_op jit(solution)/shard_map/dot_general | solution.py:77
  60.5 4.6 %collective-permute-start.2 = (f32[2,2,3,2,48,256]{5,4,3,2,1,0:T(8,128)S(1)}, f32[2,2,3,2,48,256]{5,4,3,2,1,0:T(8,128)}, u32[]{:S(2)}, u32[]{:S(2)}) collective-permute-start(f32[2,2,3,2,48,256]{5,4,3,2,1,0:T(8,128)S(1)} %dynamic-slice_bitcast_fusion), channel_id=1, source_target_pairs={{0,16},{16,0},{32,48},{48,32},{64,80},{80,64},{96,112},{112,96},{1... | collective-permute-start | bytes 3538952 | tf_op jit(solution)/shard_map/ppermute | solution.py:19
  65.2 2.5 %collective-permute-done.2 = f32[2,2,3,2,48,256]{5,4,3,2,1,0:T(8,128)} collective-permute-done((f32[2,2,3,2,48,256]{5,4,3,2,1,0:T(8,128)S(1)}, f32[2,2,3,2,48,256]{5,4,3,2,1,0:T(8,128)}, u32[]{:S(2)}, u32[]{:S(2)}) %collective-permute-start.2) | collective-permute-done | bytes 1179680 | tf_op jit(solution)/shard_map/ppermute | solution.py:19
  70.4 4.6 %collective-permute-start.3 = (f32[2,3,2,48,256]{4,3,2,1,0:T(8,128)}, f32[2,3,2,48,256]{4,3,2,1,0:T(8,128)}, u32[]{:S(2)}, u32[]{:S(2)}) collective-permute-start(f32[2,3,2,48,256]{4,3,2,1,0:T(8,128)} %dynamic-slice_bitcast_fusion.1), channel_id=1, source_target_pairs={{0,384},{16,400},{32,416},{48,432},{64,448},{80,464},{96,480},{112... | collective-permute-start | bytes 1769480 | tf_op jit(solution)/shard_map/ppermute | solution.py:19
  75.1 13.7 %collective-permute-done.3 = f32[2,3,2,48,256]{4,3,2,1,0:T(8,128)} collective-permute-done((f32[2,3,2,48,256]{4,3,2,1,0:T(8,128)}, f32[2,3,2,48,256]{4,3,2,1,0:T(8,128)}, u32[]{:S(2)}, u32[]{:S(2)}) %collective-permute-start.3) | collective-permute-done | bytes 589856 | tf_op jit(solution)/shard_map/ppermute | solution.py:19
  90.8 3.1 %collective-permute-start.4 = (f32[3,2,48,256]{3,2,1,0:T(8,128)S(1)}, f32[3,2,48,256]{3,2,1,0:T(8,128)S(1)}, u32[]{:S(2)}, u32[]{:S(2)}) collective-permute-start(f32[3,2,48,256]{3,2,1,0:T(8,128)S(1)} %dynamic-slice_bitcast_fusion.2), channel_id=1, source_target_pairs={{0,192},{16,208},{32,224},{48,240},{64,256},{80,272},{96,288},{112... | collective-permute-start | bytes 884744 | tf_op jit(solution)/shard_map/ppermute | solution.py:19
  94.0 6.6 %collective-permute-done.4 = f32[3,2,48,256]{3,2,1,0:T(8,128)S(1)} collective-permute-done((f32[3,2,48,256]{3,2,1,0:T(8,128)S(1)}, f32[3,2,48,256]{3,2,1,0:T(8,128)S(1)}, u32[]{:S(2)}, u32[]{:S(2)}) %collective-permute-start.4) | collective-permute-done | bytes 294944 | tf_op jit(solution)/shard_map/ppermute | solution.py:19
  101.7 5.6 %collective-permute-start.6 = (f32[2,48,256]{2,1,0:T(8,128)S(1)}, f32[2,48,256]{2,1,0:T(8,128)S(1)}, u32[]{:S(2)}, u32[]{:S(2)}) collective-permute-start(f32[2,48,256]{2,1,0:T(8,128)S(1)} %get-tuple-element.7), channel_id=1, source_target_pairs={{0,128},{16,144},{32,160},{48,176},{64,0},{80,16},{96,32},{112,48}... | collective-permute-start | bytes 294920 | tf_op jit(solution)/shard_map/ppermute | solution.py:32
  107.3 1.9 %collective-permute-start.5 = (f32[2,48,256]{2,1,0:T(8,128)S(1)}, f32[2,48,256]{2,1,0:T(8,128)S(1)}, u32[]{:S(2)}, u32[]{:S(2)}) collective-permute-start(f32[2,48,256]{2,1,0:T(8,128)S(1)} %get-tuple-element.6), channel_id=1, source_target_pairs={{0,64},{16,80},{32,96},{48,112},{64,128},{80,144},{96,160},{112,17... | collective-permute-start | bytes 294920 | tf_op jit(solution)/shard_map/ppermute | solution.py:32
  109.3 8.5 %collective-permute-done.5 = f32[2,48,256]{2,1,0:T(8,128)S(1)} collective-permute-done((f32[2,48,256]{2,1,0:T(8,128)S(1)}, f32[2,48,256]{2,1,0:T(8,128)S(1)}, u32[]{:S(2)}, u32[]{:S(2)}) %collective-permute-start.5) | collective-permute-done | bytes 98336 | tf_op jit(solution)/shard_map/ppermute | solution.py:32
  117.8 1.9 %collective-permute-start.7 = (f32[48,256]{1,0:T(8,128)S(1)}, f32[48,256]{1,0:T(8,128)S(1)}, u32[]{:S(2)}, u32[]{:S(2)}) collective-permute-start(f32[48,256]{1,0:T(8,128)S(1)} %dynamic-slice_bitcast_fusion.5), channel_id=1, source_target_pairs={{0,32},{16,48},{32,0},{48,16},{64,96},{80,112},{96,64},{112,80},{1... | collective-permute-start | bytes 147464 | tf_op jit(solution)/shard_map/ppermute | solution.py:19
  119.7 3.3 %collective-permute-done.7 = f32[48,256]{1,0:T(8,128)S(1)} collective-permute-done((f32[48,256]{1,0:T(8,128)S(1)}, f32[48,256]{1,0:T(8,128)S(1)}, u32[]{:S(2)}, u32[]{:S(2)}) %collective-permute-start.7) | collective-permute-done | bytes 49184 | tf_op jit(solution)/shard_map/ppermute | solution.py:19
  123.1 1.9 %collective-permute-start.8 = (f32[48,128]{1,0:T(8,128)S(1)}, f32[48,128]{1,0:T(8,128)S(1)}, u32[]{:S(2)}, u32[]{:S(2)}) collective-permute-start(f32[48,128]{1,0:T(8,128)S(1)} %bitcast.76), channel_id=1, source_target_pairs={{0,8},{1,9},{2,10},{3,11},{4,12},{5,13},{6,14},{7,15},{8,0},{9,1},... | collective-permute-start | bytes 73736 | tf_op jit(solution)/shard_map/ppermute | solution.py:19
  125.1 9.6 %collective-permute-done.8 = f32[48,128]{1,0:T(8,128)S(1)} collective-permute-done((f32[48,128]{1,0:T(8,128)S(1)}, f32[48,128]{1,0:T(8,128)S(1)}, u32[]{:S(2)}, u32[]{:S(2)}) %collective-permute-start.8) | collective-permute-done | bytes 24608 | tf_op jit(solution)/shard_map/ppermute | solution.py:19
  134.8 1.9 %collective-permute-start.9 = (f32[48,64]{1,0:T(8,128)S(1)}, f32[48,64]{1,0:T(8,128)S(1)}, u32[]{:S(2)}, u32[]{:S(2)}) collective-permute-start(f32[48,64]{1,0:T(8,128)S(1)} %bitcast.77), channel_id=1, source_target_pairs={{0,4},{1,5},{2,6},{3,7},{4,0},{5,1},{6,2},{7,3},{8,12},{9,13},{10,... | collective-permute-start | bytes 36872 | tf_op jit(solution)/shard_map/ppermute | solution.py:19
  136.8 6.5 %collective-permute-done.9 = f32[48,64]{1,0:T(8,128)S(1)} collective-permute-done((f32[48,64]{1,0:T(8,128)S(1)}, f32[48,64]{1,0:T(8,128)S(1)}, u32[]{:S(2)}, u32[]{:S(2)}) %collective-permute-start.9) | collective-permute-done | bytes 12320 | tf_op jit(solution)/shard_map/ppermute | solution.py:19
  145.3 3.7 %collective-permute-done.10 = f32[48,32]{0,1:T(8,128)S(1)} collective-permute-done((f32[48,32]{0,1:T(8,128)S(1)}, f32[48,32]{0,1:T(8,128)S(1)}, u32[]{:S(2)}, u32[]{:S(2)}) %collective-permute-start.10) | collective-permute-done | bytes 6176 | tf_op jit(solution)/shard_map/ppermute | solution.py:19
  149.1 2.1 %collective-permute-start.11 = (f32[48,16]{0,1:T(8,128)S(1)}, f32[48,16]{0,1:T(8,128)S(1)}, u32[]{:S(2)}, u32[]{:S(2)}) collective-permute-start(f32[48,16]{0,1:T(8,128)S(1)} %dynamic-slice_bitcast_fusion.7), channel_id=1, source_target_pairs={{0,1},{1,0},{2,3},{3,2},{4,5},{5,4},{6,7},{7,6},{8,9},{9,8},{10,11... | collective-permute-start | bytes 9224 | tf_op jit(solution)/shard_map/ppermute | solution.py:19
  151.2 14.8 %all-gather.2.cloned.1.call-done = bf16[2304,256]{1,0:T(8,128)(2,1)} async-done(((bf16[48,256]{1,0:T(8,128)(2,1)}), bf16[2304,256]{1,0:T(8,128)(2,1)}) %all-gather.2.cloned.1.call-update) | async-done | bytes 1179664 | tf_op jit(solution)/shard_map/all_gather | solution.py:50
  165.9 7.9 %add_bitcast_fusion = f32[1,16,128,256]{3,2,1,0:T(8,128)} fusion(bf16[16,128,2304]{2,1,0:T(8,128)(2,1)} %copy-done.4, bf16[2304,256]{1,0:T(8,128)(2,1)} %all-gather.2.cloned.1.call-done, bf16[1,16,128,256]{3,2,1,0:T(8,128)(2,1)S(1)} %copy-done.1), kind=kOutput, calls=%fused_computation.5 | convolution fusion | flops 2416967680 | bytes 13762560 | tf_op jit(solution)/shard_map/dot_general | solution.py:92
  (64 shorter events, 19.5 us)
Async XLA Ops:
  7.2 48.2 %copy-start = (bf16[1,16,128,256]{3,2,1,0:T(8,128)(2,1)S(1)}, bf16[1,16,128,256]{3,2,1,0:T(8,128)(2,1)}, u32[]{:S(2)}) copy-start(bf16[1,16,128,256]{3,2,1,0:T(8,128)(2,1)} %param.7) | copy-start | bytes 3145732
  8.2 42.4 %collective-permute-start.1 = (bf16[1,128,256]{2,1,0:T(8,128)(2,1)S(1)}, bf16[1,128,256]{2,1,0:T(8,128)(2,1)S(1)}, u32[]{:S(2)}, u32[]{:S(2)}) collective-permute-start(bf16[1,128,256]{2,1,0:T(8,128)(2,1)S(1)} %get-tuple-element.5), channel_id=1, source_target_pairs={{1,0},{2,1},{3,2},{4,3},{5,4},{6,5},{7,6},{8,7},{9,8},{10,9},{11,1... | collective-permute-start | bytes 196616 | tf_op jit(solution)/shard_map/ppermute | solution.py:53
  9.5 41.1 %collective-permute-start = (bf16[1,128,256]{2,1,0:T(8,128)(2,1)S(1)}, bf16[1,128,256]{2,1,0:T(8,128)(2,1)S(1)}, u32[]{:S(2)}, u32[]{:S(2)}) collective-permute-start(bf16[1,128,256]{2,1,0:T(8,128)(2,1)S(1)} %get-tuple-element.4), channel_id=1, source_target_pairs={{0,1},{1,2},{2,3},{3,4},{4,5},{5,6},{6,7},{7,8},{8,9},{9,10},{10,1... | collective-permute-start | bytes 196616 | tf_op jit(solution)/shard_map/ppermute | solution.py:52
  16.8 33.3 %all-to-all-start = ((f32[16,1,64]{2,1,0:T(1,128)}), f32[16,1,64]{2,1,0:T(1,128)S(1)}, u32[]{:S(2)}, u32[]{:S(2)}) async-start(f32[16,1,64]{2,1,0:T(1,128)} %broadcast_in_dim.32), calls=%async_computation | async-start | bytes 16384 | tf_op jit(solution)/shard_map/all_to_all | solution.py:57
  36.5 129.4 %all-gather.2.cloned.1.call-start = ((), (), s32[]{:S(2)}) async-start(), calls=%async_computation.1 | async-start | bytes 1204224 | tf_op jit(solution)/shard_map/all_gather | solution.py:50
  55.4 3.7 %copy-start.4 = (bf16[16,128,2304]{2,1,0:T(8,128)(2,1)}, bf16[16,128,2304]{2,1,0:T(8,128)(2,1)S(1)}, u32[]{:S(2)}) copy-start(bf16[16,128,2304]{2,1,0:T(8,128)(2,1)S(1)} %slice_dynamic-update-slice_fusion.3) | copy-start | bytes 28311556
  59.0 1.4 copy-start.2
  60.5 7.2 %collective-permute-start.2 = (f32[2,2,3,2,48,256]{5,4,3,2,1,0:T(8,128)S(1)}, f32[2,2,3,2,48,256]{5,4,3,2,1,0:T(8,128)}, u32[]{:S(2)}, u32[]{:S(2)}) collective-permute-start(f32[2,2,3,2,48,256]{5,4,3,2,1,0:T(8,128)S(1)} %dynamic-slice_bitcast_fusion), channel_id=1, source_target_pairs={{0,16},{16,0},{32,48},{48,32},{64,80},{80,64},{96,112},{112,96},{1... | collective-permute-start | bytes 3538952 | tf_op jit(solution)/shard_map/ppermute | solution.py:19
  70.4 18.5 %collective-permute-start.3 = (f32[2,3,2,48,256]{4,3,2,1,0:T(8,128)}, f32[2,3,2,48,256]{4,3,2,1,0:T(8,128)}, u32[]{:S(2)}, u32[]{:S(2)}) collective-permute-start(f32[2,3,2,48,256]{4,3,2,1,0:T(8,128)} %dynamic-slice_bitcast_fusion.1), channel_id=1, source_target_pairs={{0,384},{16,400},{32,416},{48,432},{64,448},{80,464},{96,480},{112... | collective-permute-start | bytes 1769480 | tf_op jit(solution)/shard_map/ppermute | solution.py:19
  75.1 90.8 %copy-start.1 = (bf16[1,16,128,256]{3,2,1,0:T(8,128)(2,1)S(1)}, bf16[1,16,128,256]{3,2,1,0:T(8,128)(2,1)}, u32[]{:S(2)}) copy-start(bf16[1,16,128,256]{3,2,1,0:T(8,128)(2,1)} %param.6) | copy-start | bytes 3145732
  90.0 0.8 copy-start.3
  90.8 9.8 %collective-permute-start.4 = (f32[3,2,48,256]{3,2,1,0:T(8,128)S(1)}, f32[3,2,48,256]{3,2,1,0:T(8,128)S(1)}, u32[]{:S(2)}, u32[]{:S(2)}) collective-permute-start(f32[3,2,48,256]{3,2,1,0:T(8,128)S(1)} %dynamic-slice_bitcast_fusion.2), channel_id=1, source_target_pairs={{0,192},{16,208},{32,224},{48,240},{64,256},{80,272},{96,288},{112... | collective-permute-start | bytes 884744 | tf_op jit(solution)/shard_map/ppermute | solution.py:19
  101.7 7.5 %collective-permute-start.6 = (f32[2,48,256]{2,1,0:T(8,128)S(1)}, f32[2,48,256]{2,1,0:T(8,128)S(1)}, u32[]{:S(2)}, u32[]{:S(2)}) collective-permute-start(f32[2,48,256]{2,1,0:T(8,128)S(1)} %get-tuple-element.7), channel_id=1, source_target_pairs={{0,128},{16,144},{32,160},{48,176},{64,0},{80,16},{96,32},{112,48}... | collective-permute-start | bytes 294920 | tf_op jit(solution)/shard_map/ppermute | solution.py:32
  107.3 10.4 %collective-permute-start.5 = (f32[2,48,256]{2,1,0:T(8,128)S(1)}, f32[2,48,256]{2,1,0:T(8,128)S(1)}, u32[]{:S(2)}, u32[]{:S(2)}) collective-permute-start(f32[2,48,256]{2,1,0:T(8,128)S(1)} %get-tuple-element.6), channel_id=1, source_target_pairs={{0,64},{16,80},{32,96},{48,112},{64,128},{80,144},{96,160},{112,17... | collective-permute-start | bytes 294920 | tf_op jit(solution)/shard_map/ppermute | solution.py:32
  117.8 5.3 %collective-permute-start.7 = (f32[48,256]{1,0:T(8,128)S(1)}, f32[48,256]{1,0:T(8,128)S(1)}, u32[]{:S(2)}, u32[]{:S(2)}) collective-permute-start(f32[48,256]{1,0:T(8,128)S(1)} %dynamic-slice_bitcast_fusion.5), channel_id=1, source_target_pairs={{0,32},{16,48},{32,0},{48,16},{64,96},{80,112},{96,64},{112,80},{1... | collective-permute-start | bytes 147464 | tf_op jit(solution)/shard_map/ppermute | solution.py:19
  123.1 11.5 %collective-permute-start.8 = (f32[48,128]{1,0:T(8,128)S(1)}, f32[48,128]{1,0:T(8,128)S(1)}, u32[]{:S(2)}, u32[]{:S(2)}) collective-permute-start(f32[48,128]{1,0:T(8,128)S(1)} %bitcast.76), channel_id=1, source_target_pairs={{0,8},{1,9},{2,10},{3,11},{4,12},{5,13},{6,14},{7,15},{8,0},{9,1},... | collective-permute-start | bytes 73736 | tf_op jit(solution)/shard_map/ppermute | solution.py:19
  134.8 8.5 %collective-permute-start.9 = (f32[48,64]{1,0:T(8,128)S(1)}, f32[48,64]{1,0:T(8,128)S(1)}, u32[]{:S(2)}, u32[]{:S(2)}) collective-permute-start(f32[48,64]{1,0:T(8,128)S(1)} %bitcast.77), channel_id=1, source_target_pairs={{0,4},{1,5},{2,6},{3,7},{4,0},{5,1},{6,2},{7,3},{8,12},{9,13},{10,... | collective-permute-start | bytes 36872 | tf_op jit(solution)/shard_map/ppermute | solution.py:19
  143.4 5.7 %collective-permute-start.10 = (f32[48,32]{0,1:T(8,128)S(1)}, f32[48,32]{0,1:T(8,128)S(1)}, u32[]{:S(2)}, u32[]{:S(2)}) collective-permute-start(f32[48,32]{0,1:T(8,128)S(1)} %dynamic-slice_bitcast_fusion.6), channel_id=1, source_target_pairs={{0,2},{1,3},{2,0},{3,1},{4,6},{5,7},{6,4},{7,5},{8,10},{9,11},{10,... | collective-permute-start | bytes 18440 | tf_op jit(solution)/shard_map/ppermute | solution.py:19
  149.1 24.8 %collective-permute-start.11 = (f32[48,16]{0,1:T(8,128)S(1)}, f32[48,16]{0,1:T(8,128)S(1)}, u32[]{:S(2)}, u32[]{:S(2)}) collective-permute-start(f32[48,16]{0,1:T(8,128)S(1)} %dynamic-slice_bitcast_fusion.7), channel_id=1, source_target_pairs={{0,1},{1,0},{2,3},{3,2},{4,5},{5,4},{6,7},{7,6},{8,9},{9,8},{10,11... | collective-permute-start | bytes 9224 | tf_op jit(solution)/shard_map/ppermute | solution.py:19
Sparse Core Ops, SparseCore 0:
  75.2 90.7 all-gather.1

commit v5 on v4

--- a/solution.py
+++ b/solution.py
@@ -33,14 +33,7 @@
     return acc
 
 
-def gather_a2a(x, axis):
-    n = lax.axis_size(axis)
-    spread = jnp.broadcast_to(x[None], (n,) + x.shape)
-    got = lax.all_to_all(spread, axis, 0, 0)
-    return got.reshape((n * x.shape[0],) + x.shape[1:])
-
-
-def body(features, cotangent, conv_weight, norm_gain, norm_bias, film_rows):
+def body_inner(features, cotangent, conv_weight, norm_gain, norm_bias, film_rows):
     rows = features.shape[1]
     cols = features.shape[2]
     width = features.shape[3]
@@ -77,11 +70,10 @@
         lax.dot_general(cot_rows, patches, (((0,), (0,)), ((), ())), preferred_element_type=jnp.float32)
     )
     per = part_t.shape[1] // ndp
-    q = width // ntile
     g = part_t.T.reshape(2, 2, 3, 2, 2, per, width)
     g = halve(g, 4, "dp", 1)
+    g = halve(g, 1, "dp", 12)
     g = halve(g, 0, "dp", 24)
-    g = halve(g, 0, "dp", 12)
     g = direct(g, 0, "dp", 4, 3)
     g = halve(g, 0, "dp", 2)
     span = width
@@ -104,4 +96,4 @@
         P("dp", None),
     )
     out_specs = (P("dp", "tile", None, None), P("dp", "tile"))
-    return jax.shard_map(body, mesh=mesh, in_specs=in_specs, out_specs=out_specs, check_vma=False)
+    return jax.shard_map(body_inner, mesh=mesh, in_specs=in_specs, out_specs=out_specs, check_vma=False)

time: 182 us -> 182 us (level)
  no operation moved by 1% of the time
where the time goes in v5:
time: 182 us; the launch traced here: 181 us
  waiting for transfers between devices  81.4 us (45%)
  starting transfers between devices  56.1 us (31%)
  between operations  14.8 us (8%)
  matrix products  10.7 us (6%)
  other arithmetic  9.55 us (5%)
  local copies, waits for them, and re-layouts  8.94 us (5%)
    ppermute x8, waiting for transfers between devices, halve(): return mine + lax.ppermute(other, axis, pairs)  46 us
    ppermute x8, starting transfers between devices, halve(): return mine + lax.ppermute(other, axis, pairs)  22.2 us
    all_to_all x1, starting transfers between devices, body_inner(): lax.all_to_all(jnp.broadcast_to(stats[None], (ntile,) + stats.shape), 'ti...  19.8 us
    all_gather x1, waiting for transfers between devices, body_inner(): full_weight = lax.all_gather(conv_weight, 'dp', axis=0, tiled=True)  14.1 us
    all_to_all x1, waiting for transfers between devices, body_inner(): lax.all_to_all(jnp.broadcast_to(stats[None], (ntile,) + stats.shape), 'ti...  12.8 us
    ppermute x2, waiting for transfers between devices, direct(): acc = acc + lax.ppermute(piece, axis, pairs)  8.5 us
    ppermute x2, starting transfers between devices, direct(): acc = acc + lax.ppermute(piece, axis, pairs)  8.14 us
    dot_general x1, matrix products, body_inner(): conv = jnp.dot(patches, full_weight, preferred_element_type=jnp.float32)  7.91 us
  transfers between devices with their start and end apart: 14, of which 10 were waited for; matrix products, arithmetic and copies ran while one was open for 8% of the time, Pallas kernels for 0%

profile of v5, /device:TPU:1, one launch (start us, length us, event | category | flops | bytes accessed | tf_op | source)
XLA Modules:
  0.0 181.5 jit_solution(6142922764438192776)
XLA Ops:
  9.5 4.7 %collective-permute-start = (bf16[1,128,256]{2,1,0:T(8,128)(2,1)S(1)}, bf16[1,128,256]{2,1,0:T(8,128)(2,1)S(1)}, u32[]{:S(2)}, u32[]{:S(2)}) collective-permute-start(bf16[1,128,256]{2,1,0:T(8,128)(2,1)S(1)} %get-tuple-element.4), channel_id=1, source_target_pairs={{0,1},{1,2},{2,3},{3,4},{4,5},{5,6},{6,7},{7,8},{8,9},{9,10},{10,1... | collective-permute-start | bytes 196616 | tf_op jit(solution)/shard_map/ppermute | solution.py:45
  16.8 19.8 %all-to-all-start = ((f32[16,1,64]{2,1,0:T(1,128)}), f32[16,1,64]{2,1,0:T(1,128)S(1)}, u32[]{:S(2)}, u32[]{:S(2)}) async-start(f32[16,1,64]{2,1,0:T(1,128)} %broadcast_in_dim.32), calls=%async_computation | async-start | bytes 16384 | tf_op jit(solution)/shard_map/all_to_all | solution.py:50
  37.3 12.8 %all-to-all-done = f32[16,1,64]{2,1,0:T(1,128)S(1)} async-done(((f32[16,1,64]{2,1,0:T(1,128)}), f32[16,1,64]{2,1,0:T(1,128)S(1)}, u32[]{:S(2)}, u32[]{:S(2)}) %all-to-all-start) | async-done | bytes 4128 | tf_op jit(solution)/shard_map/all_to_all | solution.py:50
  50.5 2.3 %fusion.1 = bf16[18,128,256]{2,1,0:T(8,128)(2,1)S(1)} fusion(bf16[1,128,256]{2,1,0:T(8,128)(2,1)S(1)} %collective-permute-done.1, bf16[16,128,256]{2,1,0:T(8,128)(2,1)} %bitcast.65, bf16[1,128,256]{2,1,0:T(8,128)(2,1)S(1)} %collective-permute-done, f32[256]{0:T(256)S(1)} %bitcast.79, f32[256]{0:T(256)S(1)} %bitcast.78, f32[256]{0:T(256)} %param.10, ...), kind=kLoop, calls=%fused_computation.6 | loop fusion | flops 8847360 | bytes 2365458 | tf_op jit(solution)/shard_map/jit(_where)/select_n | solution.py:63
  55.4 2.8 %convolution_bitcast_fusion = f32[256,2304]{0,1:T(8,128)S(1)} fusion(bf16[2048,2304]{1,0:T(8,128)(2,1)S(1)} %bitcast.70, bf16[2048,256]{1,0:T(8,128)(2,1)S(1)} %bitcast.64), kind=kOutput, calls=%fused_computation | convolution fusion | flops 2415919104 | bytes 12845056 | tf_op jit(solution)/shard_map/dot_general | solution.py:70
  60.5 4.6 %collective-permute-start.2 = (f32[2,2,3,2,48,256]{5,4,3,2,1,0:T(8,128)S(1)}, f32[2,2,3,2,48,256]{5,4,3,2,1,0:T(8,128)}, u32[]{:S(2)}, u32[]{:S(2)}) collective-permute-start(f32[2,2,3,2,48,256]{5,4,3,2,1,0:T(8,128)S(1)} %dynamic-slice_bitcast_fusion), channel_id=1, source_target_pairs={{0,16},{16,0},{32,48},{48,32},{64,80},{80,64},{96,112},{112,96},{1... | collective-permute-start | bytes 3538952 | tf_op jit(solution)/shard_map/ppermute | solution.py:19
  65.2 2.5 %collective-permute-done.2 = f32[2,2,3,2,48,256]{5,4,3,2,1,0:T(8,128)} collective-permute-done((f32[2,2,3,2,48,256]{5,4,3,2,1,0:T(8,128)S(1)}, f32[2,2,3,2,48,256]{5,4,3,2,1,0:T(8,128)}, u32[]{:S(2)}, u32[]{:S(2)}) %collective-permute-start.2) | collective-permute-done | bytes 1179680 | tf_op jit(solution)/shard_map/ppermute | solution.py:19
  70.4 3.1 %collective-permute-start.3 = (f32[2,3,2,48,256]{4,3,2,1,0:T(8,128)}, f32[2,3,2,48,256]{4,3,2,1,0:T(8,128)}, u32[]{:S(2)}, u32[]{:S(2)}) collective-permute-start(f32[2,3,2,48,256]{4,3,2,1,0:T(8,128)} %dynamic-slice_bitcast_fusion.1), channel_id=1, source_target_pairs={{0,192},{16,208},{32,224},{48,240},{64,256},{80,272},{96,288},{112... | collective-permute-start | bytes 1769480 | tf_op jit(solution)/shard_map/ppermute | solution.py:19
  73.6 13.8 %collective-permute-done.3 = f32[2,3,2,48,256]{4,3,2,1,0:T(8,128)} collective-permute-done((f32[2,3,2,48,256]{4,3,2,1,0:T(8,128)}, f32[2,3,2,48,256]{4,3,2,1,0:T(8,128)}, u32[]{:S(2)}, u32[]{:S(2)}) %collective-permute-start.3) | collective-permute-done | bytes 589856 | tf_op jit(solution)/shard_map/ppermute | solution.py:19
  89.3 4.7 %collective-permute-start.4 = (f32[3,2,48,256]{3,2,1,0:T(8,128)S(1)}, f32[3,2,48,256]{3,2,1,0:T(8,128)S(1)}, u32[]{:S(2)}, u32[]{:S(2)}) collective-permute-start(f32[3,2,48,256]{3,2,1,0:T(8,128)S(1)} %dynamic-slice_bitcast_fusion.2), channel_id=1, source_target_pairs={{0,384},{16,400},{32,416},{48,432},{64,448},{80,464},{96,480},{112... | collective-permute-start | bytes 884744 | tf_op jit(solution)/shard_map/ppermute | solution.py:19
  94.1 6.8 %collective-permute-done.4 = f32[3,2,48,256]{3,2,1,0:T(8,128)S(1)} collective-permute-done((f32[3,2,48,256]{3,2,1,0:T(8,128)S(1)}, f32[3,2,48,256]{3,2,1,0:T(8,128)S(1)}, u32[]{:S(2)}, u32[]{:S(2)}) %collective-permute-start.4) | collective-permute-done | bytes 294944 | tf_op jit(solution)/shard_map/ppermute | solution.py:19
  101.9 6.2 %collective-permute-start.6 = (f32[2,48,256]{2,1,0:T(8,128)S(1)}, f32[2,48,256]{2,1,0:T(8,128)S(1)}, u32[]{:S(2)}, u32[]{:S(2)}) collective-permute-start(f32[2,48,256]{2,1,0:T(8,128)S(1)} %get-tuple-element.7), channel_id=1, source_target_pairs={{0,128},{16,144},{32,160},{48,176},{64,0},{80,16},{96,32},{112,48}... | collective-permute-start | bytes 294920 | tf_op jit(solution)/shard_map/ppermute | solution.py:32
  108.1 1.9 %collective-permute-start.5 = (f32[2,48,256]{2,1,0:T(8,128)S(1)}, f32[2,48,256]{2,1,0:T(8,128)S(1)}, u32[]{:S(2)}, u32[]{:S(2)}) collective-permute-start(f32[2,48,256]{2,1,0:T(8,128)S(1)} %get-tuple-element.6), channel_id=1, source_target_pairs={{0,64},{16,80},{32,96},{48,112},{64,128},{80,144},{96,160},{112,17... | collective-permute-start | bytes 294920 | tf_op jit(solution)/shard_map/ppermute | solution.py:32
  110.1 8.5 %collective-permute-done.5 = f32[2,48,256]{2,1,0:T(8,128)S(1)} collective-permute-done((f32[2,48,256]{2,1,0:T(8,128)S(1)}, f32[2,48,256]{2,1,0:T(8,128)S(1)}, u32[]{:S(2)}, u32[]{:S(2)}) %collective-permute-start.5) | collective-permute-done | bytes 98336 | tf_op jit(solution)/shard_map/ppermute | solution.py:32
  118.7 1.9 %collective-permute-start.7 = (f32[48,256]{1,0:T(8,128)S(1)}, f32[48,256]{1,0:T(8,128)S(1)}, u32[]{:S(2)}, u32[]{:S(2)}) collective-permute-start(f32[48,256]{1,0:T(8,128)S(1)} %dynamic-slice_bitcast_fusion.5), channel_id=1, source_target_pairs={{0,32},{16,48},{32,0},{48,16},{64,96},{80,112},{96,64},{112,80},{1... | collective-permute-start | bytes 147464 | tf_op jit(solution)/shard_map/ppermute | solution.py:19
  120.6 3.4 %collective-permute-done.7 = f32[48,256]{1,0:T(8,128)S(1)} collective-permute-done((f32[48,256]{1,0:T(8,128)S(1)}, f32[48,256]{1,0:T(8,128)S(1)}, u32[]{:S(2)}, u32[]{:S(2)}) %collective-permute-start.7) | collective-permute-done | bytes 49184 | tf_op jit(solution)/shard_map/ppermute | solution.py:19
  124.2 2.0 %collective-permute-start.8 = (f32[48,128]{1,0:T(8,128)S(1)}, f32[48,128]{1,0:T(8,128)S(1)}, u32[]{:S(2)}, u32[]{:S(2)}) collective-permute-start(f32[48,128]{1,0:T(8,128)S(1)} %bitcast.76), channel_id=1, source_target_pairs={{0,8},{1,9},{2,10},{3,11},{4,12},{5,13},{6,14},{7,15},{8,0},{9,1},... | collective-permute-start | bytes 73736 | tf_op jit(solution)/shard_map/ppermute | solution.py:19
  126.3 9.2 %collective-permute-done.8 = f32[48,128]{1,0:T(8,128)S(1)} collective-permute-done((f32[48,128]{1,0:T(8,128)S(1)}, f32[48,128]{1,0:T(8,128)S(1)}, u32[]{:S(2)}, u32[]{:S(2)}) %collective-permute-start.8) | collective-permute-done | bytes 24608 | tf_op jit(solution)/shard_map/ppermute | solution.py:19
  135.6 1.9 %collective-permute-start.9 = (f32[48,64]{1,0:T(8,128)S(1)}, f32[48,64]{1,0:T(8,128)S(1)}, u32[]{:S(2)}, u32[]{:S(2)}) collective-permute-start(f32[48,64]{1,0:T(8,128)S(1)} %bitcast.77), channel_id=1, source_target_pairs={{0,4},{1,5},{2,6},{3,7},{4,0},{5,1},{6,2},{7,3},{8,12},{9,13},{10,... | collective-permute-start | bytes 36872 | tf_op jit(solution)/shard_map/ppermute | solution.py:19
  137.6 6.5 %collective-permute-done.9 = f32[48,64]{1,0:T(8,128)S(1)} collective-permute-done((f32[48,64]{1,0:T(8,128)S(1)}, f32[48,64]{1,0:T(8,128)S(1)}, u32[]{:S(2)}, u32[]{:S(2)}) %collective-permute-start.9) | collective-permute-done | bytes 12320 | tf_op jit(solution)/shard_map/ppermute | solution.py:19
  146.1 3.7 %collective-permute-done.10 = f32[48,32]{0,1:T(8,128)S(1)} collective-permute-done((f32[48,32]{0,1:T(8,128)S(1)}, f32[48,32]{0,1:T(8,128)S(1)}, u32[]{:S(2)}, u32[]{:S(2)}) %collective-permute-start.10) | collective-permute-done | bytes 6176 | tf_op jit(solution)/shard_map/ppermute | solution.py:19
  149.9 2.1 %collective-permute-start.11 = (f32[48,16]{0,1:T(8,128)S(1)}, f32[48,16]{0,1:T(8,128)S(1)}, u32[]{:S(2)}, u32[]{:S(2)}) collective-permute-start(f32[48,16]{0,1:T(8,128)S(1)} %dynamic-slice_bitcast_fusion.7), channel_id=1, source_target_pairs={{0,1},{1,0},{2,3},{3,2},{4,5},{5,4},{6,7},{7,6},{8,9},{9,8},{10,11... | collective-permute-start | bytes 9224 | tf_op jit(solution)/shard_map/ppermute | solution.py:19
  152.0 14.1 %all-gather.2.cloned.1.call-done = bf16[2304,256]{1,0:T(8,128)(2,1)} async-done(((bf16[48,256]{1,0:T(8,128)(2,1)}), bf16[2304,256]{1,0:T(8,128)(2,1)}) %all-gather.2.cloned.1.call-update) | async-done | bytes 1179664 | tf_op jit(solution)/shard_map/all_gather | solution.py:43
  166.1 7.9 %add_bitcast_fusion = f32[1,16,128,256]{3,2,1,0:T(8,128)} fusion(bf16[16,128,2304]{2,1,0:T(8,128)(2,1)} %copy-done.4, bf16[2304,256]{1,0:T(8,128)(2,1)} %all-gather.2.cloned.1.call-done, bf16[1,16,128,256]{3,2,1,0:T(8,128)(2,1)S(1)} %copy-done.1), kind=kOutput, calls=%fused_computation.5 | convolution fusion | flops 2416967680 | bytes 13762560 | tf_op jit(solution)/shard_map/dot_general | solution.py:84
  (64 shorter events, 19.5 us)
Async XLA Ops:
  7.2 48.2 %copy-start = (bf16[1,16,128,256]{3,2,1,0:T(8,128)(2,1)S(1)}, bf16[1,16,128,256]{3,2,1,0:T(8,128)(2,1)}, u32[]{:S(2)}) copy-start(bf16[1,16,128,256]{3,2,1,0:T(8,128)(2,1)} %param.7) | copy-start | bytes 3145732
  8.2 42.4 %collective-permute-start.1 = (bf16[1,128,256]{2,1,0:T(8,128)(2,1)S(1)}, bf16[1,128,256]{2,1,0:T(8,128)(2,1)S(1)}, u32[]{:S(2)}, u32[]{:S(2)}) collective-permute-start(bf16[1,128,256]{2,1,0:T(8,128)(2,1)S(1)} %get-tuple-element.5), channel_id=1, source_target_pairs={{1,0},{2,1},{3,2},{4,3},{5,4},{6,5},{7,6},{8,7},{9,8},{10,9},{11,1... | collective-permute-start | bytes 196616 | tf_op jit(solution)/shard_map/ppermute | solution.py:46
  9.5 41.1 %collective-permute-start = (bf16[1,128,256]{2,1,0:T(8,128)(2,1)S(1)}, bf16[1,128,256]{2,1,0:T(8,128)(2,1)S(1)}, u32[]{:S(2)}, u32[]{:S(2)}) collective-permute-start(bf16[1,128,256]{2,1,0:T(8,128)(2,1)S(1)} %get-tuple-element.4), channel_id=1, source_target_pairs={{0,1},{1,2},{2,3},{3,4},{4,5},{5,6},{6,7},{7,8},{8,9},{9,10},{10,1... | collective-permute-start | bytes 196616 | tf_op jit(solution)/shard_map/ppermute | solution.py:45
  16.8 33.3 %all-to-all-start = ((f32[16,1,64]{2,1,0:T(1,128)}), f32[16,1,64]{2,1,0:T(1,128)S(1)}, u32[]{:S(2)}, u32[]{:S(2)}) async-start(f32[16,1,64]{2,1,0:T(1,128)} %broadcast_in_dim.32), calls=%async_computation | async-start | bytes 16384 | tf_op jit(solution)/shard_map/all_to_all | solution.py:50
  36.5 129.6 %all-gather.2.cloned.1.call-start = ((), (), s32[]{:S(2)}) async-start(), calls=%async_computation.1 | async-start | bytes 1204224 | tf_op jit(solution)/shard_map/all_gather | solution.py:43
  55.4 3.7 %copy-start.4 = (bf16[16,128,2304]{2,1,0:T(8,128)(2,1)}, bf16[16,128,2304]{2,1,0:T(8,128)(2,1)S(1)}, u32[]{:S(2)}) copy-start(bf16[16,128,2304]{2,1,0:T(8,128)(2,1)S(1)} %slice_dynamic-update-slice_fusion.3) | copy-start | bytes 28311556
  59.0 1.4 copy-start.2
  60.5 7.2 %collective-permute-start.2 = (f32[2,2,3,2,48,256]{5,4,3,2,1,0:T(8,128)S(1)}, f32[2,2,3,2,48,256]{5,4,3,2,1,0:T(8,128)}, u32[]{:S(2)}, u32[]{:S(2)}) collective-permute-start(f32[2,2,3,2,48,256]{5,4,3,2,1,0:T(8,128)S(1)} %dynamic-slice_bitcast_fusion), channel_id=1, source_target_pairs={{0,16},{16,0},{32,48},{48,32},{64,80},{80,64},{96,112},{112,96},{1... | collective-permute-start | bytes 3538952 | tf_op jit(solution)/shard_map/ppermute | solution.py:19
  70.4 17.0 %collective-permute-start.3 = (f32[2,3,2,48,256]{4,3,2,1,0:T(8,128)}, f32[2,3,2,48,256]{4,3,2,1,0:T(8,128)}, u32[]{:S(2)}, u32[]{:S(2)}) collective-permute-start(f32[2,3,2,48,256]{4,3,2,1,0:T(8,128)} %dynamic-slice_bitcast_fusion.1), channel_id=1, source_target_pairs={{0,192},{16,208},{32,224},{48,240},{64,256},{80,272},{96,288},{112... | collective-permute-start | bytes 1769480 | tf_op jit(solution)/shard_map/ppermute | solution.py:19
  73.6 92.5 %copy-start.1 = (bf16[1,16,128,256]{3,2,1,0:T(8,128)(2,1)S(1)}, bf16[1,16,128,256]{3,2,1,0:T(8,128)(2,1)}, u32[]{:S(2)}) copy-start(bf16[1,16,128,256]{3,2,1,0:T(8,128)(2,1)} %param.6) | copy-start | bytes 3145732
  88.5 0.8 copy-start.3
  89.3 11.5 %collective-permute-start.4 = (f32[3,2,48,256]{3,2,1,0:T(8,128)S(1)}, f32[3,2,48,256]{3,2,1,0:T(8,128)S(1)}, u32[]{:S(2)}, u32[]{:S(2)}) collective-permute-start(f32[3,2,48,256]{3,2,1,0:T(8,128)S(1)} %dynamic-slice_bitcast_fusion.2), channel_id=1, source_target_pairs={{0,384},{16,400},{32,416},{48,432},{64,448},{80,464},{96,480},{112... | collective-permute-start | bytes 884744 | tf_op jit(solution)/shard_map/ppermute | solution.py:19
  101.9 8.2 %collective-permute-start.6 = (f32[2,48,256]{2,1,0:T(8,128)S(1)}, f32[2,48,256]{2,1,0:T(8,128)S(1)}, u32[]{:S(2)}, u32[]{:S(2)}) collective-permute-start(f32[2,48,256]{2,1,0:T(8,128)S(1)} %get-tuple-element.7), channel_id=1, source_target_pairs={{0,128},{16,144},{32,160},{48,176},{64,0},{80,16},{96,32},{112,48}... | collective-permute-start | bytes 294920 | tf_op jit(solution)/shard_map/ppermute | solution.py:32
  108.1 10.5 %collective-permute-start.5 = (f32[2,48,256]{2,1,0:T(8,128)S(1)}, f32[2,48,256]{2,1,0:T(8,128)S(1)}, u32[]{:S(2)}, u32[]{:S(2)}) collective-permute-start(f32[2,48,256]{2,1,0:T(8,128)S(1)} %get-tuple-element.6), channel_id=1, source_target_pairs={{0,64},{16,80},{32,96},{48,112},{64,128},{80,144},{96,160},{112,17... | collective-permute-start | bytes 294920 | tf_op jit(solution)/shard_map/ppermute | solution.py:32
  118.7 5.4 %collective-permute-start.7 = (f32[48,256]{1,0:T(8,128)S(1)}, f32[48,256]{1,0:T(8,128)S(1)}, u32[]{:S(2)}, u32[]{:S(2)}) collective-permute-start(f32[48,256]{1,0:T(8,128)S(1)} %dynamic-slice_bitcast_fusion.5), channel_id=1, source_target_pairs={{0,32},{16,48},{32,0},{48,16},{64,96},{80,112},{96,64},{112,80},{1... | collective-permute-start | bytes 147464 | tf_op jit(solution)/shard_map/ppermute | solution.py:19
  124.2 11.3 %collective-permute-start.8 = (f32[48,128]{1,0:T(8,128)S(1)}, f32[48,128]{1,0:T(8,128)S(1)}, u32[]{:S(2)}, u32[]{:S(2)}) collective-permute-start(f32[48,128]{1,0:T(8,128)S(1)} %bitcast.76), channel_id=1, source_target_pairs={{0,8},{1,9},{2,10},{3,11},{4,12},{5,13},{6,14},{7,15},{8,0},{9,1},... | collective-permute-start | bytes 73736 | tf_op jit(solution)/shard_map/ppermute | solution.py:19
  135.6 8.5 %collective-permute-start.9 = (f32[48,64]{1,0:T(8,128)S(1)}, f32[48,64]{1,0:T(8,128)S(1)}, u32[]{:S(2)}, u32[]{:S(2)}) collective-permute-start(f32[48,64]{1,0:T(8,128)S(1)} %bitcast.77), channel_id=1, source_target_pairs={{0,4},{1,5},{2,6},{3,7},{4,0},{5,1},{6,2},{7,3},{8,12},{9,13},{10,... | collective-permute-start | bytes 36872 | tf_op jit(solution)/shard_map/ppermute | solution.py:19
  144.2 5.7 %collective-permute-start.10 = (f32[48,32]{0,1:T(8,128)S(1)}, f32[48,32]{0,1:T(8,128)S(1)}, u32[]{:S(2)}, u32[]{:S(2)}) collective-permute-start(f32[48,32]{0,1:T(8,128)S(1)} %dynamic-slice_bitcast_fusion.6), channel_id=1, source_target_pairs={{0,2},{1,3},{2,0},{3,1},{4,6},{5,7},{6,4},{7,5},{8,10},{9,11},{10,... | collective-permute-start | bytes 18440 | tf_op jit(solution)/shard_map/ppermute | solution.py:19
  149.9 24.1 %collective-permute-start.11 = (f32[48,16]{0,1:T(8,128)S(1)}, f32[48,16]{0,1:T(8,128)S(1)}, u32[]{:S(2)}, u32[]{:S(2)}) collective-permute-start(f32[48,16]{0,1:T(8,128)S(1)} %dynamic-slice_bitcast_fusion.7), channel_id=1, source_target_pairs={{0,1},{1,0},{2,3},{3,2},{4,5},{5,4},{6,7},{7,6},{8,9},{9,8},{10,11... | collective-permute-start | bytes 9224 | tf_op jit(solution)/shard_map/ppermute | solution.py:19
Sparse Core Ops, SparseCore 0:
  73.6 92.4 all-gather.1

commit v6 on v5

--- a/solution.py
+++ b/solution.py
@@ -47,7 +47,8 @@
     values = raw.astype(jnp.float32)
     grouped = values.reshape(rows, cols, G, width // G)
     stats = jnp.concatenate([jnp.sum(grouped, axis=(0, 1, 3)), jnp.sum(grouped * grouped, axis=(0, 1, 3))])
-    stats = jnp.sum(lax.all_to_all(jnp.broadcast_to(stats[None], (ntile,) + stats.shape), "tile", 0, 0), axis=0)
+    stats = lax.all_to_all(jnp.broadcast_to(stats[None], (ntile,) + stats.shape), "tile", 0, 0)
+    stats = jnp.sum(stats, axis=0)
     sums, squares = stats[:G], stats[G:]
     count = rows * ntile * cols * (width // G)
     mean = sums / count
@@ -72,10 +73,14 @@
     per = part_t.shape[1] // ndp
     g = part_t.T.reshape(2, 2, 3, 2, 2, per, width)
     g = halve(g, 4, "dp", 1)
-    g = halve(g, 1, "dp", 12)
+    half = width // 2
+    ga = halve(g[..., :half], 1, "dp", 12)
+    gb = halve(g[..., half:], 3, "dp", 2)
+    ga = halve(ga, 2, "dp", 2)
+    gb = halve(gb, 1, "dp", 12)
+    g = jnp.concatenate([ga, gb], axis=-1)
     g = halve(g, 0, "dp", 24)
     g = direct(g, 0, "dp", 4, 3)
-    g = halve(g, 0, "dp", 2)
     span = width
     for stride in (8, 4, 2, 1):
         span //= 2

time: 182 us -> 176 us (0.967)
  waiting for transfers between devices: 81.4 us -> 73.1 us
  starting transfers between devices: 56.1 us -> 63.6 us
  other arithmetic: 9.55 us -> 5.89 us
    ppermute x8 -> x10, waiting for transfers between devices: 46 us -> 34 us  [halve(): return mine + lax.ppermute(other, axis, pairs)]
    ppermute x8 -> x10, starting transfers between devices: 22.2 us -> 29.9 us  [halve(): return mine + lax.ppermute(other, axis, pairs)]
    all_gather x1, waiting for transfers between devices: 14.1 us -> 18.8 us  [body_inner(): full_weight = lax.all_gather(conv_weight, 'dp', axis=0, tiled=True)]
    add x7 -> x9, other arithmetic: 3.97 us -> 0.29 us  [halve(): return mine + lax.ppermute(other, axis, pairs)]
    unnamed x18 -> x14, local copies, waits for them, and re-layouts: 5.13 us -> 2.91 us
  transfers between devices with their start and end apart: 14 -> 16, of which waited for: 10 -> 12; matrix products, arithmetic and copies ran while one was open for 8% -> 3% of each run, Pallas kernels for 0% -> 0%
where the time goes in v6:
time: 176 us; the launch traced here: 175 us
  waiting for transfers between devices  73.1 us (42%)
  starting transfers between devices  63.6 us (36%)
  between operations  14.8 us (8%)
  matrix products  10.7 us (6%)
  local copies, waits for them, and re-layouts  7.24 us (4%)
  other arithmetic  5.89 us (3%)
    ppermute x10, waiting for transfers between devices, halve(): return mine + lax.ppermute(other, axis, pairs)  34 us
    ppermute x10, starting transfers between devices, halve(): return mine + lax.ppermute(other, axis, pairs)  29.9 us
    all_to_all x1, starting transfers between devices, body_inner(): lax.all_to_all(jnp.broadcast_to(stats[None], (ntile,) + stats.shape), 'ti...  19.8 us
    all_gather x1, waiting for transfers between devices, body_inner(): full_weight = lax.all_gather(conv_weight, 'dp', axis=0, tiled=True)  18.8 us
    all_to_all x1, waiting for transfers between devices, body_inner(): lax.all_to_all(jnp.broadcast_to(stats[None], (ntile,) + stats.shape), 'ti...  12.8 us
    ppermute x2, starting transfers between devices, direct(): acc = acc + lax.ppermute(piece, axis, pairs)  7.93 us
    dot_general x1, matrix products, body_inner(): conv = jnp.dot(patches, full_weight, preferred_element_type=jnp.float32)  7.92 us
    ppermute x2, waiting for transfers between devices, direct(): acc = acc + lax.ppermute(piece, axis, pairs)  7.43 us
  transfers between devices with their start and end apart: 16, of which 12 were waited for; matrix products, arithmetic and copies ran while one was open for 3% of the time, Pallas kernels for 0%

profile of v6, /device:TPU:1, one launch (start us, length us, event | category | flops | bytes accessed | tf_op | source)
XLA Modules:
  0.0 175.3 jit_solution(16335999928540851942)
XLA Ops:
  9.5 4.7 %collective-permute-start = (bf16[1,128,256]{2,1,0:T(8,128)(2,1)S(1)}, bf16[1,128,256]{2,1,0:T(8,128)(2,1)S(1)}, u32[]{:S(2)}, u32[]{:S(2)}) collective-permute-start(bf16[1,128,256]{2,1,0:T(8,128)(2,1)S(1)} %get-tuple-element.8), channel_id=1, source_target_pairs={{0,1},{1,2},{2,3},{3,4},{4,5},{5,6},{6,7},{7,8},{8,9},{9,10},{10,1... | collective-permute-start | bytes 196616 | tf_op jit(solution)/shard_map/ppermute | solution.py:45
  16.8 19.8 %all-to-all-start = ((f32[16,1,64]{2,1,0:T(1,128)}), f32[16,1,64]{2,1,0:T(1,128)S(1)}, u32[]{:S(2)}, u32[]{:S(2)}) async-start(f32[16,1,64]{2,1,0:T(1,128)} %broadcast_in_dim.32), calls=%async_computation | async-start | bytes 16384 | tf_op jit(solution)/shard_map/all_to_all | solution.py:50
  37.3 12.8 %all-to-all-done = f32[16,1,64]{2,1,0:T(1,128)S(1)} async-done(((f32[16,1,64]{2,1,0:T(1,128)}), f32[16,1,64]{2,1,0:T(1,128)S(1)}, u32[]{:S(2)}, u32[]{:S(2)}) %all-to-all-start) | async-done | bytes 4128 | tf_op jit(solution)/shard_map/all_to_all | solution.py:50
  50.5 2.3 %fusion.1 = bf16[18,128,256]{2,1,0:T(8,128)(2,1)S(1)} fusion(bf16[1,128,256]{2,1,0:T(8,128)(2,1)S(1)} %collective-permute-done.1, bf16[16,128,256]{2,1,0:T(8,128)(2,1)} %bitcast.77, bf16[1,128,256]{2,1,0:T(8,128)(2,1)S(1)} %collective-permute-done, f32[256]{0:T(256)S(1)} %bitcast.91, f32[256]{0:T(256)S(1)} %bitcast.90, f32[256]{0:T(256)} %param.10, ...), kind=kLoop, calls=%fused_computation.6 | loop fusion | flops 8847360 | bytes 2365458 | tf_op jit(solution)/shard_map/jit(_where)/select_n | solution.py:64
  55.4 2.8 %convolution_bitcast_fusion = f32[256,2304]{0,1:T(8,128)S(1)} fusion(bf16[2048,2304]{1,0:T(8,128)(2,1)S(1)} %bitcast.82, bf16[2048,256]{1,0:T(8,128)(2,1)S(1)} %bitcast.76), kind=kOutput, calls=%fused_computation | convolution fusion | flops 2415919104 | bytes 12845056 | tf_op jit(solution)/shard_map/dot_general | solution.py:71
  60.3 4.6 %collective-permute-start.2 = (f32[2,2,3,2,48,256]{5,4,3,2,0,1:T(8,128)}, f32[2,2,3,2,48,256]{5,4,3,2,0,1:T(8,128)S(1)}, u32[]{:S(2)}, u32[]{:S(2)}) collective-permute-start(f32[2,2,3,2,48,256]{5,4,3,2,0,1:T(8,128)} %bitcast.74), channel_id=1, source_target_pairs={{0,16},{16,0},{32,48},{48,32},{64,80},{80,64},{96,112},{112,96},{1... | collective-permute-start | bytes 3538952 | tf_op jit(solution)/shard_map/ppermute | solution.py:19
  64.9 2.6 %collective-permute-done.2 = f32[2,2,3,2,48,256]{5,4,3,2,0,1:T(8,128)S(1)} collective-permute-done((f32[2,2,3,2,48,256]{5,4,3,2,0,1:T(8,128)}, f32[2,2,3,2,48,256]{5,4,3,2,0,1:T(8,128)S(1)}, u32[]{:S(2)}, u32[]{:S(2)}) %collective-permute-start.2) | collective-permute-done | bytes 1179680 | tf_op jit(solution)/shard_map/ppermute | solution.py:19
  67.8 3.1 %collective-permute-start.3 = (f32[2,3,2,48,128]{4,3,2,1,0:T(8,128)S(1)}, f32[2,3,2,48,128]{4,3,2,1,0:T(8,128)S(1)}, u32[]{:S(2)}, u32[]{:S(2)}) collective-permute-start(f32[2,3,2,48,128]{4,3,2,1,0:T(8,128)S(1)} %dynamic-slice_bitcast_fusion), channel_id=1, source_target_pairs={{0,192},{16,208},{32,224},{48,240},{64,256},{80,272},{96,288},{112... | collective-permute-start | bytes 884744 | tf_op jit(solution)/shard_map/ppermute | solution.py:19
  71.2 3.1 %collective-permute-start.5 = (f32[2,2,3,48,128]{4,3,2,1,0:T(8,128)S(1)}, f32[2,2,3,48,128]{4,3,2,1,0:T(8,128)S(1)}, u32[]{:S(2)}, u32[]{:S(2)}) collective-permute-start(f32[2,2,3,48,128]{4,3,2,1,0:T(8,128)S(1)} %bitcast.79), channel_id=1, source_target_pairs={{0,32},{16,48},{32,0},{48,16},{64,96},{80,112},{96,64},{112,80},{1... | collective-permute-start | bytes 884744 | tf_op jit(solution)/shard_map/ppermute | solution.py:19
  74.3 3.7 %collective-permute-done.3 = f32[2,3,2,48,128]{4,3,2,1,0:T(8,128)S(1)} collective-permute-done((f32[2,3,2,48,128]{4,3,2,1,0:T(8,128)S(1)}, f32[2,3,2,48,128]{4,3,2,1,0:T(8,128)S(1)}, u32[]{:S(2)}, u32[]{:S(2)}) %collective-permute-start.3) | collective-permute-done | bytes 294944 | tf_op jit(solution)/shard_map/ppermute | solution.py:19
  78.0 3.2 %collective-permute-start.4 = (f32[2,3,48,128]{3,2,1,0:T(8,128)S(1)}, f32[2,3,48,128]{3,2,1,0:T(8,128)S(1)}, u32[]{:S(2)}, u32[]{:S(2)}) collective-permute-start(f32[2,3,48,128]{3,2,1,0:T(8,128)S(1)} %dynamic-slice_bitcast_fusion.2), channel_id=1, source_target_pairs={{0,32},{16,48},{32,0},{48,16},{64,96},{80,112},{96,64},{112,80},{1... | collective-permute-start | bytes 442376 | tf_op jit(solution)/shard_map/ppermute | solution.py:19
  81.3 3.1 %collective-permute-start.6 = (f32[2,3,48,128]{3,2,1,0:T(8,128)S(1)}, f32[2,3,48,128]{3,2,1,0:T(8,128)S(1)}, u32[]{:S(2)}, u32[]{:S(2)}) collective-permute-start(f32[2,3,48,128]{3,2,1,0:T(8,128)S(1)} %dynamic-slice_bitcast_fusion.1), channel_id=1, source_target_pairs={{0,192},{16,208},{32,224},{48,240},{64,256},{80,272},{96,288},{112... | collective-permute-start | bytes 442376 | tf_op jit(solution)/shard_map/ppermute | solution.py:19
  84.8 2.6 %collective-permute-done.6 = f32[2,3,48,128]{3,2,1,0:T(8,128)S(1)} collective-permute-done((f32[2,3,48,128]{3,2,1,0:T(8,128)S(1)}, f32[2,3,48,128]{3,2,1,0:T(8,128)S(1)}, u32[]{:S(2)}, u32[]{:S(2)}) %collective-permute-start.6) | collective-permute-done | bytes 147488 | tf_op jit(solution)/shard_map/ppermute | solution.py:19
  87.4 4.6 %collective-permute-start.7 = (f32[3,48,256]{2,1,0:T(8,128)S(1)}, f32[3,48,256]{2,1,0:T(8,128)S(1)}, u32[]{:S(2)}, u32[]{:S(2)}) collective-permute-start(f32[3,48,256]{2,1,0:T(8,128)S(1)} %fusion.4), channel_id=1, source_target_pairs={{0,384},{16,400},{32,416},{48,432},{64,448},{80,464},{96,480},{112... | collective-permute-start | bytes 442376 | tf_op jit(solution)/shard_map/ppermute | solution.py:19
  92.1 2.9 %collective-permute-done.7 = f32[3,48,256]{2,1,0:T(8,128)S(1)} collective-permute-done((f32[3,48,256]{2,1,0:T(8,128)S(1)}, f32[3,48,256]{2,1,0:T(8,128)S(1)}, u32[]{:S(2)}, u32[]{:S(2)}) %collective-permute-start.7) | collective-permute-done | bytes 147488 | tf_op jit(solution)/shard_map/ppermute | solution.py:19
  95.1 6.0 %collective-permute-start.9 = (f32[48,256]{1,0:T(8,128)S(1)}, f32[48,256]{1,0:T(8,128)S(1)}, u32[]{:S(2)}, u32[]{:S(2)}) collective-permute-start(f32[48,256]{1,0:T(8,128)S(1)} %get-tuple-element.13), channel_id=1, source_target_pairs={{0,128},{16,144},{32,160},{48,176},{64,0},{80,16},{96,32},{112,48}... | collective-permute-start | bytes 147464 | tf_op jit(solution)/shard_map/ppermute | solution.py:32
  103.1 7.4 %collective-permute-done.8 = f32[48,256]{1,0:T(8,128)S(1)} collective-permute-done((f32[48,256]{1,0:T(8,128)S(1)}, f32[48,256]{1,0:T(8,128)S(1)}, u32[]{:S(2)}, u32[]{:S(2)}) %collective-permute-start.8) | collective-permute-done | bytes 49184 | tf_op jit(solution)/shard_map/ppermute | solution.py:32
  112.6 9.3 %collective-permute-done.10 = f32[48,128]{1,0:T(8,128)S(1)} collective-permute-done((f32[48,128]{1,0:T(8,128)S(1)}, f32[48,128]{1,0:T(8,128)S(1)}, u32[]{:S(2)}, u32[]{:S(2)}) %collective-permute-start.10) | collective-permute-done | bytes 24608 | tf_op jit(solution)/shard_map/ppermute | solution.py:19
  122.0 2.2 %collective-permute-start.11 = (f32[48,64]{1,0:T(8,128)S(1)}, f32[48,64]{1,0:T(8,128)S(1)}, u32[]{:S(2)}, u32[]{:S(2)}) collective-permute-start(f32[48,64]{1,0:T(8,128)S(1)} %bitcast.89), channel_id=1, source_target_pairs={{0,4},{1,5},{2,6},{3,7},{4,0},{5,1},{6,2},{7,3},{8,12},{9,13},{10,... | collective-permute-start | bytes 36872 | tf_op jit(solution)/shard_map/ppermute | solution.py:19
  124.3 6.3 %collective-permute-done.11 = f32[48,64]{1,0:T(8,128)S(1)} collective-permute-done((f32[48,64]{1,0:T(8,128)S(1)}, f32[48,64]{1,0:T(8,128)S(1)}, u32[]{:S(2)}, u32[]{:S(2)}) %collective-permute-start.11) | collective-permute-done | bytes 12320 | tf_op jit(solution)/shard_map/ppermute | solution.py:19
  132.6 3.7 %collective-permute-done.12 = f32[48,32]{0,1:T(8,128)S(1)} collective-permute-done((f32[48,32]{0,1:T(8,128)S(1)}, f32[48,32]{0,1:T(8,128)S(1)}, u32[]{:S(2)}, u32[]{:S(2)}) %collective-permute-start.12) | collective-permute-done | bytes 6176 | tf_op jit(solution)/shard_map/ppermute | solution.py:19
  138.4 2.7 %collective-permute-done.13 = f32[48,16]{0,1:T(8,128)S(1)} collective-permute-done((f32[48,16]{0,1:T(8,128)S(1)}, f32[48,16]{0,1:T(8,128)S(1)}, u32[]{:S(2)}, u32[]{:S(2)}) %collective-permute-start.13) | collective-permute-done | bytes 3104 | tf_op jit(solution)/shard_map/ppermute | solution.py:19
  141.7 18.8 %all-gather.2.cloned.1.call-done = bf16[2304,256]{1,0:T(8,128)(2,1)} async-done(((bf16[48,256]{1,0:T(8,128)(2,1)}), bf16[2304,256]{1,0:T(8,128)(2,1)}) %all-gather.2.cloned.1.call-update) | async-done | bytes 1179664 | tf_op jit(solution)/shard_map/all_gather | solution.py:43
  160.5 7.9 %add_bitcast_fusion = f32[1,16,128,256]{3,2,1,0:T(8,128)} fusion(bf16[16,128,2304]{2,1,0:T(8,128)(2,1)} %copy-done.2, bf16[2304,256]{1,0:T(8,128)(2,1)} %all-gather.2.cloned.1.call-done, bf16[1,16,128,256]{3,2,1,0:T(8,128)(2,1)S(1)} %copy-done.1), kind=kOutput, calls=%fused_computation.5 | convolution fusion | flops 2416967680 | bytes 13762560 | tf_op jit(solution)/shard_map/dot_general | solution.py:89
  (71 shorter events, 20.3 us)
Async XLA Ops:
  7.2 48.2 %copy-start = (bf16[1,16,128,256]{3,2,1,0:T(8,128)(2,1)S(1)}, bf16[1,16,128,256]{3,2,1,0:T(8,128)(2,1)}, u32[]{:S(2)}) copy-start(bf16[1,16,128,256]{3,2,1,0:T(8,128)(2,1)} %param.7) | copy-start | bytes 3145732
  8.2 42.4 %collective-permute-start.1 = (bf16[1,128,256]{2,1,0:T(8,128)(2,1)S(1)}, bf16[1,128,256]{2,1,0:T(8,128)(2,1)S(1)}, u32[]{:S(2)}, u32[]{:S(2)}) collective-permute-start(bf16[1,128,256]{2,1,0:T(8,128)(2,1)S(1)} %get-tuple-element.9), channel_id=1, source_target_pairs={{1,0},{2,1},{3,2},{4,3},{5,4},{6,5},{7,6},{8,7},{9,8},{10,9},{11,1... | collective-permute-start | bytes 196616 | tf_op jit(solution)/shard_map/ppermute | solution.py:46
  9.5 41.1 %collective-permute-start = (bf16[1,128,256]{2,1,0:T(8,128)(2,1)S(1)}, bf16[1,128,256]{2,1,0:T(8,128)(2,1)S(1)}, u32[]{:S(2)}, u32[]{:S(2)}) collective-permute-start(bf16[1,128,256]{2,1,0:T(8,128)(2,1)S(1)} %get-tuple-element.8), channel_id=1, source_target_pairs={{0,1},{1,2},{2,3},{3,4},{4,5},{5,6},{6,7},{7,8},{8,9},{9,10},{10,1... | collective-permute-start | bytes 196616 | tf_op jit(solution)/shard_map/ppermute | solution.py:45
  16.8 33.3 %all-to-all-start = ((f32[16,1,64]{2,1,0:T(1,128)}), f32[16,1,64]{2,1,0:T(1,128)S(1)}, u32[]{:S(2)}, u32[]{:S(2)}) async-start(f32[16,1,64]{2,1,0:T(1,128)} %broadcast_in_dim.32), calls=%async_computation | async-start | bytes 16384 | tf_op jit(solution)/shard_map/all_to_all | solution.py:50
  36.5 124.0 %all-gather.2.cloned.1.call-start = ((), (), s32[]{:S(2)}) async-start(), calls=%async_computation.1 | async-start | bytes 1204224 | tf_op jit(solution)/shard_map/all_gather | solution.py:43
  55.4 3.6 %copy-start.2 = (bf16[16,128,2304]{2,1,0:T(8,128)(2,1)}, bf16[16,128,2304]{2,1,0:T(8,128)(2,1)S(1)}, u32[]{:S(2)}) copy-start(bf16[16,128,2304]{2,1,0:T(8,128)(2,1)S(1)} %slice_dynamic-update-slice_fusion.3) | copy-start | bytes 28311556
  60.3 7.2 %collective-permute-start.2 = (f32[2,2,3,2,48,256]{5,4,3,2,0,1:T(8,128)}, f32[2,2,3,2,48,256]{5,4,3,2,0,1:T(8,128)S(1)}, u32[]{:S(2)}, u32[]{:S(2)}) collective-permute-start(f32[2,2,3,2,48,256]{5,4,3,2,0,1:T(8,128)} %bitcast.74), channel_id=1, source_target_pairs={{0,16},{16,0},{32,48},{48,32},{64,80},{80,64},{96,112},{112,96},{1... | collective-permute-start | bytes 3538952 | tf_op jit(solution)/shard_map/ppermute | solution.py:19
  67.8 10.1 %collective-permute-start.3 = (f32[2,3,2,48,128]{4,3,2,1,0:T(8,128)S(1)}, f32[2,3,2,48,128]{4,3,2,1,0:T(8,128)S(1)}, u32[]{:S(2)}, u32[]{:S(2)}) collective-permute-start(f32[2,3,2,48,128]{4,3,2,1,0:T(8,128)S(1)} %dynamic-slice_bitcast_fusion), channel_id=1, source_target_pairs={{0,192},{16,208},{32,224},{48,240},{64,256},{80,272},{96,288},{112... | collective-permute-start | bytes 884744 | tf_op jit(solution)/shard_map/ppermute | solution.py:19
  71.2 10.1 %collective-permute-start.5 = (f32[2,2,3,48,128]{4,3,2,1,0:T(8,128)S(1)}, f32[2,2,3,48,128]{4,3,2,1,0:T(8,128)S(1)}, u32[]{:S(2)}, u32[]{:S(2)}) collective-permute-start(f32[2,2,3,48,128]{4,3,2,1,0:T(8,128)S(1)} %bitcast.79), channel_id=1, source_target_pairs={{0,32},{16,48},{32,0},{48,16},{64,96},{80,112},{96,64},{112,80},{1... | collective-permute-start | bytes 884744 | tf_op jit(solution)/shard_map/ppermute | solution.py:19
  78.0 82.5 %copy-start.1 = (bf16[1,16,128,256]{3,2,1,0:T(8,128)(2,1)S(1)}, bf16[1,16,128,256]{3,2,1,0:T(8,128)(2,1)}, u32[]{:S(2)}) copy-start(bf16[1,16,128,256]{3,2,1,0:T(8,128)(2,1)} %param.6) | copy-start | bytes 3145732
  78.0 6.7 %collective-permute-start.4 = (f32[2,3,48,128]{3,2,1,0:T(8,128)S(1)}, f32[2,3,48,128]{3,2,1,0:T(8,128)S(1)}, u32[]{:S(2)}, u32[]{:S(2)}) collective-permute-start(f32[2,3,48,128]{3,2,1,0:T(8,128)S(1)} %dynamic-slice_bitcast_fusion.2), channel_id=1, source_target_pairs={{0,32},{16,48},{32,0},{48,16},{64,96},{80,112},{96,64},{112,80},{1... | collective-permute-start | bytes 442376 | tf_op jit(solution)/shard_map/ppermute | solution.py:19
  81.3 6.0 %collective-permute-start.6 = (f32[2,3,48,128]{3,2,1,0:T(8,128)S(1)}, f32[2,3,48,128]{3,2,1,0:T(8,128)S(1)}, u32[]{:S(2)}, u32[]{:S(2)}) collective-permute-start(f32[2,3,48,128]{3,2,1,0:T(8,128)S(1)} %dynamic-slice_bitcast_fusion.1), channel_id=1, source_target_pairs={{0,192},{16,208},{32,224},{48,240},{64,256},{80,272},{96,288},{112... | collective-permute-start | bytes 442376 | tf_op jit(solution)/shard_map/ppermute | solution.py:19
  87.4 7.6 %collective-permute-start.7 = (f32[3,48,256]{2,1,0:T(8,128)S(1)}, f32[3,48,256]{2,1,0:T(8,128)S(1)}, u32[]{:S(2)}, u32[]{:S(2)}) collective-permute-start(f32[3,48,256]{2,1,0:T(8,128)S(1)} %fusion.4), channel_id=1, source_target_pairs={{0,384},{16,400},{32,416},{48,432},{64,448},{80,464},{96,480},{112... | collective-permute-start | bytes 442376 | tf_op jit(solution)/shard_map/ppermute | solution.py:19
  95.1 8.0 %collective-permute-start.9 = (f32[48,256]{1,0:T(8,128)S(1)}, f32[48,256]{1,0:T(8,128)S(1)}, u32[]{:S(2)}, u32[]{:S(2)}) collective-permute-start(f32[48,256]{1,0:T(8,128)S(1)} %get-tuple-element.13), channel_id=1, source_target_pairs={{0,128},{16,144},{32,160},{48,176},{64,0},{80,16},{96,32},{112,48}... | collective-permute-start | bytes 147464 | tf_op jit(solution)/shard_map/ppermute | solution.py:32
  101.1 9.4 %collective-permute-start.8 = (f32[48,256]{1,0:T(8,128)S(1)}, f32[48,256]{1,0:T(8,128)S(1)}, u32[]{:S(2)}, u32[]{:S(2)}) collective-permute-start(f32[48,256]{1,0:T(8,128)S(1)} %get-tuple-element.12), channel_id=1, source_target_pairs={{0,64},{16,80},{32,96},{48,112},{64,128},{80,144},{96,160},{112,17... | collective-permute-start | bytes 147464 | tf_op jit(solution)/shard_map/ppermute | solution.py:32
  110.6 11.3 %collective-permute-start.10 = (f32[48,128]{1,0:T(8,128)S(1)}, f32[48,128]{1,0:T(8,128)S(1)}, u32[]{:S(2)}, u32[]{:S(2)}) collective-permute-start(f32[48,128]{1,0:T(8,128)S(1)} %bitcast.88), channel_id=1, source_target_pairs={{0,8},{1,9},{2,10},{3,11},{4,12},{5,13},{6,14},{7,15},{8,0},{9,1},... | collective-permute-start | bytes 73736 | tf_op jit(solution)/shard_map/ppermute | solution.py:19
  122.0 8.5 %collective-permute-start.11 = (f32[48,64]{1,0:T(8,128)S(1)}, f32[48,64]{1,0:T(8,128)S(1)}, u32[]{:S(2)}, u32[]{:S(2)}) collective-permute-start(f32[48,64]{1,0:T(8,128)S(1)} %bitcast.89), channel_id=1, source_target_pairs={{0,4},{1,5},{2,6},{3,7},{4,0},{5,1},{6,2},{7,3},{8,12},{9,13},{10,... | collective-permute-start | bytes 36872 | tf_op jit(solution)/shard_map/ppermute | solution.py:19
  130.6 5.7 %collective-permute-start.12 = (f32[48,32]{0,1:T(8,128)S(1)}, f32[48,32]{0,1:T(8,128)S(1)}, u32[]{:S(2)}, u32[]{:S(2)}) collective-permute-start(f32[48,32]{0,1:T(8,128)S(1)} %dynamic-slice_bitcast_fusion.5), channel_id=1, source_target_pairs={{0,2},{1,3},{2,0},{3,1},{4,6},{5,7},{6,4},{7,5},{8,10},{9,11},{10,... | collective-permute-start | bytes 18440 | tf_op jit(solution)/shard_map/ppermute | solution.py:19
  136.3 4.8 %collective-permute-start.13 = (f32[48,16]{0,1:T(8,128)S(1)}, f32[48,16]{0,1:T(8,128)S(1)}, u32[]{:S(2)}, u32[]{:S(2)}) collective-permute-start(f32[48,16]{0,1:T(8,128)S(1)} %dynamic-slice_bitcast_fusion.6), channel_id=1, source_target_pairs={{0,1},{1,0},{2,3},{3,2},{4,5},{5,4},{6,7},{7,6},{8,9},{9,8},{10,11... | collective-permute-start | bytes 9224 | tf_op jit(solution)/shard_map/ppermute | solution.py:19
Sparse Core Ops, SparseCore 0:
  71.1 89.3 all-gather.1

commit v7 on v6

--- a/solution.py
+++ b/solution.py
@@ -47,8 +47,7 @@
     values = raw.astype(jnp.float32)
     grouped = values.reshape(rows, cols, G, width // G)
     stats = jnp.concatenate([jnp.sum(grouped, axis=(0, 1, 3)), jnp.sum(grouped * grouped, axis=(0, 1, 3))])
-    stats = lax.all_to_all(jnp.broadcast_to(stats[None], (ntile,) + stats.shape), "tile", 0, 0)
-    stats = jnp.sum(stats, axis=0)
+    stats = jnp.sum(lax.all_to_all(jnp.broadcast_to(stats[None], (ntile,) + stats.shape), "tile", 0, 0), axis=0)
     sums, squares = stats[:G], stats[G:]
     count = rows * ntile * cols * (width // G)
     mean = sums / count
@@ -79,10 +78,16 @@
     ga = halve(ga, 2, "dp", 2)
     gb = halve(gb, 1, "dp", 12)
     g = jnp.concatenate([ga, gb], axis=-1)
-    g = halve(g, 0, "dp", 24)
+    quarter = half // 2
+    ga = halve(g[..., :half], 0, "dp", 24)
+    gb = halve(g[..., half:].reshape(g.shape[:-1] + (2, quarter)), 3, "tile", 4)
+    ga = halve(ga.reshape(ga.shape[:-1] + (2, quarter)), 2, "tile", 4)
+    gb = halve(gb, 0, "dp", 24)
+    g = jnp.stack([ga, gb], axis=2)
     g = direct(g, 0, "dp", 4, 3)
-    span = width
-    for stride in (8, 4, 2, 1):
+    g = halve(g, 1, "tile", 8)
+    span = quarter
+    for stride in (2, 1):
         span //= 2
         g = halve(g.reshape(per, 2, span), 1, "tile", stride)
     grad_weight = g / jnp.sqrt(jnp.float32(positions))

time: 176 us -> 176 us (level)
  waiting for transfers between devices: 73.1 us -> 62.2 us
  starting transfers between devices: 63.6 us -> 73.7 us
    ppermute x10 -> x12, starting transfers between devices: 29.9 us -> 38.4 us  [halve(): return mine + lax.ppermute(other, axis, pairs)]
    all_gather x1, waiting for transfers between devices: 18.8 us -> 10.6 us  [body_inner(): full_weight = lax.all_gather(conv_weight, 'dp', axis=0, tiled=True)]
    ppermute x10 -> x12, waiting for transfers between devices: 34 us -> 33 us  [halve(): return mine + lax.ppermute(other, axis, pairs)]
  transfers between devices with their start and end apart: 16 -> 18, of which waited for: 12 -> 13; matrix products, arithmetic and copies ran while one was open for 3% -> 3% of each run, Pallas kernels for 0% -> 0%
where the time goes in v7:
time: 176 us; the launch traced here: 175 us
  starting transfers between devices  73.7 us (42%)
  waiting for transfers between devices  62.2 us (35%)
  between operations  14.8 us (8%)
  matrix products  10.7 us (6%)
  local copies, waits for them, and re-layouts  7.84 us (4%)
  other arithmetic  5.93 us (3%)
    ppermute x12, starting transfers between devices, halve(): return mine + lax.ppermute(other, axis, pairs)  38.4 us
    ppermute x12, waiting for transfers between devices, halve(): return mine + lax.ppermute(other, axis, pairs)  33 us
    all_to_all x1, starting transfers between devices, body_inner(): lax.all_to_all(jnp.broadcast_to(stats[None], (ntile,) + stats.shape), 'ti...  19.8 us
    all_to_all x1, waiting for transfers between devices, body_inner(): lax.all_to_all(jnp.broadcast_to(stats[None], (ntile,) + stats.shape), 'ti...  12.8 us
    all_gather x1, waiting for transfers between devices, body_inner(): full_weight = lax.all_gather(conv_weight, 'dp', axis=0, tiled=True)  10.6 us
    ppermute x2, starting transfers between devices, direct(): acc = acc + lax.ppermute(piece, axis, pairs)  9.52 us
    dot_general x1, matrix products, body_inner(): conv = jnp.dot(patches, full_weight, preferred_element_type=jnp.float32)  7.91 us
    ppermute x2, waiting for transfers between devices, direct(): acc = acc + lax.ppermute(piece, axis, pairs)  5.75 us
  transfers between devices with their start and end apart: 18, of which 13 were waited for; matrix products, arithmetic and copies ran while one was open for 3% of the time, Pallas kernels for 0%

profile of v7, /device:TPU:1, one launch (start us, length us, event | category | flops | bytes accessed | tf_op | source)
XLA Modules:
  0.0 175.2 jit_solution(16533140318161381661)
XLA Ops:
  9.5 4.7 %collective-permute-start = (bf16[1,128,256]{2,1,0:T(8,128)(2,1)S(1)}, bf16[1,128,256]{2,1,0:T(8,128)(2,1)S(1)}, u32[]{:S(2)}, u32[]{:S(2)}) collective-permute-start(bf16[1,128,256]{2,1,0:T(8,128)(2,1)S(1)} %get-tuple-element.8), channel_id=1, source_target_pairs={{0,1},{1,2},{2,3},{3,4},{4,5},{5,6},{6,7},{7,8},{8,9},{9,10},{10,1... | collective-permute-start | bytes 196616 | tf_op jit(solution)/shard_map/ppermute | solution.py:45
  16.8 19.8 %all-to-all-start = ((f32[16,1,64]{2,1,0:T(1,128)}), f32[16,1,64]{2,1,0:T(1,128)S(1)}, u32[]{:S(2)}, u32[]{:S(2)}) async-start(f32[16,1,64]{2,1,0:T(1,128)} %broadcast_in_dim.32), calls=%async_computation | async-start | bytes 16384 | tf_op jit(solution)/shard_map/all_to_all | solution.py:50
  37.3 12.8 %all-to-all-done = f32[16,1,64]{2,1,0:T(1,128)S(1)} async-done(((f32[16,1,64]{2,1,0:T(1,128)}), f32[16,1,64]{2,1,0:T(1,128)S(1)}, u32[]{:S(2)}, u32[]{:S(2)}) %all-to-all-start) | async-done | bytes 4128 | tf_op jit(solution)/shard_map/all_to_all | solution.py:50
  55.4 2.8 %convolution_bitcast_fusion = f32[256,2304]{0,1:T(8,128)S(1)} fusion(bf16[2048,2304]{1,0:T(8,128)(2,1)S(1)} %bitcast.98, bf16[2048,256]{1,0:T(8,128)(2,1)S(1)} %bitcast.90), kind=kOutput, calls=%fused_computation | convolution fusion | flops 2415919104 | bytes 12845056 | tf_op jit(solution)/shard_map/dot_general | solution.py:70
  60.3 4.6 %collective-permute-start.2 = (f32[2,2,3,2,48,256]{5,4,3,2,0,1:T(8,128)}, f32[2,2,3,2,48,256]{5,4,3,2,0,1:T(8,128)S(1)}, u32[]{:S(2)}, u32[]{:S(2)}) collective-permute-start(f32[2,2,3,2,48,256]{5,4,3,2,0,1:T(8,128)} %bitcast.89), channel_id=1, source_target_pairs={{0,16},{16,0},{32,48},{48,32},{64,80},{80,64},{96,112},{112,96},{1... | collective-permute-start | bytes 3538952 | tf_op jit(solution)/shard_map/ppermute | solution.py:19
  64.9 2.6 %collective-permute-done.2 = f32[2,2,3,2,48,256]{5,4,3,2,0,1:T(8,128)S(1)} collective-permute-done((f32[2,2,3,2,48,256]{5,4,3,2,0,1:T(8,128)}, f32[2,2,3,2,48,256]{5,4,3,2,0,1:T(8,128)S(1)}, u32[]{:S(2)}, u32[]{:S(2)}) %collective-permute-start.2) | collective-permute-done | bytes 1179680 | tf_op jit(solution)/shard_map/ppermute | solution.py:19
  67.9 3.1 %collective-permute-start.3 = (f32[2,3,2,48,128]{4,3,2,1,0:T(8,128)S(1)}, f32[2,3,2,48,128]{4,3,2,1,0:T(8,128)S(1)}, u32[]{:S(2)}, u32[]{:S(2)}) collective-permute-start(f32[2,3,2,48,128]{4,3,2,1,0:T(8,128)S(1)} %dynamic-slice_bitcast_fusion.1), channel_id=1, source_target_pairs={{0,192},{16,208},{32,224},{48,240},{64,256},{80,272},{96,288},{112... | collective-permute-start | bytes 884744 | tf_op jit(solution)/shard_map/ppermute | solution.py:19
  71.2 3.1 %collective-permute-start.7 = (f32[2,2,3,48,128]{4,3,2,0,1:T(8,128)S(1)}, f32[2,2,3,48,128]{4,3,2,0,1:T(8,128)S(1)}, u32[]{:S(2)}, u32[]{:S(2)}) collective-permute-start(f32[2,2,3,48,128]{4,3,2,0,1:T(8,128)S(1)} %dynamic-slice_bitcast_fusion), channel_id=1, source_target_pairs={{0,32},{16,48},{32,0},{48,16},{64,96},{80,112},{96,64},{112,80},{1... | collective-permute-start | bytes 884744 | tf_op jit(solution)/shard_map/ppermute | solution.py:19
  74.3 3.6 %collective-permute-done.3 = f32[2,3,2,48,128]{4,3,2,1,0:T(8,128)S(1)} collective-permute-done((f32[2,3,2,48,128]{4,3,2,1,0:T(8,128)S(1)}, f32[2,3,2,48,128]{4,3,2,1,0:T(8,128)S(1)}, u32[]{:S(2)}, u32[]{:S(2)}) %collective-permute-start.3) | collective-permute-done | bytes 294944 | tf_op jit(solution)/shard_map/ppermute | solution.py:19
  78.0 3.1 %collective-permute-start.4 = (f32[2,3,48,128]{3,2,1,0:T(8,128)S(1)}, f32[2,3,48,128]{3,2,1,0:T(8,128)S(1)}, u32[]{:S(2)}, u32[]{:S(2)}) collective-permute-start(f32[2,3,48,128]{3,2,1,0:T(8,128)S(1)} %dynamic-slice_bitcast_fusion.3), channel_id=1, source_target_pairs={{0,32},{16,48},{32,0},{48,16},{64,96},{80,112},{96,64},{112,80},{1... | collective-permute-start | bytes 442376 | tf_op jit(solution)/shard_map/ppermute | solution.py:19
  81.2 3.1 %collective-permute-start.8 = (f32[2,3,48,128]{3,2,1,0:T(8,128)S(1)}, f32[2,3,48,128]{3,2,1,0:T(8,128)S(1)}, u32[]{:S(2)}, u32[]{:S(2)}) collective-permute-start(f32[2,3,48,128]{3,2,1,0:T(8,128)S(1)} %dynamic-slice_bitcast_fusion.2), channel_id=1, source_target_pairs={{0,192},{16,208},{32,224},{48,240},{64,256},{80,272},{96,288},{112... | collective-permute-start | bytes 442376 | tf_op jit(solution)/shard_map/ppermute | solution.py:19
  84.7 4.2 %collective-permute-start.5 = (f32[3,48,128]{2,1,0:T(8,128)S(1)}, f32[3,48,128]{2,1,0:T(8,128)S(1)}, u32[]{:S(2)}, u32[]{:S(2)}) collective-permute-start(f32[3,48,128]{2,1,0:T(8,128)S(1)} %dynamic-slice_bitcast_fusion.5), channel_id=1, source_target_pairs={{0,384},{16,400},{32,416},{48,432},{64,448},{80,464},{96,480},{112... | collective-permute-start | bytes 221192 | tf_op jit(solution)/shard_map/ppermute | solution.py:19
  92.5 6.9 %collective-permute-done.9 = f32[2,3,48,64]{3,2,1,0:T(8,128)S(1)} collective-permute-done((f32[2,3,48,64]{3,2,1,0:T(8,128)S(1)}, f32[2,3,48,64]{3,2,1,0:T(8,128)S(1)}, u32[]{:S(2)}, u32[]{:S(2)}) %collective-permute-start.9) | collective-permute-done | bytes 73760 | tf_op jit(solution)/shard_map/ppermute | solution.py:19
  99.4 3.1 %collective-permute-start.10 = (f32[3,48,64]{2,1,0:T(8,128)S(1)}, f32[3,48,64]{2,1,0:T(8,128)S(1)}, u32[]{:S(2)}, u32[]{:S(2)}) collective-permute-start(f32[3,48,64]{2,1,0:T(8,128)S(1)} %dynamic-slice_bitcast_fusion.4), channel_id=1, source_target_pairs={{0,384},{16,400},{32,416},{48,432},{64,448},{80,464},{96,480},{112... | collective-permute-start | bytes 110600 | tf_op jit(solution)/shard_map/ppermute | solution.py:19
  106.2 5.5 %collective-permute-done.6 = f32[3,48,64]{2,1,0:T(8,128)S(1)} collective-permute-done((f32[3,48,64]{2,1,0:T(8,128)S(1)}, f32[3,48,64]{2,1,0:T(8,128)S(1)}, u32[]{:S(2)}, u32[]{:S(2)}) %collective-permute-start.6) | collective-permute-done | bytes 36896 | tf_op jit(solution)/shard_map/ppermute | solution.py:19
  111.7 5.9 %collective-permute-start.12 = (f32[48,2,64]{2,0,1:T(8,128)S(1)}, f32[48,2,64]{2,0,1:T(8,128)S(1)}, u32[]{:S(2)}, u32[]{:S(2)}) collective-permute-start(f32[48,2,64]{2,0,1:T(8,128)S(1)} %get-tuple-element.13), channel_id=1, source_target_pairs={{0,128},{16,144},{32,160},{48,176},{64,0},{80,16},{96,32},{112,48}... | collective-permute-start | bytes 73736 | tf_op jit(solution)/shard_map/ppermute | solution.py:32
  117.6 3.6 %collective-permute-start.11 = (f32[48,2,64]{2,0,1:T(8,128)S(1)}, f32[48,2,64]{2,0,1:T(8,128)S(1)}, u32[]{:S(2)}, u32[]{:S(2)}) collective-permute-start(f32[48,2,64]{2,0,1:T(8,128)S(1)} %get-tuple-element.12), channel_id=1, source_target_pairs={{0,64},{16,80},{32,96},{48,112},{64,128},{80,144},{96,160},{112,17... | collective-permute-start | bytes 73736 | tf_op jit(solution)/shard_map/ppermute | solution.py:32
  121.3 5.7 %collective-permute-done.11 = f32[48,2,64]{2,0,1:T(8,128)S(1)} collective-permute-done((f32[48,2,64]{2,0,1:T(8,128)S(1)}, f32[48,2,64]{2,0,1:T(8,128)S(1)}, u32[]{:S(2)}, u32[]{:S(2)}) %collective-permute-start.11) | collective-permute-done | bytes 24608 | tf_op jit(solution)/shard_map/ppermute | solution.py:32
  127.2 3.3 %collective-permute-start.13 = (f32[48,64]{0,1:T(8,128)S(1)}, f32[48,64]{0,1:T(8,128)S(1)}, u32[]{:S(2)}, u32[]{:S(2)}) collective-permute-start(f32[48,64]{0,1:T(8,128)S(1)} %bitcast.102), channel_id=1, source_target_pairs={{0,8},{1,9},{2,10},{3,11},{4,12},{5,13},{6,14},{7,15},{8,0},{9,1},... | collective-permute-start | bytes 36872 | tf_op jit(solution)/shard_map/ppermute | solution.py:19
  130.6 7.7 %collective-permute-done.13 = f32[48,64]{0,1:T(8,128)S(1)} collective-permute-done((f32[48,64]{0,1:T(8,128)S(1)}, f32[48,64]{0,1:T(8,128)S(1)}, u32[]{:S(2)}, u32[]{:S(2)}) %collective-permute-start.13) | collective-permute-done | bytes 12320 | tf_op jit(solution)/shard_map/ppermute | solution.py:19
  140.2 3.4 %collective-permute-done.14 = f32[48,32]{0,1:T(8,128)S(1)} collective-permute-done((f32[48,32]{0,1:T(8,128)S(1)}, f32[48,32]{0,1:T(8,128)S(1)}, u32[]{:S(2)}, u32[]{:S(2)}) %collective-permute-start.14) | collective-permute-done | bytes 6176 | tf_op jit(solution)/shard_map/ppermute | solution.py:19
  143.7 4.3 %collective-permute-start.15 = (f32[48,16]{0,1:T(8,128)S(1)}, f32[48,16]{0,1:T(8,128)S(1)}, u32[]{:S(2)}, u32[]{:S(2)}) collective-permute-start(f32[48,16]{0,1:T(8,128)S(1)} %dynamic-slice_bitcast_fusion.7), channel_id=1, source_target_pairs={{0,1},{1,0},{2,3},{3,2},{4,5},{5,4},{6,7},{7,6},{8,9},{9,8},{10,11... | collective-permute-start | bytes 9224 | tf_op jit(solution)/shard_map/ppermute | solution.py:19
  149.8 10.6 %all-gather.2.cloned.1.call-done = bf16[2304,256]{1,0:T(8,128)(2,1)} async-done(((bf16[48,256]{1,0:T(8,128)(2,1)}), bf16[2304,256]{1,0:T(8,128)(2,1)}) %all-gather.2.cloned.1.call-update) | async-done | bytes 1179664 | tf_op jit(solution)/shard_map/all_gather | solution.py:43
  160.5 7.9 %add_bitcast_fusion = f32[1,16,128,256]{3,2,1,0:T(8,128)} fusion(bf16[16,128,2304]{2,1,0:T(8,128)(2,1)} %copy-done.2, bf16[2304,256]{1,0:T(8,128)(2,1)} %all-gather.2.cloned.1.call-done, bf16[1,16,128,256]{3,2,1,0:T(8,128)(2,1)S(1)} %copy-done.1), kind=kOutput, calls=%fused_computation.5 | convolution fusion | flops 2416967680 | bytes 13762560 | tf_op jit(solution)/shard_map/dot_general | solution.py:94
  (79 shorter events, 25.0 us)
Async XLA Ops:
  7.2 48.2 %copy-start = (bf16[1,16,128,256]{3,2,1,0:T(8,128)(2,1)S(1)}, bf16[1,16,128,256]{3,2,1,0:T(8,128)(2,1)}, u32[]{:S(2)}) copy-start(bf16[1,16,128,256]{3,2,1,0:T(8,128)(2,1)} %param.7) | copy-start | bytes 3145732
  8.2 42.4 %collective-permute-start.1 = (bf16[1,128,256]{2,1,0:T(8,128)(2,1)S(1)}, bf16[1,128,256]{2,1,0:T(8,128)(2,1)S(1)}, u32[]{:S(2)}, u32[]{:S(2)}) collective-permute-start(bf16[1,128,256]{2,1,0:T(8,128)(2,1)S(1)} %get-tuple-element.9), channel_id=1, source_target_pairs={{1,0},{2,1},{3,2},{4,3},{5,4},{6,5},{7,6},{8,7},{9,8},{10,9},{11,1... | collective-permute-start | bytes 196616 | tf_op jit(solution)/shard_map/ppermute | solution.py:46
  9.5 41.1 %collective-permute-start = (bf16[1,128,256]{2,1,0:T(8,128)(2,1)S(1)}, bf16[1,128,256]{2,1,0:T(8,128)(2,1)S(1)}, u32[]{:S(2)}, u32[]{:S(2)}) collective-permute-start(bf16[1,128,256]{2,1,0:T(8,128)(2,1)S(1)} %get-tuple-element.8), channel_id=1, source_target_pairs={{0,1},{1,2},{2,3},{3,4},{4,5},{5,6},{6,7},{7,8},{8,9},{9,10},{10,1... | collective-permute-start | bytes 196616 | tf_op jit(solution)/shard_map/ppermute | solution.py:45
  16.8 33.3 %all-to-all-start = ((f32[16,1,64]{2,1,0:T(1,128)}), f32[16,1,64]{2,1,0:T(1,128)S(1)}, u32[]{:S(2)}, u32[]{:S(2)}) async-start(f32[16,1,64]{2,1,0:T(1,128)} %broadcast_in_dim.32), calls=%async_computation | async-start | bytes 16384 | tf_op jit(solution)/shard_map/all_to_all | solution.py:50
  36.5 124.0 %all-gather.2.cloned.1.call-start = ((), (), s32[]{:S(2)}) async-start(), calls=%async_computation.1 | async-start | bytes 1204224 | tf_op jit(solution)/shard_map/all_gather | solution.py:43
  55.4 3.7 %copy-start.2 = (bf16[16,128,2304]{2,1,0:T(8,128)(2,1)}, bf16[16,128,2304]{2,1,0:T(8,128)(2,1)S(1)}, u32[]{:S(2)}) copy-start(bf16[16,128,2304]{2,1,0:T(8,128)(2,1)S(1)} %slice_dynamic-update-slice_fusion.3) | copy-start | bytes 28311556
  60.3 7.2 %collective-permute-start.2 = (f32[2,2,3,2,48,256]{5,4,3,2,0,1:T(8,128)}, f32[2,2,3,2,48,256]{5,4,3,2,0,1:T(8,128)S(1)}, u32[]{:S(2)}, u32[]{:S(2)}) collective-permute-start(f32[2,2,3,2,48,256]{5,4,3,2,0,1:T(8,128)} %bitcast.89), channel_id=1, source_target_pairs={{0,16},{16,0},{32,48},{48,32},{64,80},{80,64},{96,112},{112,96},{1... | collective-permute-start | bytes 3538952 | tf_op jit(solution)/shard_map/ppermute | solution.py:19
  67.9 10.1 %collective-permute-start.3 = (f32[2,3,2,48,128]{4,3,2,1,0:T(8,128)S(1)}, f32[2,3,2,48,128]{4,3,2,1,0:T(8,128)S(1)}, u32[]{:S(2)}, u32[]{:S(2)}) collective-permute-start(f32[2,3,2,48,128]{4,3,2,1,0:T(8,128)S(1)} %dynamic-slice_bitcast_fusion.1), channel_id=1, source_target_pairs={{0,192},{16,208},{32,224},{48,240},{64,256},{80,272},{96,288},{112... | collective-permute-start | bytes 884744 | tf_op jit(solution)/shard_map/ppermute | solution.py:19
  71.2 9.9 %collective-permute-start.7 = (f32[2,2,3,48,128]{4,3,2,0,1:T(8,128)S(1)}, f32[2,2,3,48,128]{4,3,2,0,1:T(8,128)S(1)}, u32[]{:S(2)}, u32[]{:S(2)}) collective-permute-start(f32[2,2,3,48,128]{4,3,2,0,1:T(8,128)S(1)} %dynamic-slice_bitcast_fusion), channel_id=1, source_target_pairs={{0,32},{16,48},{32,0},{48,16},{64,96},{80,112},{96,64},{112,80},{1... | collective-permute-start | bytes 884744 | tf_op jit(solution)/shard_map/ppermute | solution.py:19
  78.0 6.6 %collective-permute-start.4 = (f32[2,3,48,128]{3,2,1,0:T(8,128)S(1)}, f32[2,3,48,128]{3,2,1,0:T(8,128)S(1)}, u32[]{:S(2)}, u32[]{:S(2)}) collective-permute-start(f32[2,3,48,128]{3,2,1,0:T(8,128)S(1)} %dynamic-slice_bitcast_fusion.3), channel_id=1, source_target_pairs={{0,32},{16,48},{32,0},{48,16},{64,96},{80,112},{96,64},{112,80},{1... | collective-permute-start | bytes 442376 | tf_op jit(solution)/shard_map/ppermute | solution.py:19
  81.2 7.7 %collective-permute-start.8 = (f32[2,3,48,128]{3,2,1,0:T(8,128)S(1)}, f32[2,3,48,128]{3,2,1,0:T(8,128)S(1)}, u32[]{:S(2)}, u32[]{:S(2)}) collective-permute-start(f32[2,3,48,128]{3,2,1,0:T(8,128)S(1)} %dynamic-slice_bitcast_fusion.2), channel_id=1, source_target_pairs={{0,192},{16,208},{32,224},{48,240},{64,256},{80,272},{96,288},{112... | collective-permute-start | bytes 442376 | tf_op jit(solution)/shard_map/ppermute | solution.py:19
  84.6 75.8 %copy-start.1 = (bf16[1,16,128,256]{3,2,1,0:T(8,128)(2,1)S(1)}, bf16[1,16,128,256]{3,2,1,0:T(8,128)(2,1)}, u32[]{:S(2)}) copy-start(bf16[1,16,128,256]{3,2,1,0:T(8,128)(2,1)} %param.6) | copy-start | bytes 3145732
  84.7 7.7 %collective-permute-start.5 = (f32[3,48,128]{2,1,0:T(8,128)S(1)}, f32[3,48,128]{2,1,0:T(8,128)S(1)}, u32[]{:S(2)}, u32[]{:S(2)}) collective-permute-start(f32[3,48,128]{2,1,0:T(8,128)S(1)} %dynamic-slice_bitcast_fusion.5), channel_id=1, source_target_pairs={{0,384},{16,400},{32,416},{48,432},{64,448},{80,464},{96,480},{112... | collective-permute-start | bytes 221192 | tf_op jit(solution)/shard_map/ppermute | solution.py:19
  89.4 10.0 %collective-permute-start.9 = (f32[2,3,48,64]{3,2,1,0:T(8,128)S(1)}, f32[2,3,48,64]{3,2,1,0:T(8,128)S(1)}, u32[]{:S(2)}, u32[]{:S(2)}) collective-permute-start(f32[2,3,48,64]{3,2,1,0:T(8,128)S(1)} %bitcast.95), channel_id=1, source_target_pairs={{0,4},{1,5},{2,6},{3,7},{4,0},{5,1},{6,2},{7,3},{8,12},{9,13},{10,... | collective-permute-start | bytes 221192 | tf_op jit(solution)/shard_map/ppermute | solution.py:19
  99.4 6.7 %collective-permute-start.10 = (f32[3,48,64]{2,1,0:T(8,128)S(1)}, f32[3,48,64]{2,1,0:T(8,128)S(1)}, u32[]{:S(2)}, u32[]{:S(2)}) collective-permute-start(f32[3,48,64]{2,1,0:T(8,128)S(1)} %dynamic-slice_bitcast_fusion.4), channel_id=1, source_target_pairs={{0,384},{16,400},{32,416},{48,432},{64,448},{80,464},{96,480},{112... | collective-permute-start | bytes 110600 | tf_op jit(solution)/shard_map/ppermute | solution.py:19
  102.7 9.0 %collective-permute-start.6 = (f32[3,48,64]{2,1,0:T(8,128)S(1)}, f32[3,48,64]{2,1,0:T(8,128)S(1)}, u32[]{:S(2)}, u32[]{:S(2)}) collective-permute-start(f32[3,48,64]{2,1,0:T(8,128)S(1)} %bitcast.99), channel_id=1, source_target_pairs={{0,4},{1,5},{2,6},{3,7},{4,0},{5,1},{6,2},{7,3},{8,12},{9,13},{10,... | collective-permute-start | bytes 110600 | tf_op jit(solution)/shard_map/ppermute | solution.py:19
  111.7 9.6 %collective-permute-start.12 = (f32[48,2,64]{2,0,1:T(8,128)S(1)}, f32[48,2,64]{2,0,1:T(8,128)S(1)}, u32[]{:S(2)}, u32[]{:S(2)}) collective-permute-start(f32[48,2,64]{2,0,1:T(8,128)S(1)} %get-tuple-element.13), channel_id=1, source_target_pairs={{0,128},{16,144},{32,160},{48,176},{64,0},{80,16},{96,32},{112,48}... | collective-permute-start | bytes 73736 | tf_op jit(solution)/shard_map/ppermute | solution.py:32
  117.6 9.4 %collective-permute-start.11 = (f32[48,2,64]{2,0,1:T(8,128)S(1)}, f32[48,2,64]{2,0,1:T(8,128)S(1)}, u32[]{:S(2)}, u32[]{:S(2)}) collective-permute-start(f32[48,2,64]{2,0,1:T(8,128)S(1)} %get-tuple-element.12), channel_id=1, source_target_pairs={{0,64},{16,80},{32,96},{48,112},{64,128},{80,144},{96,160},{112,17... | collective-permute-start | bytes 73736 | tf_op jit(solution)/shard_map/ppermute | solution.py:32
  127.2 11.1 %collective-permute-start.13 = (f32[48,64]{0,1:T(8,128)S(1)}, f32[48,64]{0,1:T(8,128)S(1)}, u32[]{:S(2)}, u32[]{:S(2)}) collective-permute-start(f32[48,64]{0,1:T(8,128)S(1)} %bitcast.102), channel_id=1, source_target_pairs={{0,8},{1,9},{2,10},{3,11},{4,12},{5,13},{6,14},{7,15},{8,0},{9,1},... | collective-permute-start | bytes 36872 | tf_op jit(solution)/shard_map/ppermute | solution.py:19
  138.3 5.4 %collective-permute-start.14 = (f32[48,32]{0,1:T(8,128)S(1)}, f32[48,32]{0,1:T(8,128)S(1)}, u32[]{:S(2)}, u32[]{:S(2)}) collective-permute-start(f32[48,32]{0,1:T(8,128)S(1)} %dynamic-slice_bitcast_fusion.6), channel_id=1, source_target_pairs={{0,2},{1,3},{2,0},{3,1},{4,6},{5,7},{6,4},{7,5},{8,10},{9,11},{10,... | collective-permute-start | bytes 18440 | tf_op jit(solution)/shard_map/ppermute | solution.py:19
  143.7 5.6 %collective-permute-start.15 = (f32[48,16]{0,1:T(8,128)S(1)}, f32[48,16]{0,1:T(8,128)S(1)}, u32[]{:S(2)}, u32[]{:S(2)}) collective-permute-start(f32[48,16]{0,1:T(8,128)S(1)} %dynamic-slice_bitcast_fusion.7), channel_id=1, source_target_pairs={{0,1},{1,0},{2,3},{3,2},{4,5},{5,4},{6,7},{7,6},{8,9},{9,8},{10,11... | collective-permute-start | bytes 9224 | tf_op jit(solution)/shard_map/ppermute | solution.py:19
Sparse Core Ops, SparseCore 0:
  71.1 89.3 all-gather.1
